TPU v7x, 32 devices: a whole 2x2x4 slice. The times are simulated.
32 devices in a mesh: wide: 8 (over z, y), tm: 4 (over x, core).
Axes of the slice: x: 2, y: 2, z: 4, core: 2. Of those that a mesh axis runs over, the one named last changes fastest.
Arguments:
- samples: bfloat16 [32, 1024, 2048], P('tm', 'wide'), may hold values from -6 to 6
- feed_input_wiring: int32 [1024], replicated, may hold values from 0 to 1023, each once
- input_flags: int32 [1024], replicated, may hold values 0 or 1
Outputs:
- delay_spectra: float32 [4096, 2, 512], P(('wide', 'tm'))
Inputs may be any that keep to these rules, and one draw needn't show every extreme that they name: `feed_input_wiring`: a permutation of the inputs.
All inputs are finite; a program needn't handle non-finite values.
Results may differ from a plain program's by a relative error of at most 0.0058.
Values may be sent and summed in bfloat16 or wider, within the bound.
No kernel may reach another device: no remote copies, remote signals or barrier semaphores. Data moves between devices by JAX's collectives and lax.ppermute only.
A program may use at most 128 MiB of HBM per device.

v0:
```python
import math

import jax
import jax.numpy as jnp
from jax import lax
from jax.sharding import PartitionSpec as P

CYL = 4
FEEDS = 256
NSAMP = 2048
CH = 512
CHAN_LO = 256
NBASE = 4096


def channel_table(length, frequency_channels, first):
    samples_at = jnp.arange(length, dtype=jnp.int32)
    channel_at = jnp.arange(frequency_channels, dtype=jnp.int32) + first
    turns = samples_at[:, None] * channel_at[None, :] % length
    phase = turns.astype(jnp.float32) * (2.0 * math.pi / length)
    scale = 1.0 / math.sqrt(length)
    both = jnp.stack([jnp.cos(phase) * scale, -jnp.sin(phase) * scale], axis=2)
    return both.reshape(length, 2 * frequency_channels).astype(jnp.bfloat16)


def diag_sums(tiles):
    length = tiles.shape[-1]
    leading = tiles.shape[:-2]
    flattened = tiles.reshape(leading + (length * length,))
    flattened = jnp.pad(flattened, [(0, 0)] * len(leading) + [(0, length)])
    skewed = flattened.reshape(leading + (length, length + 1))[..., :length]
    row_at = jnp.arange(length, dtype=jnp.int32)[:, None]
    col_at = jnp.arange(length, dtype=jnp.int32)[None, :]
    inside = col_at < length - row_at
    return jnp.sum(jnp.where(inside, skewed, jnp.zeros_like(skewed)), axis=-2)


def pair_keep():
    same = jnp.eye(CYL, dtype=jnp.float32)[:, :, None]
    first = (jnp.arange(FEEDS, dtype=jnp.int32) == 0).astype(jnp.float32)[None, None, :]
    return 1.0 - same * first


def stack_counts(feed_input_wiring, input_flags):
    placed = input_flags[feed_input_wiring].astype(jnp.float32).reshape(CYL, FEEDS)
    tiles = placed[:, None, :, None] * placed[None, :, None, :]
    return (diag_sums(tiles) * pair_keep()).reshape(NBASE)


def feed_tables():
    padded_length = 2 * FEEDS
    feed_at = jnp.arange(FEEDS, dtype=jnp.int32)
    bin_at = jnp.arange(padded_length, dtype=jnp.int32)
    turns = feed_at[:, None] * bin_at[None, :] % padded_length
    phase = turns.astype(jnp.float32) * (2.0 * math.pi / padded_length)
    return (jnp.cos(phase), jnp.sin(phase))


def correlate(turned, feed_input_wiring, input_flags):
    weighted_visibility = turned * input_flags.astype(jnp.bfloat16)
    placed = jnp.take(weighted_visibility, feed_input_wiring, axis=3)
    local_channels, _, frames_here, _ = placed.shape
    padded_length = 2 * FEEDS
    high = lax.Precision.HIGHEST
    feed_data = placed.astype(jnp.float32).reshape(local_channels, 2, frames_here, CYL, FEEDS)
    cos_table, sin_table = feed_tables()
    both_tables = jnp.concatenate([cos_table, sin_table], axis=1)
    projected = jnp.einsum("cptai,ig->cptag", feed_data, both_tables, precision=high)
    real_cos = projected[:, 0, :, :, :padded_length]
    real_sin = projected[:, 0, :, :, padded_length:]
    imag_cos = projected[:, 1, :, :, :padded_length]
    imag_sin = projected[:, 1, :, :, padded_length:]
    freq_real = real_cos + imag_sin
    freq_imag = imag_cos - real_sin
    cross_real = jnp.einsum("ctaf,ctbf->cabf", freq_real, freq_real, precision=high) + jnp.einsum(
        "ctaf,ctbf->cabf", freq_imag, freq_imag, precision=high
    )
    cross_imag = jnp.einsum("ctaf,ctbf->cabf", freq_imag, freq_real, precision=high) - jnp.einsum(
        "ctaf,ctbf->cabf", freq_real, freq_imag, precision=high
    )
    back_cos = jnp.transpose(cos_table) * (1.0 / padded_length)
    back_sin = jnp.transpose(sin_table) * (1.0 / padded_length)
    lag_real = jnp.einsum("cabf,fk->cabk", cross_real, back_cos, precision=high) + jnp.einsum(
        "cabf,fk->cabk", cross_imag, back_sin, precision=high
    )
    lag_imag = jnp.einsum("cabf,fk->cabk", cross_imag, back_cos, precision=high) - jnp.einsum(
        "cabf,fk->cabk", cross_real, back_sin, precision=high
    )
    stacked = jnp.stack([lag_real, lag_imag], axis=1) * pair_keep()
    return stacked.reshape(local_channels, 2, NBASE)


def delay_transform(visibility_product, counts, frames_all):
    frequency_channels = visibility_product.shape[0]
    index = jnp.arange(frequency_channels, dtype=jnp.int32)
    phase = (index[:, None] * index[None, :] % frequency_channels).astype(jnp.float32) * (
        2.0 * math.pi / frequency_channels
    )
    cosine = jnp.cos(phase)
    sine = jnp.sin(phase)
    high = lax.Precision.HIGHEST
    real_part = jnp.einsum(
        "cb,ct->bt", visibility_product[:, 0], cosine, precision=high
    ) + jnp.einsum("cb,ct->bt", visibility_product[:, 1], sine, precision=high)
    imag_part = jnp.einsum(
        "cb,ct->bt", visibility_product[:, 1], cosine, precision=high
    ) - jnp.einsum("cb,ct->bt", visibility_product[:, 0], sine, precision=high)
    weight = 1.0 / jnp.sqrt(frames_all * frequency_channels * jnp.maximum(counts, 1.0))
    return jnp.stack([real_part, imag_part], axis=1) * weight[:, None, None]


def body(samples, feed_input_wiring, input_flags):
    frames_here, inputs_here, length = samples.shape
    group_count = lax.axis_size("tm")
    frames_all = frames_here * group_count
    table = channel_table(NSAMP, CH, CHAN_LO)
    flattened = samples.reshape(frames_here * inputs_here, length)
    spectra = lax.dot_general(
        table, flattened, (((0,), (1,)), ((), ())), preferred_element_type=jnp.float32
    )
    spectra = spectra.astype(jnp.bfloat16).reshape(CH, 2, frames_here, inputs_here)
    turned = lax.all_to_all(
        lax.all_to_all(spectra, "wide", split_axis=0, concat_axis=3, tiled=True),
        "tm",
        split_axis=0,
        concat_axis=2,
        tiled=True,
    )
    partial_sums = correlate(turned, feed_input_wiring, input_flags)
    visibility_product = lax.all_to_all(
        partial_sums, ("wide", "tm"), split_axis=2, concat_axis=0, tiled=True
    )
    local_baseline_pairs = visibility_product.shape[2]
    device_position = lax.axis_index("wide") * group_count + lax.axis_index("tm")
    global_stack_counts = stack_counts(feed_input_wiring, input_flags)
    local_stack_counts = lax.dynamic_slice_in_dim(
        global_stack_counts, device_position * local_baseline_pairs, local_baseline_pairs
    )
    return delay_transform(visibility_product, local_stack_counts, frames_all)


def solution(mesh):
    return jax.shard_map(
        body,
        mesh=mesh,
        in_specs=(P("tm", "wide", None), P(), P()),
        out_specs=P(("wide", "tm"), None, None),
        check_vma=False,
    )
```

profile of v0, /device:TPU:0, one launch (start us, length us, event | category | flops | bytes accessed | tf_op | source)
XLA Modules:
  0.0 575.3 jit_solution(8129795477907743647)
XLA Ops:
  0.0 17.1 %multiply_convert_fusion.1 = (bf16[2048,512,1]{1,0,2:T(8,128)(2,1)S(1)}, bf16[2048,512,1]{1,0,2:T(8,128)(2,1)S(1)}) fusion(s32[512]{0:T(512)S(1)} %iota_add_fusion), kind=kLoop, calls=%fused_computation.18 | loop fusion | flops 19922944 | bytes 4196352 | tf_op jit(solution)/shard_map/convert
  19.4 11.3 %copy.102 = bf16[2048,512,2]{0,2,1:T(2,128)(2,1)} copy(bf16[2048,512,2]{1,0,2:T(8,128)(2,1)} %pad_maximum_fusion) | data formatting | bytes 8388608 | tf_op jit(solution)/shard_map/stack | solution.py:22
  30.8 7.2 %convert_element_type.94 = bf16[2048,1024]{0,1:T(8,128)(2,1)} reshape(bf16[2048,512,2]{0,2,1:T(2,128)(2,1)} %copy.102) | data formatting | bytes 8388608 | tf_op jit(solution)/shard_map/convert_element_type | solution.py:23
  38.0 8.0 %convert_bitcast_fusion = bf16[128,8,8,128]{3,1,2,0:T(8,128)(2,1)S(1)} fusion(bf16[2048,1024]{0,1:T(8,128)(2,1)} %convert_element_type.94, bf16[1024,2048]{1,0:T(8,128)(2,1)} %bitcast.110), kind=kOutput, calls=%fused_computation.27 | convolution fusion | flops 4296015872 | bytes 10485760 | tf_op jit(solution)/shard_map/dot_general | solution.py:118
  46.6 55.3 %all_to_all.54 = bf16[512,2,8,128]{3,2,1,0:T(8,128)(2,1)S(1)} all-to-all(bf16[512,2,8,128]{3,2,1,0:T(8,128)(2,1)S(1)} %bitcast.98), channel_id=1, replica_groups=mesh['wide'=8,'tm'=4] {'wide'}, dimensions={0} | all-to-all | bytes 4194304 | tf_op jit(solution)/shard_map/all_to_all | solution.py:123
  103.9 4.0 all-to-all-start.1
  108.1 4.5 gather_fusion.1
  118.1 15.5 %all-to-all-done.1 = bf16[64,2,8,1024]{3,2,1,0:T(8,128)(2,1)S(1)} async-done(((bf16[64,2,8,1024]{3,2,1,0:T(8,128)(2,1)}), bf16[64,2,8,1024]{3,2,1,0:T(8,128)(2,1)S(1)}, u32[]{:S(2)}, u32[]{:S(2)}) %all-to-all-start.1) | async-done | bytes 2097184 | tf_op jit(solution)/shard_map/all_to_all | solution.py:122
  136.6 8.6 %copy.105 = bf16[16,2,32,1024]{2,0,3,1:T(8,128)(2,1)} copy(bf16[16,2,32,1024]{3,2,1,0:T(8,128)(2,1)S(1)} %bitcast_multiply_fusion) | data formatting | bytes 4194304 | tf_op jit(solution)/shard_map/mul | solution.py:60
  145.2 13.7 %gather_fusion = bf16[1024,16,2,32]{3,1,2,0:T(8,128)(2,1)} fusion(bf16[16,2,32,1024]{2,0,3,1:T(8,128)(2,1)} %copy.105, s32[1024]{0:T(1024)S(1)} %fusion.57), kind=kCustom, calls=%fused_computation | custom fusion | bytes 4198400 | tf_op jit(solution)/shard_map/jit(_take)/gather | solution.py:61
  158.9 9.4 %copy.129 = bf16[16,2,32,4,256]{4,3,2,1,0:T(4,128)(2,1)S(1)} copy(bf16[16,2,32,4,256]{2,0,1,4,3:T(8,128)(2,1)} %bitcast.95) | data formatting | bytes 4194304 | tf_op jit(solution)/shard_map/jit(_take)/gather | solution.py:61
  169.5 10.2 %fusion.9 = f32[16,2,32,4,1024]{4,2,3,1,0:T(8,128)} fusion(bf16[16,2,32,4,256]{4,3,2,1,0:T(4,128)(2,1)S(1)} %broadcast_select_fusion, f32[256,512]{1,0:T(8,128)S(1)} %copy-done.4, f32[256,512]{1,0:T(8,128)S(1)} %copy-done.5), kind=kOutput, calls=%fused_computation.24 | convolution fusion | flops 12885164032 | bytes 19922944 | tf_op jit(solution)/shard_map/cptai,ig->cptag/dot_general | solution.py:68
  179.8 12.2 %fusion.4 = (f32[16,32,4,512]{3,1,2,0:T(8,128)}, f32[16,32,4,512]{3,1,2,0:T(8,128)}) fusion(f32[16,2,32,4,1024]{4,2,3,1,0:T(8,128)} %fusion.9), kind=kLoop, calls=%fused_computation.13 | loop fusion | flops 2097152 | bytes 25165824 | tf_op jit(solution)/shard_map/sub | solution.py:74
  192.0 14.3 %copy.108 = f32[16,32,4,512]{1,2,3,0:T(4,128)} copy(f32[16,32,4,512]{3,1,2,0:T(8,128)} %get-tuple-element.6) | data formatting | bytes 8388608 | tf_op jit(solution)/shard_map/add | solution.py:73
  206.3 24.6 %copy.110 = f32[16,32,4,512]{1,2,3,0:T(4,128)} copy(f32[16,32,4,512]{3,1,2,0:T(8,128)} %get-tuple-element.5) | data formatting | bytes 8388608 | tf_op jit(solution)/shard_map/sub | solution.py:74
  230.9 62.3 %fusion.97 = f32[16,512,4,4]{3,2,1,0:T(4,128)} fusion(f32[16,32,4,512]{1,2,3,0:T(4,128)} %copy.108), kind=kOutput, calls=%fused_computation.139 | convolution fusion | flops 50331648 | bytes 4718592 | tf_op jit(solution)/shard_map/ctaf,ctbf->cabf/dot_general | solution.py:75
  293.2 59.5 %fusion.98 = f32[16,512,4,4]{3,2,1,0:T(4,128)} fusion(f32[16,32,4,512]{1,2,3,0:T(4,128)S(1)} %copy-done.1, f32[16,32,4,512]{1,2,3,0:T(4,128)} %copy.110), kind=kOutput, calls=%fused_computation.140 | convolution fusion | flops 50331648 | bytes 8912896 | tf_op jit(solution)/shard_map/ctaf,ctbf->cabf/dot_general | solution.py:78
  352.6 59.9 %subtract_bitcast_fusion = f32[16,4,4,512]{1,2,3,0:T(4,128)} fusion(f32[16,512,4,4]{3,2,1,0:T(4,128)} %fusion.98, f32[16,32,4,512]{1,2,3,0:T(4,128)} %copy.110, f32[16,32,4,512]{1,2,3,0:T(4,128)S(1)} %copy-done.1), kind=kOutput, calls=%fused_computation.2 | convolution fusion | flops 50462720 | bytes 9437184 | tf_op jit(solution)/shard_map/ctaf,ctbf->cabf/dot_general | solution.py:78
  412.5 10.0 %copy.117 = f32[16,4,4,512]{3,0,2,1:T(8,128)S(1)} copy(f32[16,4,4,512]{1,2,3,0:T(4,128)} %subtract_bitcast_fusion) | data formatting | bytes 1048576 | tf_op jit(solution)/shard_map/sub | solution.py:78
  422.5 61.2 %add_bitcast_fusion = f32[16,4,4,512]{1,2,3,0:T(4,128)} fusion(f32[16,512,4,4]{3,2,1,0:T(4,128)} %fusion.97, f32[16,32,4,512]{1,2,3,0:T(4,128)} %copy.110), kind=kOutput, calls=%fused_computation.3 | convolution fusion | flops 50462720 | bytes 5242880 | tf_op jit(solution)/shard_map/ctaf,ctbf->cabf/dot_general | solution.py:75
  483.7 10.2 %copy.112 = f32[16,4,4,512]{3,0,2,1:T(8,128)S(1)} copy(f32[16,4,4,512]{1,2,3,0:T(4,128)} %add_bitcast_fusion) | data formatting | bytes 1048576 | tf_op jit(solution)/shard_map/add | solution.py:75
  504.8 4.4 copy.122
  509.1 8.0 %reshape.214 = f32[32,1,4096]{2,1,0:T(1,128)} reshape(f32[4096,2,16]{2,1,0:T(2,128)} %bitcast.93) | data formatting | bytes 1048576
  517.1 2.9 all-to-all-start.2
  522.8 4.9 pad.4
  527.7 8.3 %reshape.192 = f32[4,4,256,257]{3,2,1,0:T(8,128)} reshape(f32[4,4,65792]{2,1,0:T(4,128)} %pad.4) | data formatting | bytes 8421376 | tf_op jit(solution)/shard_map/reshape | solution.py:31
  541.2 6.9 %reshape.215 = f32[4096,2,16]{2,1,0:T(2,128)} reshape(f32[32,4096]{1,0:T(8,128)S(1)} %reduce) | data formatting | bytes 1048576
  548.1 5.1 copy.131
  553.2 5.0 fusion.37
  558.2 5.0 fusion.35
  563.2 5.3 fusion.12
  568.5 5.0 fusion.11
  (54 shorter events, 34.7 us)
Async XLA Ops:
  101.9 5.9 %copy-start = (s32[1024]{0:T(1024)S(1)}, s32[1024]{0:T(1024)}, u32[]{:S(2)}) copy-start(s32[1024]{0:T(1024)} %param.5) | copy-start | bytes 12292
  101.9 6.0 %copy-start.6 = (s32[1024]{0:T(1024)S(1)}, s32[1024]{0:T(1024)}, u32[]{:S(2)}) copy-start(s32[1024]{0:T(1024)} %param.4) | copy-start | bytes 12292
  103.9 29.6 %all-to-all-start.1 = ((bf16[64,2,8,1024]{3,2,1,0:T(8,128)(2,1)}), bf16[64,2,8,1024]{3,2,1,0:T(8,128)(2,1)S(1)}, u32[]{:S(2)}, u32[]{:S(2)}) async-start(bf16[64,2,8,1024]{3,2,1,0:T(8,128)(2,1)} %bitcast.97), calls=%async_computation.1 | async-start | bytes 4194304 | tf_op jit(solution)/shard_map/all_to_all | solution.py:122
  133.5 1.3 copy-start.2
  168.3 1.0 copy-start.4
  168.4 1.2 copy-start.5
  230.9 62.3 %copy-start.1 = (f32[16,32,4,512]{1,2,3,0:T(4,128)S(1)}, f32[16,32,4,512]{1,2,3,0:T(4,128)}, u32[]{:S(2)}) copy-start(f32[16,32,4,512]{1,2,3,0:T(4,128)} %copy.108) | copy-start | bytes 12582916
  504.8 15.2 %copy-start.3 = (f32[1,4,256,256]{3,1,2,0:T(4,128)S(1)}, f32[1,4,256,256]{3,1,2,0:T(4,128)}, u32[]{:S(2)}) copy-start(f32[1,4,256,256]{3,1,2,0:T(4,128)} %copy.136) | copy-start | bytes 3145732
  517.1 21.6 %all-to-all-start.2 = ((f32[32,1,4096]{2,1,0:T(1,128)}), f32[32,1,4096]{2,1,0:T(1,128)S(1)}, u32[]{:S(2)}, u32[]{:S(2)}) async-start(f32[32,1,4096]{2,1,0:T(1,128)} %reshape.214), calls=%async_computation.2 | async-start | bytes 1048576 | tf_op jit(solution)/shard_map/all_to_all | solution.py:130
where the time goes:
time: 578 us; the launch traced here: 575 us
  matrix products  291 us (50%)
  local copies, waits for them, and re-layouts  161 us (28%)
  blocking collectives  55.3 us (10%)
  other arithmetic  44.8 us (8%)
  waiting for transfers between devices  15.5 us (3%)
  starting transfers between devices  6.87 us (1%)
    dot_general x1, matrix products, correlate(): jnp.einsum('ctaf,ctbf->cabf', freq_real, freq_real, precision=high)  62.3 us
    dot_general x1, matrix products, correlate(): jnp.einsum('ctaf,ctbf->cabf', freq_imag, freq_imag, precision=high)  61.2 us
    dot_general x1, matrix products, correlate(): jnp.einsum('ctaf,ctbf->cabf', freq_real, freq_imag, precision=high)  59.9 us
    dot_general x1, matrix products, correlate(): jnp.einsum('ctaf,ctbf->cabf', freq_imag, freq_real, precision=high)  59.5 us
    all_to_all x1, blocking collectives, body(): lax.all_to_all(spectra, 'wide', split_axis=0, concat_axis=3, tiled=True)  55.3 us
    sub x1, local copies, waits for them, and re-layouts, correlate(): freq_imag = imag_cos - real_sin  24.6 us
    gather x2, local copies, waits for them, and re-layouts, correlate(): placed = jnp.take(weighted_visibility, feed_input_wiring, axis=3)  23.1 us
    unnamed x22, local copies, waits for them, and re-layouts  19.7 us
  transfers between devices with their start and end apart: 2, of which 1 were waited for; matrix products, arithmetic and copies ran while one was open for 5% of the time, Pallas kernels for 0%

commit v1 on v0

v1 whole, which is shorter than its diff:
```python
import math

import numpy as np
import jax
import jax.numpy as jnp
from jax import lax
from jax.experimental import pallas as pl
from jax.experimental.pallas import tpu as pltpu
from jax.sharding import PartitionSpec as P

CYL = 4
FEEDS = 256
NSAMP = 2048
CH = 512
CHAN_LO = 256
NBASE = 4096

NT = (((1,), (1,)), ((), ()))


def channel_table_const(length, frequency_channels, first):
    samples_at = np.arange(length, dtype=np.int64)
    channel_at = np.arange(frequency_channels, dtype=np.int64) + first
    turns = (channel_at[:, None] * samples_at[None, :]) % length
    phase = turns.astype(np.float32) * np.float32(2.0 * math.pi / length)
    scale = np.float32(1.0 / math.sqrt(length))
    both = np.stack([np.cos(phase) * scale, -np.sin(phase) * scale], axis=1)
    return jnp.asarray(both.reshape(2 * frequency_channels, length), dtype=jnp.bfloat16)


def delay_matrix_const(frequency_channels):
    index = np.arange(frequency_channels, dtype=np.int64)
    phase = ((index[:, None] * index[None, :]) % frequency_channels).astype(np.float32) * np.float32(
        2.0 * math.pi / frequency_channels
    )
    cosine = np.cos(phase).astype(np.float32)
    sine = np.sin(phase).astype(np.float32)
    w = np.zeros((frequency_channels, 2, 2, frequency_channels), np.float32)
    w[:, 0, 0] = cosine
    w[:, 1, 0] = sine
    w[:, 0, 1] = -sine
    w[:, 1, 1] = cosine
    return jnp.asarray(w.reshape(2 * frequency_channels, 2 * frequency_channels))


def pair_keep():
    same = jnp.eye(CYL, dtype=jnp.float32)[:, :, None]
    first = (jnp.arange(FEEDS, dtype=jnp.int32) == 0).astype(jnp.float32)[None, None, :]
    return 1.0 - same * first


def stack_counts(feed_input_wiring, input_flags):
    placed = input_flags[feed_input_wiring].astype(jnp.float32).reshape(CYL, FEEDS)
    padded = jnp.pad(placed, ((0, 0), (0, FEEDS)))[:, None, :]
    kernel = placed[:, None, :]
    corr = lax.conv_general_dilated(
        padded, kernel, (1,), "VALID", dimension_numbers=("NCH", "OIH", "NCH"),
        precision=lax.Precision.HIGHEST,
    )
    counts = jnp.transpose(corr[:, :, :FEEDS], (1, 0, 2))
    return (counts * pair_keep()).reshape(NBASE)


def correlate_kernel(x_ref, pt_ref, ptr_ref, rm_ref, o_ref):
    wide_parts = x_ref.shape[0]
    g = None
    gr = None
    for w in range(wide_parts):
        xw = x_ref[w].reshape(-1, x_ref.shape[-1])
        gw = lax.dot_general(pt_ref[w], xw, NT, preferred_element_type=jnp.float32)
        grw = lax.dot_general(ptr_ref[w], xw, NT, preferred_element_type=jnp.float32)
        g = gw if g is None else g + gw
        gr = grw if gr is None else gr + grw
    g = g.astype(jnp.bfloat16)
    gr = gr.astype(jnp.bfloat16)
    yr = jnp.dot(gr, rm_ref[...], preferred_element_type=jnp.float32).astype(jnp.bfloat16)
    row_at = lax.broadcasted_iota(jnp.int32, (FEEDS, FEEDS), 0)
    col_at = lax.broadcasted_iota(jnp.int32, (FEEDS, FEEDS), 1)
    upper = col_at >= row_at
    for a in range(CYL):
        left = g[a * FEEDS:(a + 1) * FEEDS]
        for b in range(a, CYL):
            for part, right in enumerate((gr, yr)):
                tile = lax.dot_general(
                    left, right[b * FEEDS:(b + 1) * FEEDS], NT, preferred_element_type=jnp.float32
                )
                skewed = pltpu.roll(tile, 0, 1, stride=1, stride_axis=0)
                up = jnp.sum(jnp.where(upper, skewed, 0.0), axis=0, keepdims=True)
                o_ref[0, part, pl.ds(a * CYL + b, 1), :] = up
                if a < b:
                    total = jnp.sum(skewed, axis=0, keepdims=True)
                    o_ref[0, part, pl.ds(b * CYL + a, 1), :] = total - up


def correlate(blocks, pt, ptr, rm):
    wide_parts, tm_parts, local_channels, rows_each, inputs_each = blocks.shape
    return pl.pallas_call(
        correlate_kernel,
        grid=(local_channels,),
        in_specs=[
            pl.BlockSpec((wide_parts, tm_parts, None, rows_each, inputs_each), lambda c: (0, 0, c, 0, 0)),
            pl.BlockSpec(pt.shape, lambda c: (0, 0, 0)),
            pl.BlockSpec(ptr.shape, lambda c: (0, 0, 0)),
            pl.BlockSpec(rm.shape, lambda c: (0, 0)),
        ],
        out_specs=pl.BlockSpec((1, 2, CYL * CYL, FEEDS), lambda c: (c, 0, 0, 0)),
        out_shape=jax.ShapeDtypeStruct((local_channels, 2, CYL * CYL, FEEDS), jnp.float32),
    )(blocks, pt, ptr, rm)


def unskew(sums):
    sign = jnp.array([1.0, -1.0], jnp.float32)[None, :, None]
    pieces = {}
    for a in range(CYL):
        for b in range(a, CYL):
            forward = jnp.flip(sums[:, :, a * CYL + b, :], axis=-1)
            pieces[(a, b)] = forward
            if a < b:
                lower = sums[:, :, b * CYL + a, :]
                backward = jnp.concatenate([forward[:, :, :1], lower[:, :, : FEEDS - 1]], axis=-1)
                pieces[(b, a)] = backward * sign
    stacked = jnp.stack([pieces[(a, b)] for a in range(CYL) for b in range(CYL)], axis=2)
    return stacked * pair_keep().reshape(1, 1, CYL * CYL, FEEDS)


def body(samples, feed_input_wiring, input_flags):
    frames_here, inputs_here, length = samples.shape
    tm_parts = lax.axis_size("tm")
    wide_parts = lax.axis_size("wide")
    devices = tm_parts * wide_parts
    frames_all = frames_here * tm_parts
    local_channels = CH // devices
    table = channel_table_const(NSAMP, CH, CHAN_LO)
    flattened = samples.reshape(frames_here * inputs_here, length)
    spectra = lax.dot_general(table, flattened, NT, preferred_element_type=jnp.float32)
    spectra = spectra.astype(jnp.bfloat16).reshape(devices, local_channels, 2 * frames_here, inputs_here)
    turned = lax.all_to_all(spectra, ("wide", "tm"), 0, 0, tiled=True)
    blocks = turned.reshape(wide_parts, tm_parts, local_channels, 2 * frames_here, inputs_here)

    inputs_all = wide_parts * inputs_here
    flags = input_flags.astype(jnp.bfloat16)
    source = jnp.arange(inputs_all, dtype=jnp.int32)
    feed_at = jnp.arange(CYL * FEEDS, dtype=jnp.int32)
    reversed_at = (feed_at // FEEDS) * FEEDS + (FEEDS - 1 - feed_at % FEEDS)
    wiring_rev = feed_input_wiring[reversed_at]
    pt = jnp.where(feed_input_wiring[:, None] == source[None, :], flags[None, :], jnp.bfloat16(0))
    ptr = jnp.where(wiring_rev[:, None] == source[None, :], flags[None, :], jnp.bfloat16(0))
    pt = pt.reshape(CYL * FEEDS, wide_parts, inputs_here).transpose(1, 0, 2)
    ptr = ptr.reshape(CYL * FEEDS, wide_parts, inputs_here).transpose(1, 0, 2)

    rows = tm_parts * 2 * frames_here
    r_at = np.arange(rows)
    frame_at = r_at % frames_here
    part_at = (r_at // frames_here) % 2
    group_at = r_at // (2 * frames_here)
    rm = np.zeros((rows, rows), np.float32)
    for r in range(rows):
        partner = group_at[r] * 2 * frames_here + (1 - part_at[r]) * frames_here + frame_at[r]
        rm[partner, r] = -1.0 if part_at[r] == 0 else 1.0
    rm = jnp.asarray(rm, dtype=jnp.bfloat16)

    sums = correlate(blocks, pt, ptr, rm)
    partial_sums = unskew(sums).reshape(local_channels, 2, NBASE)
    visibility_product = lax.all_to_all(partial_sums, ("wide", "tm"), 2, 0, tiled=True)
    local_baselines = visibility_product.shape[2]
    device_position = lax.axis_index("wide") * tm_parts + lax.axis_index("tm")
    global_stack_counts = stack_counts(feed_input_wiring, input_flags)
    local_stack_counts = lax.dynamic_slice_in_dim(
        global_stack_counts, device_position * local_baselines, local_baselines
    )
    delay = delay_matrix_const(CH)
    stacked_in = visibility_product.reshape(CH * 2, local_baselines)
    spectra_out = lax.dot_general(
        stacked_in, delay, (((0,), (0,)), ((), ())), precision=lax.Precision.HIGHEST,
        preferred_element_type=jnp.float32,
    )
    weight = 1.0 / jnp.sqrt(frames_all * CH * jnp.maximum(local_stack_counts, 1.0))
    return spectra_out.reshape(local_baselines, 2, CH) * weight[:, None, None]


def solution(mesh):
    return jax.shard_map(
        body,
        mesh=mesh,
        in_specs=(P("tm", "wide", None), P(), P()),
        out_specs=P(("wide", "tm"), None, None),
        check_vma=False,
    )
```

time: 578 us -> 297 us (0.51)
  matrix products: 291 us -> 142 us
  local copies, waits for them, and re-layouts: 161 us -> 49.4 us
  blocking collectives: 55.3 us -> 0 us
  Pallas kernels: 0 us -> 47.8 us
  other arithmetic: 44.8 us -> 5.39 us
  waiting for transfers between devices: 15.5 us -> 36.6 us
    dot_general x14 -> x2, matrix products: 291 us -> 14.7 us  [the longest x1 7.99 us: body(): lax.dot_general(table, flattened, NT, preferred_element_type=jnp.float32)]
    transpose x0 -> x1, matrix products: none -> 127 us  [stack_counts(): counts = jnp.transpose(corr[:, :, :FEEDS], (1, 0, 2))]
    all_to_all x1 -> x0, blocking collectives: 55.3 us -> none  [body(): lax.all_to_all(spectra, 'wide', split_axis=0, concat_axis=3, tiled=True)]
    pallas_call x0 -> x1, Pallas kernels: none -> 47.8 us  [correlate(): pl.pallas_call(correlate_kernel, grid=(local_channels,), in_specs=[pl.Blo...]
    sub x3 -> x0, local copies, waits for them, and re-layouts: 34.8 us -> none  [the longest x1 24.6 us: correlate(): freq_imag = imag_cos - real_sin]
    add x3 -> x0, local copies, waits for them, and re-layouts: 24.7 us -> none  [the longest x1 14.3 us: correlate(): freq_real = real_cos + imag_sin]
    all_to_all x2, waiting for transfers between devices: 15.5 us -> 36.6 us  [the longest x1 36.6 us: body(): turned = lax.all_to_all(spectra, ('wide', 'tm'), 0, 0, tiled=True)]
    another operation x2 -> x0, other arithmetic: 19.4 us -> none
  transfers between devices with their start and end apart: 2 -> 2, of which waited for: 1 -> 1; matrix products, arithmetic and copies ran while one was open for 5% -> 48% of each run, Pallas kernels for 0% -> 0%
where the time goes in v1:
time: 297 us; the launch traced here: 294 us
  matrix products  142 us (48%)
  local copies, waits for them, and re-layouts  49.4 us (17%)
  Pallas kernels  47.8 us (16%)
  waiting for transfers between devices  36.6 us (12%)
  starting transfers between devices  11.5 us (4%)
  other arithmetic  5.39 us (2%)
    transpose x1, matrix products, stack_counts(): counts = jnp.transpose(corr[:, :, :FEEDS], (1, 0, 2))  127 us
    pallas_call x1, Pallas kernels, correlate(): pl.pallas_call(correlate_kernel, grid=(local_channels,), in_specs=[pl.Blo...  47.8 us
    all_to_all x1, waiting for transfers between devices, body(): turned = lax.all_to_all(spectra, ('wide', 'tm'), 0, 0, tiled=True)  36.6 us
    unnamed x38, local copies, waits for them, and re-layouts  16.6 us
    dot_general x1, matrix products, body(): lax.dot_general(table, flattened, NT, preferred_element_type=jnp.float32)  7.99 us
    all_to_all x1, starting transfers between devices, body(): turned = lax.all_to_all(spectra, ('wide', 'tm'), 0, 0, tiled=True)  7.51 us
    dot_general x1, matrix products, body(): lax.dot_general(stacked_in, delay, (((0,), (0,)), ((), ())), precision=la...  6.67 us
  transfers between devices with their start and end apart: 2, of which 1 were waited for; matrix products, arithmetic and copies ran while one was open for 48% of the time, Pallas kernels for 0%

profile of v1, /device:TPU:0, one launch (start us, length us, event | category | flops | bytes accessed | tf_op | source)
XLA Modules:
  0.0 293.6 jit_solution(6327485503324015421)
XLA Ops:
  0.0 8.0 %convolution_convert_fusion = bf16[1024,1024]{1,0:T(8,128)(2,1)S(1)} fusion(bf16[1024,2048]{1,0:T(8,128)(2,1)} %constant.72.clone, bf16[1024,2048]{1,0:T(8,128)(2,1)} %bitcast.149), kind=kOutput, calls=%fused_computation.4 | convolution fusion | flops 4296015872 | bytes 10485760 | tf_op jit(solution)/shard_map/dot_general | solution.py:135
  8.0 2.3 reshape.348
  10.3 7.5 %all-to-all-start = ((bf16[32,16,16,128]{3,2,1,0:T(8,128)(2,1)}), bf16[32,16,16,128]{3,2,1,0:T(8,128)(2,1)S(1)}, u32[]{:S(2)}, u32[]{:S(2)}) async-start(bf16[32,16,16,128]{3,2,1,0:T(8,128)(2,1)} %reshape.348), calls=%async_computation | async-start | bytes 4194304 | tf_op jit(solution)/shard_map/all_to_all | solution.py:137
  17.9 4.5 %gather_fusion.1 = s32[1024]{0:T(1024)S(1)} fusion(s32[1024]{0:T(1024)S(1)} %copy-done.1, s32[1024]{0:T(1024)S(1)} %get-tuple-element.23), kind=kCustom, calls=%fused_computation.1 | custom fusion | bytes 12288 | tf_op jit(solution)/shard_map/gather | solution.py:53
  22.5 4.5 %gather_fusion = s32[1024]{0:T(1024)S(1)} fusion(s32[1024]{0:T(1024)S(1)} %copy-done, s32[1024]{0:T(1024)S(1)} %get-tuple-element.24), kind=kCustom, calls=%fused_computation | custom fusion | bytes 12288 | tf_op jit(solution)/shard_map/gather | solution.py:145
  27.6 2.6 compare_select_fusion
  30.1 36.6 %all-to-all-done = bf16[32,16,16,128]{3,2,1,0:T(8,128)(2,1)S(1)} async-done(((bf16[32,16,16,128]{3,2,1,0:T(8,128)(2,1)}), bf16[32,16,16,128]{3,2,1,0:T(8,128)(2,1)S(1)}, u32[]{:S(2)}, u32[]{:S(2)}) %all-to-all-start) | async-done | bytes 2097184 | tf_op jit(solution)/shard_map/all_to_all | solution.py:137
  66.7 1.3 copy-done.2
  68.0 47.8 %shard_map.73 = f32[16,2,16,256]{3,2,1,0:T(8,128)} custom-call(bf16[8,4,16,16,128]{4,3,2,1,0:T(8,128)(2,1)} %bitcast.115, bf16[8,1024,128]{2,1,0:T(8,128)(2,1)} %get-tuple-element.22.pt_ref, bf16[8,1024,128]{2,1,0:T(8,128)(2,1)} %get-tuple-element.21.ptr_ref, bf16[64,64]{1,0:T(8,128)(2,1)} %constant.73.clone.rm_ref), custom_call_target="tpu_custom_call" | custom-call | tf_op jit(solution)/shard_map/pallas_call | solution.py:97
  115.9 4.2 %fusion.12 = (f32[16,2,1,256]{3,2,1,0:T(1,128)S(1)}, f32[16,2,1,256]{3,2,1,0:T(1,128)S(1)}, f32[16,2,1,256]{3,2,1,0:T(1,128)S(1)}, f32[16,2,1,256]{3,2,1,0:T(1,1...) fusion(f32[16,2,16,256]{3,2,1,0:T(8,128)} %shard_map.73), kind=kLoop, calls=%fused_computation.73 | loop fusion | bytes 1048576 | tf_op jit(solution)/shard_map/slice | solution.py:116
  120.1 0.3 rev.32
  120.5 0.3 rev.33
  120.9 0.3 rev.36
  121.3 0.3 rev.34
  121.7 0.3 rev.37
  122.1 0.3 rev.39
  122.4 0.3 rev.31
  123.0 0.3 rev.35
  123.7 0.3 rev.38
  124.7 0.3 rev.40
  125.8 0.3 copy.135
  126.3 4.4 %copy.136 = f32[16,2,4096]{0,1,2:T(2,128)} copy(f32[16,2,4096]{2,0,1:T(8,128)S(1)} %broadcast_multiply_fusion) | data formatting | bytes 1048576 | tf_op jit(solution)/shard_map/mul | solution.py:123
  130.7 8.0 %reshape.375 = f32[32,1,4096]{2,1,0:T(1,128)} reshape(f32[4096,2,16]{2,1,0:T(2,128)} %bitcast.113) | data formatting | bytes 1048576
  138.7 4.0 %all-to-all-start.1 = ((f32[32,1,4096]{2,1,0:T(1,128)}), f32[32,1,4096]{2,1,0:T(1,128)S(1)}, u32[]{:S(2)}, u32[]{:S(2)}) async-start(f32[32,1,4096]{2,1,0:T(1,128)} %reshape.375), calls=%async_computation.1 | async-start | bytes 1048576 | tf_op jit(solution)/shard_map/all_to_all | solution.py:164
  142.7 127.1 %fusion.13 = f32[4,4,256]{0,1,2:T(4,128)S(1)} fusion(f32[4,1,512]{0,1,2:T(1,128)S(1)} %bitcast.116, f32[4,1,256]{0,1,2:T(1,128)S(1)} %copy.140), kind=kOutput, calls=%fused_computation.74 | convolution fusion | flops 12582912 | bytes 28672 | tf_op jit(solution)/shard_map/transpose | solution.py:60
  270.2 0.5 broadcast.237
  270.7 1.9 reduce
  272.6 6.9 %reshape.376 = f32[4096,2,16]{2,1,0:T(2,128)} reshape(f32[32,4096]{1,0:T(8,128)S(1)} %reduce) | data formatting | bytes 1048576
  279.5 5.2 %copy.137 = f32[16,2,4096]{2,1,0:T(2,128)S(1)} copy(f32[16,2,4096]{0,1,2:T(2,128)} %bitcast.114) | data formatting | bytes 1048576 | tf_op jit(solution)/shard_map/all_to_all | solution.py:164
  284.7 0.5 reshape.353
  285.2 6.7 %convolution_multiply_fusion = f32[128,2,512]{2,0,1:T(8,128)S(1)} fusion(f32[2,512,1024]{2,1,0:T(8,128)} %constant.82, f32[1024,128]{1,0:T(8,128)S(1)} %reshape.353, f32[128]{0:T(128)S(1)} %multiply_rsqrt_fusion), kind=kOutput, calls=%fused_computation.5 | convolution fusion | flops 1610743808 | bytes 5243392 | tf_op jit(solution)/shard_map/dot_general | solution.py:173
  291.9 1.2 copy.142
  (87 shorter events, 3.8 us)
Async XLA Ops:
  8.0 9.9 %copy-start = (s32[1024]{0:T(1024)S(1)}, s32[1024]{0:T(1024)}, u32[]{:S(2)}) copy-start(s32[1024]{0:T(1024)} %param.8) | copy-start | bytes 12292
  8.0 9.9 %copy-start.1 = (s32[1024]{0:T(1024)S(1)}, s32[1024]{0:T(1024)}, u32[]{:S(2)}) copy-start(s32[1024]{0:T(1024)} %param.9) | copy-start | bytes 12292
  10.3 56.4 %all-to-all-start = ((bf16[32,16,16,128]{3,2,1,0:T(8,128)(2,1)}), bf16[32,16,16,128]{3,2,1,0:T(8,128)(2,1)S(1)}, u32[]{:S(2)}, u32[]{:S(2)}) async-start(bf16[32,16,16,128]{3,2,1,0:T(8,128)(2,1)} %reshape.348), calls=%async_computation | async-start | bytes 4194304 | tf_op jit(solution)/shard_map/all_to_all | solution.py:137
  66.7 1.3 copy-start.2
  68.0 57.0 %copy-start.3 = (f32[2]{0:T(128)S(1)}, f32[2]{0:T(128)}, u32[]{:S(2)}) copy-start(f32[2]{0:T(128)} %constant.74.clone) | copy-start | bytes 28
  138.7 131.6 %all-to-all-start.1 = ((f32[32,1,4096]{2,1,0:T(1,128)}), f32[32,1,4096]{2,1,0:T(1,128)S(1)}, u32[]{:S(2)}, u32[]{:S(2)}) async-start(f32[32,1,4096]{2,1,0:T(1,128)} %reshape.375), calls=%async_computation.1 | async-start | bytes 1048576 | tf_op jit(solution)/shard_map/all_to_all | solution.py:164

commit v2 on v1

--- a/solution.py
+++ b/solution.py
@@ -49,20 +49,34 @@
     return 1.0 - same * first
 
 
-def stack_counts(feed_input_wiring, input_flags):
-    placed = input_flags[feed_input_wiring].astype(jnp.float32).reshape(CYL, FEEDS)
-    padded = jnp.pad(placed, ((0, 0), (0, FEEDS)))[:, None, :]
-    kernel = placed[:, None, :]
-    corr = lax.conv_general_dilated(
-        padded, kernel, (1,), "VALID", dimension_numbers=("NCH", "OIH", "NCH"),
-        precision=lax.Precision.HIGHEST,
-    )
-    counts = jnp.transpose(corr[:, :, :FEEDS], (1, 0, 2))
-    return (counts * pair_keep()).reshape(NBASE)
-
-
-def correlate_kernel(x_ref, pt_ref, ptr_ref, rm_ref, o_ref):
+def diag_pairs(left, right, upper, write):
+    for a in range(CYL):
+        for b in range(a, CYL):
+            tile = lax.dot_general(
+                left[a * FEEDS:(a + 1) * FEEDS], right[b * FEEDS:(b + 1) * FEEDS], NT,
+                preferred_element_type=jnp.float32,
+            )
+            skewed = pltpu.roll(tile, 0, 1, stride=1, stride_axis=0)
+            up = jnp.sum(jnp.where(upper, skewed, 0.0), axis=0, keepdims=True)
+            write(a * CYL + b, up)
+            if a < b:
+                total = jnp.sum(skewed, axis=0, keepdims=True)
+                write(b * CYL + a, total - up)
+
+
+def correlate_kernel(x_ref, pt_ref, ptr_ref, rm_ref, fm_ref, fmr_ref, o_ref, n_ref):
     wide_parts = x_ref.shape[0]
+    row_at = lax.broadcasted_iota(jnp.int32, (FEEDS, FEEDS), 0)
+    col_at = lax.broadcasted_iota(jnp.int32, (FEEDS, FEEDS), 1)
+    upper = col_at >= row_at
+
+    @pl.when(pl.program_id(0) == 0)
+    def _():
+        def write_count(slot, value):
+            n_ref[pl.ds(slot, 1), :] = value
+
+        diag_pairs(fm_ref[...], fmr_ref[...], upper, write_count)
+
     g = None
     gr = None
     for w in range(wide_parts):
@@ -74,25 +88,14 @@
     g = g.astype(jnp.bfloat16)
     gr = gr.astype(jnp.bfloat16)
     yr = jnp.dot(gr, rm_ref[...], preferred_element_type=jnp.float32).astype(jnp.bfloat16)
-    row_at = lax.broadcasted_iota(jnp.int32, (FEEDS, FEEDS), 0)
-    col_at = lax.broadcasted_iota(jnp.int32, (FEEDS, FEEDS), 1)
-    upper = col_at >= row_at
-    for a in range(CYL):
-        left = g[a * FEEDS:(a + 1) * FEEDS]
-        for b in range(a, CYL):
-            for part, right in enumerate((gr, yr)):
-                tile = lax.dot_general(
-                    left, right[b * FEEDS:(b + 1) * FEEDS], NT, preferred_element_type=jnp.float32
-                )
-                skewed = pltpu.roll(tile, 0, 1, stride=1, stride_axis=0)
-                up = jnp.sum(jnp.where(upper, skewed, 0.0), axis=0, keepdims=True)
-                o_ref[0, part, pl.ds(a * CYL + b, 1), :] = up
-                if a < b:
-                    total = jnp.sum(skewed, axis=0, keepdims=True)
-                    o_ref[0, part, pl.ds(b * CYL + a, 1), :] = total - up
-
-
-def correlate(blocks, pt, ptr, rm):
+    for part, right in enumerate((gr, yr)):
+        def write_vis(slot, value, part=part):
+            o_ref[0, part, pl.ds(slot, 1), :] = value
+
+        diag_pairs(g, right, upper, write_vis)
+
+
+def correlate(blocks, pt, ptr, rm, fm, fmr):
     wide_parts, tm_parts, local_channels, rows_each, inputs_each = blocks.shape
     return pl.pallas_call(
         correlate_kernel,
@@ -102,25 +105,32 @@
             pl.BlockSpec(pt.shape, lambda c: (0, 0, 0)),
             pl.BlockSpec(ptr.shape, lambda c: (0, 0, 0)),
             pl.BlockSpec(rm.shape, lambda c: (0, 0)),
+            pl.BlockSpec(fm.shape, lambda c: (0, 0)),
+            pl.BlockSpec(fmr.shape, lambda c: (0, 0)),
         ],
-        out_specs=pl.BlockSpec((1, 2, CYL * CYL, FEEDS), lambda c: (c, 0, 0, 0)),
-        out_shape=jax.ShapeDtypeStruct((local_channels, 2, CYL * CYL, FEEDS), jnp.float32),
-    )(blocks, pt, ptr, rm)
-
-
-def unskew(sums):
-    sign = jnp.array([1.0, -1.0], jnp.float32)[None, :, None]
+        out_specs=[
+            pl.BlockSpec((1, 2, CYL * CYL, FEEDS), lambda c: (c, 0, 0, 0)),
+            pl.BlockSpec((CYL * CYL, FEEDS), lambda c: (0, 0)),
+        ],
+        out_shape=[
+            jax.ShapeDtypeStruct((local_channels, 2, CYL * CYL, FEEDS), jnp.float32),
+            jax.ShapeDtypeStruct((CYL * CYL, FEEDS), jnp.float32),
+        ],
+    )(blocks, pt, ptr, rm, fm, fmr)
+
+
+def unskew(sums, sign):
     pieces = {}
     for a in range(CYL):
         for b in range(a, CYL):
-            forward = jnp.flip(sums[:, :, a * CYL + b, :], axis=-1)
+            forward = jnp.flip(sums[..., a * CYL + b, :], axis=-1)
             pieces[(a, b)] = forward
             if a < b:
-                lower = sums[:, :, b * CYL + a, :]
-                backward = jnp.concatenate([forward[:, :, :1], lower[:, :, : FEEDS - 1]], axis=-1)
+                lower = sums[..., b * CYL + a, :]
+                backward = jnp.concatenate([forward[..., :1], lower[..., : FEEDS - 1]], axis=-1)
                 pieces[(b, a)] = backward * sign
-    stacked = jnp.stack([pieces[(a, b)] for a in range(CYL) for b in range(CYL)], axis=2)
-    return stacked * pair_keep().reshape(1, 1, CYL * CYL, FEEDS)
+    stacked = jnp.stack([pieces[(a, b)] for a in range(CYL) for b in range(CYL)], axis=-2)
+    return stacked * pair_keep().reshape(CYL * CYL, FEEDS)
 
 
 def body(samples, feed_input_wiring, input_flags):
@@ -140,13 +150,14 @@
     inputs_all = wide_parts * inputs_here
     flags = input_flags.astype(jnp.bfloat16)
     source = jnp.arange(inputs_all, dtype=jnp.int32)
-    feed_at = jnp.arange(CYL * FEEDS, dtype=jnp.int32)
-    reversed_at = (feed_at // FEEDS) * FEEDS + (FEEDS - 1 - feed_at % FEEDS)
-    wiring_rev = feed_input_wiring[reversed_at]
-    pt = jnp.where(feed_input_wiring[:, None] == source[None, :], flags[None, :], jnp.bfloat16(0))
-    ptr = jnp.where(wiring_rev[:, None] == source[None, :], flags[None, :], jnp.bfloat16(0))
-    pt = pt.reshape(CYL * FEEDS, wide_parts, inputs_here).transpose(1, 0, 2)
-    ptr = ptr.reshape(CYL * FEEDS, wide_parts, inputs_here).transpose(1, 0, 2)
+    wiring_rev = jnp.flip(feed_input_wiring.reshape(CYL, FEEDS), axis=1).reshape(CYL * FEEDS)
+    pt_full = jnp.where(feed_input_wiring[:, None] == source[None, :], flags[None, :], jnp.bfloat16(0))
+    ptr_full = jnp.where(wiring_rev[:, None] == source[None, :], flags[None, :], jnp.bfloat16(0))
+    first_lane = (lax.broadcasted_iota(jnp.int32, (CYL * FEEDS, 128), 1) == 0).astype(jnp.bfloat16)
+    fm = jnp.sum(pt_full.astype(jnp.float32), axis=1).astype(jnp.bfloat16)[:, None] * first_lane
+    fmr = jnp.sum(ptr_full.astype(jnp.float32), axis=1).astype(jnp.bfloat16)[:, None] * first_lane
+    pt = pt_full.reshape(CYL * FEEDS, wide_parts, inputs_here).transpose(1, 0, 2)
+    ptr = ptr_full.reshape(CYL * FEEDS, wide_parts, inputs_here).transpose(1, 0, 2)
 
     rows = tm_parts * 2 * frames_here
     r_at = np.arange(rows)
@@ -159,17 +170,19 @@
         rm[partner, r] = -1.0 if part_at[r] == 0 else 1.0
     rm = jnp.asarray(rm, dtype=jnp.bfloat16)
 
-    sums = correlate(blocks, pt, ptr, rm)
-    partial_sums = unskew(sums).reshape(local_channels, 2, NBASE)
-    visibility_product = lax.all_to_all(partial_sums, ("wide", "tm"), 2, 0, tiled=True)
-    local_baselines = visibility_product.shape[2]
+    sums, count_sums = correlate(blocks, pt, ptr, rm, fm, fmr)
+    conj_sign = jnp.array([1.0, -1.0], jnp.float32)[None, :, None]
+    vis = unskew(sums, conj_sign)
+    local_baselines = NBASE // devices
+    send = vis.reshape(local_channels, 2, devices, local_baselines).transpose(2, 0, 1, 3)
+    received = lax.all_to_all(send, ("wide", "tm"), 0, 0, tiled=True)
+    stacked_in = received.reshape(CH * 2, local_baselines)
     device_position = lax.axis_index("wide") * tm_parts + lax.axis_index("tm")
-    global_stack_counts = stack_counts(feed_input_wiring, input_flags)
+    global_stack_counts = unskew(count_sums, 1.0).reshape(NBASE)
     local_stack_counts = lax.dynamic_slice_in_dim(
         global_stack_counts, device_position * local_baselines, local_baselines
     )
     delay = delay_matrix_const(CH)
-    stacked_in = visibility_product.reshape(CH * 2, local_baselines)
     spectra_out = lax.dot_general(
         stacked_in, delay, (((0,), (0,)), ((), ())), precision=lax.Precision.HIGHEST,
         preferred_element_type=jnp.float32,

time: 297 us -> 156 us (0.53)
  matrix products: 142 us -> 14.6 us
  local copies, waits for them, and re-layouts: 49.4 us -> 18.2 us
  waiting for transfers between devices: 36.6 us -> 51.8 us
  other arithmetic: 5.39 us -> 10.1 us
    transpose x1 -> x0, matrix products: 127 us -> none  [stack_counts(): counts = jnp.transpose(corr[:, :, :FEEDS], (1, 0, 2))]
    unnamed x38 -> x20, local copies, waits for them, and re-layouts: 16.6 us -> 1.47 us
    gather x2 -> x0, local copies, waits for them, and re-layouts: 9.06 us -> none  [the longest x1 4.53 us: stack_counts(): input_flags[feed_input_wiring].astype(jnp.float32).reshape(CYL, FEEDS)]
    all_to_all x1, waiting for transfers between devices: 0.01 us -> 8.51 us  [body(): received = lax.all_to_all(send, ('wide', 'tm'), 0, 0, tiled=True)]
    all_to_all x1, waiting for transfers between devices: 36.6 us -> 43.3 us  [body(): turned = lax.all_to_all(spectra, ('wide', 'tm'), 0, 0, tiled=True)]
    all_to_all x2 -> x0, local copies, waits for them, and re-layouts: 5.7 us -> none  [body(): lax.all_to_all(partial_sums, ('wide', 'tm'), 2, 0, tiled=True)]
    mul x1 -> x0, local copies, waits for them, and re-layouts: 4.38 us -> none  [unskew(): return stacked * pair_keep().reshape(1, 1, CYL * CYL, FEEDS)]
    concatenate x0 -> x6, other arithmetic: none -> 4.12 us  [unskew(): jnp.concatenate([forward[..., :1], lower[..., :FEEDS - 1]], axis=-1)]
  transfers between devices with their start and end apart: 2 -> 2, of which waited for: 1 -> 2; matrix products, arithmetic and copies ran while one was open for 48% -> 8% of each run, Pallas kernels for 0% -> 0%
where the time goes in v2:
time: 156 us; the launch traced here: 155 us
  waiting for transfers between devices  51.8 us (33%)
  Pallas kernels  48.4 us (31%)
  local copies, waits for them, and re-layouts  18.2 us (12%)
  matrix products  14.6 us (9%)
  starting transfers between devices  11.5 us (7%)
  other arithmetic  10.1 us (6%)
    pallas_call x1, Pallas kernels, correlate(): pl.pallas_call(correlate_kernel, grid=(local_channels,), in_specs=[pl.Blo...  48.4 us
    all_to_all x1, waiting for transfers between devices, body(): turned = lax.all_to_all(spectra, ('wide', 'tm'), 0, 0, tiled=True)  43.3 us
    all_to_all x1, waiting for transfers between devices, body(): received = lax.all_to_all(send, ('wide', 'tm'), 0, 0, tiled=True)  8.51 us
    dot_general x1, matrix products, body(): lax.dot_general(table, flattened, NT, preferred_element_type=jnp.float32)  7.99 us
    all_to_all x1, starting transfers between devices, body(): turned = lax.all_to_all(spectra, ('wide', 'tm'), 0, 0, tiled=True)  7.3 us
    dot_general x1, matrix products, body(): lax.dot_general(stacked_in, delay, (((0,), (0,)), ((), ())), precision=la...  6.66 us
    all_to_all x1, starting transfers between devices, body(): received = lax.all_to_all(send, ('wide', 'tm'), 0, 0, tiled=True)  4.18 us
    concatenate x6, other arithmetic, unskew(): jnp.concatenate([forward[..., :1], lower[..., :FEEDS - 1]], axis=-1)  4.12 us
  transfers between devices with their start and end apart: 2, of which 2 were waited for; matrix products, arithmetic and copies ran while one was open for 8% of the time, Pallas kernels for 0%

profile of v2, /device:TPU:0, one launch (start us, length us, event | category | flops | bytes accessed | tf_op | source)
XLA Modules:
  0.0 155.1 jit_solution(12956352926574295496)
XLA Ops:
  0.0 8.0 %convolution_convert_fusion = bf16[1024,1024]{1,0:T(8,128)(2,1)S(1)} fusion(bf16[1024,2048]{1,0:T(8,128)(2,1)} %constant.42.clone, bf16[1024,2048]{1,0:T(8,128)(2,1)} %bitcast.178), kind=kOutput, calls=%fused_computation.8 | convolution fusion | flops 4296015872 | bytes 10485760 | tf_op jit(solution)/shard_map/dot_general | solution.py:145
  8.0 2.3 %reshape.292 = bf16[32,16,16,128]{3,2,1,0:T(8,128)(2,1)} reshape(bf16[1024,1024]{1,0:T(8,128)(2,1)S(1)} %convolution_convert_fusion) | data formatting | bytes 4194304 | tf_op jit(solution)/shard_map/reshape | solution.py:146
  10.3 7.3 %all-to-all-start = ((bf16[32,16,16,128]{3,2,1,0:T(8,128)(2,1)}), bf16[32,16,16,128]{3,2,1,0:T(8,128)(2,1)S(1)}, u32[]{:S(2)}, u32[]{:S(2)}) async-start(bf16[32,16,16,128]{3,2,1,0:T(8,128)(2,1)} %reshape.292), calls=%async_computation | async-start | bytes 4194304 | tf_op jit(solution)/shard_map/all_to_all | solution.py:147
  18.1 1.4 fusion.2
  19.5 1.1 broadcast_select_fusion
  20.7 2.5 %compare_select_fusion = (bf16[8,1024,128]{2,1,0:T(8,128)(2,1)}, bf16[8,1024,128]{2,1,0:T(8,128)(2,1)}) fusion(s32[8,128]{1,0:T(8,128)S(1)} %multiply_add_fusion, s32[1024]{0:T(1024)S(1)} %bitcast.137, bf16[8,128]{1,0:T(8,128)(2,1)S(1)} %convert_bitcast_fusion, s32[1024]{0:T(1024)S(1)} %copy-done.2), kind=kLoop, calls=%fused_computation.4 | loop fusion | flops 4194304 | bytes 4208640 | tf_op jit(solution)/shard_map/jit(_where)/select_n | solution.py:155
  23.2 43.3 %all-to-all-done = bf16[32,16,16,128]{3,2,1,0:T(8,128)(2,1)S(1)} async-done(((bf16[32,16,16,128]{3,2,1,0:T(8,128)(2,1)}), bf16[32,16,16,128]{3,2,1,0:T(8,128)(2,1)S(1)}, u32[]{:S(2)}, u32[]{:S(2)}) %all-to-all-start) | async-done | bytes 2097184 | tf_op jit(solution)/shard_map/all_to_all | solution.py:147
  66.5 1.3 copy-done
  67.9 48.4 %shard_map.73 = (f32[16,2,16,256]{3,2,1,0:T(8,128)}, f32[16,256]{1,0:T(8,128)}) custom-call(bf16[8,4,16,16,128]{4,3,2,1,0:T(8,128)(2,1)} %bitcast.132, bf16[8,1024,128]{2,1,0:T(8,128)(2,1)} %get-tuple-element.49.pt_ref, bf16[8,1024,128]{2,1,0:T(8,128)(2,1)} %get-tuple-element.48.ptr_ref, bf16[64,64]{1,0:T(8,128)(2,1)} %constant.43.clone.rm_ref, ...), custom_call_target="tpu_custom_call" | custom-call | tf_op jit(solution)/shard_map/pallas_call | solution.py:100
  116.3 1.4 copy.98
  117.9 0.3 rev.68
  118.3 0.3 rev.69
  119.0 0.3 rev.70
  119.4 0.3 rev.73
  119.7 0.3 rev.75
  120.1 1.0 slice.243
  121.1 1.0 fusion.5
  122.0 0.9 fusion.7
  124.9 0.3 rev.76
  126.1 0.3 copy.125
  126.5 1.2 copy.126
  127.7 4.2 %all-to-all-start.1 = ((f32[32,16,2,128]{3,2,1,0:T(2,128)}), f32[32,16,2,128]{3,2,1,0:T(2,128)S(1)}, u32[]{:S(2)}, u32[]{:S(2)}) async-start(f32[32,16,2,128]{3,2,1,0:T(2,128)} %copy.126), calls=%async_computation.1 | async-start | bytes 1048576 | tf_op jit(solution)/shard_map/all_to_all | solution.py:178
  131.9 1.5 fusion.6
  134.4 0.8 pad_maximum_fusion
  135.2 0.6 pad_maximum_fusion.1
  135.8 0.7 pad_maximum_fusion.2
  136.5 0.7 pad_maximum_fusion.3
  137.2 0.7 pad_maximum_fusion.4
  137.9 0.6 pad_maximum_fusion.5
  138.7 8.5 %all-to-all-done.1 = f32[32,16,2,128]{3,2,1,0:T(2,128)S(1)} async-done(((f32[32,16,2,128]{3,2,1,0:T(2,128)}), f32[32,16,2,128]{3,2,1,0:T(2,128)S(1)}, u32[]{:S(2)}, u32[]{:S(2)}) %all-to-all-start.1) | async-done | bytes 524320 | tf_op jit(solution)/shard_map/all_to_all | solution.py:178
  147.3 6.7 %convolution_multiply_fusion = f32[128,2,512]{2,0,1:T(8,128)S(1)} fusion(f32[1024,128,1]{1,0,2:T(8,128)S(1)} %bitcast.133, f32[2,512,1024]{2,1,0:T(8,128)} %constant.47, f32[128]{0:T(128)S(1)} %multiply_rsqrt_fusion), kind=kOutput, calls=%fused_computation.9 | convolution fusion | flops 1610743808 | bytes 5243392 | tf_op jit(solution)/shard_map/dot_general | solution.py:186
  153.9 1.2 copy.128
  (81 shorter events, 5.4 us)
Async XLA Ops:
  8.0 9.6 %copy-start.2 = (s32[1024]{0:T(1024)S(1)}, s32[1024]{0:T(1024)}, u32[]{:S(2)}) copy-start(s32[1024]{0:T(1024)} %param.8) | copy-start | bytes 12292
  8.0 9.8 %copy-start.3 = (s32[1024]{0:T(1024)S(1)}, s32[1024]{0:T(1024)}, u32[]{:S(2)}) copy-start(s32[1024]{0:T(1024)} %param.9) | copy-start | bytes 12292
  10.3 56.2 %all-to-all-start = ((bf16[32,16,16,128]{3,2,1,0:T(8,128)(2,1)}), bf16[32,16,16,128]{3,2,1,0:T(8,128)(2,1)S(1)}, u32[]{:S(2)}, u32[]{:S(2)}) async-start(bf16[32,16,16,128]{3,2,1,0:T(8,128)(2,1)} %reshape.292), calls=%async_computation | async-start | bytes 4194304 | tf_op jit(solution)/shard_map/all_to_all | solution.py:147
  66.5 1.3 copy-start
  67.9 57.4 %copy-start.1 = (f32[2]{0:T(128)S(1)}, f32[2]{0:T(128)}, u32[]{:S(2)}) copy-start(f32[2]{0:T(128)} %constant.44.clone) | copy-start | bytes 28
  127.7 19.6 %all-to-all-start.1 = ((f32[32,16,2,128]{3,2,1,0:T(2,128)}), f32[32,16,2,128]{3,2,1,0:T(2,128)S(1)}, u32[]{:S(2)}, u32[]{:S(2)}) async-start(f32[32,16,2,128]{3,2,1,0:T(2,128)} %copy.126), calls=%async_computation.1 | async-start | bytes 1048576 | tf_op jit(solution)/shard_map/all_to_all | solution.py:178

commit v3 on v2

--- a/solution.py
+++ b/solution.py
@@ -1,3 +1,4 @@
+import functools
 import math
 
 import numpy as np
@@ -25,7 +26,7 @@
     phase = turns.astype(np.float32) * np.float32(2.0 * math.pi / length)
     scale = np.float32(1.0 / math.sqrt(length))
     both = np.stack([np.cos(phase) * scale, -np.sin(phase) * scale], axis=1)
-    return jnp.asarray(both.reshape(2 * frequency_channels, length), dtype=jnp.bfloat16)
+    return both.reshape(2 * frequency_channels, length)
 
 
 def delay_matrix_const(frequency_channels):
@@ -64,18 +65,23 @@
                 write(b * CYL + a, total - up)
 
 
-def correlate_kernel(x_ref, pt_ref, ptr_ref, rm_ref, fm_ref, fmr_ref, o_ref, n_ref):
+def correlate_kernel(*refs, with_counts):
+    if with_counts:
+        x_ref, pt_ref, ptr_ref, rm_ref, fm_ref, fmr_ref, o_ref, n_ref = refs
+    else:
+        x_ref, pt_ref, ptr_ref, rm_ref, o_ref = refs
     wide_parts = x_ref.shape[0]
     row_at = lax.broadcasted_iota(jnp.int32, (FEEDS, FEEDS), 0)
     col_at = lax.broadcasted_iota(jnp.int32, (FEEDS, FEEDS), 1)
     upper = col_at >= row_at
 
-    @pl.when(pl.program_id(0) == 0)
-    def _():
-        def write_count(slot, value):
-            n_ref[pl.ds(slot, 1), :] = value
-
-        diag_pairs(fm_ref[...], fmr_ref[...], upper, write_count)
+    if with_counts:
+        @pl.when(pl.program_id(0) == 0)
+        def _():
+            def write_count(slot, value):
+                n_ref[pl.ds(slot, 1), :] = value
+
+            diag_pairs(fm_ref[...], fmr_ref[...], upper, write_count)
 
     g = None
     gr = None
@@ -95,28 +101,38 @@
         diag_pairs(g, right, upper, write_vis)
 
 
-def correlate(blocks, pt, ptr, rm, fm, fmr):
+def correlate(blocks, pt, ptr, rm, fm=None, fmr=None):
     wide_parts, tm_parts, local_channels, rows_each, inputs_each = blocks.shape
+    with_counts = fm is not None
+    in_specs = [
+        pl.BlockSpec((wide_parts, tm_parts, None, rows_each, inputs_each), lambda c: (0, 0, c, 0, 0)),
+        pl.BlockSpec(pt.shape, lambda c: (0, 0, 0)),
+        pl.BlockSpec(ptr.shape, lambda c: (0, 0, 0)),
+        pl.BlockSpec(rm.shape, lambda c: (0, 0)),
+    ]
+    out_specs = [pl.BlockSpec((1, 2, CYL * CYL, FEEDS), lambda c: (c, 0, 0, 0))]
+    out_shape = [jax.ShapeDtypeStruct((local_channels, 2, CYL * CYL, FEEDS), jnp.float32)]
+    operands = [blocks, pt, ptr, rm]
+    if with_counts:
+        in_specs += [pl.BlockSpec(fm.shape, lambda c: (0, 0)), pl.BlockSpec(fmr.shape, lambda c: (0, 0))]
+        out_specs.append(pl.BlockSpec((CYL * CYL, FEEDS), lambda c: (0, 0)))
+        out_shape.append(jax.ShapeDtypeStruct((CYL * CYL, FEEDS), jnp.float32))
+        operands += [fm, fmr]
+    positions = CYL * FEEDS
+    rows = tm_parts * rows_each
+    flops = local_channels * (
+        2 * 2 * positions * wide_parts * inputs_each * rows + 2 * positions * rows * rows
+        + 20 * 2 * FEEDS * FEEDS * rows
+    )
+    bytes_accessed = blocks.size * 2 + pt.size * 4 + local_channels * 2 * CYL * CYL * FEEDS * 4
     return pl.pallas_call(
-        correlate_kernel,
+        functools.partial(correlate_kernel, with_counts=with_counts),
         grid=(local_channels,),
-        in_specs=[
-            pl.BlockSpec((wide_parts, tm_parts, None, rows_each, inputs_each), lambda c: (0, 0, c, 0, 0)),
-            pl.BlockSpec(pt.shape, lambda c: (0, 0, 0)),
-            pl.BlockSpec(ptr.shape, lambda c: (0, 0, 0)),
-            pl.BlockSpec(rm.shape, lambda c: (0, 0)),
-            pl.BlockSpec(fm.shape, lambda c: (0, 0)),
-            pl.BlockSpec(fmr.shape, lambda c: (0, 0)),
-        ],
-        out_specs=[
-            pl.BlockSpec((1, 2, CYL * CYL, FEEDS), lambda c: (c, 0, 0, 0)),
-            pl.BlockSpec((CYL * CYL, FEEDS), lambda c: (0, 0)),
-        ],
-        out_shape=[
-            jax.ShapeDtypeStruct((local_channels, 2, CYL * CYL, FEEDS), jnp.float32),
-            jax.ShapeDtypeStruct((CYL * CYL, FEEDS), jnp.float32),
-        ],
-    )(blocks, pt, ptr, rm, fm, fmr)
+        in_specs=in_specs,
+        out_specs=out_specs,
+        out_shape=out_shape,
+        cost_estimate=pl.CostEstimate(flops=flops, transcendentals=0, bytes_accessed=bytes_accessed),
+    )(*operands)
 
 
 def unskew(sums, sign):
@@ -141,11 +157,19 @@
     frames_all = frames_here * tm_parts
     local_channels = CH // devices
     table = channel_table_const(NSAMP, CH, CHAN_LO)
+    chunks = math.gcd(4, local_channels)
+    chunk_channels = local_channels // chunks
+    table = table.reshape(devices, chunks, chunk_channels * 2, length).transpose(1, 0, 2, 3)
+    table = jnp.asarray(table.reshape(chunks, devices * chunk_channels * 2, length), dtype=jnp.bfloat16)
     flattened = samples.reshape(frames_here * inputs_here, length)
-    spectra = lax.dot_general(table, flattened, NT, preferred_element_type=jnp.float32)
-    spectra = spectra.astype(jnp.bfloat16).reshape(devices, local_channels, 2 * frames_here, inputs_here)
-    turned = lax.all_to_all(spectra, ("wide", "tm"), 0, 0, tiled=True)
-    blocks = turned.reshape(wide_parts, tm_parts, local_channels, 2 * frames_here, inputs_here)
+    chunk_blocks = []
+    for j in range(chunks):
+        spectra = lax.dot_general(table[j], flattened, NT, preferred_element_type=jnp.float32)
+        spectra = spectra.astype(jnp.bfloat16).reshape(devices, chunk_channels, 2 * frames_here, inputs_here)
+        turned = lax.all_to_all(spectra, ("wide", "tm"), 0, 0, tiled=True)
+        chunk_blocks.append(
+            turned.reshape(wide_parts, tm_parts, chunk_channels, 2 * frames_here, inputs_here)
+        )
 
     inputs_all = wide_parts * inputs_here
     flags = input_flags.astype(jnp.bfloat16)
@@ -170,7 +194,9 @@
         rm[partner, r] = -1.0 if part_at[r] == 0 else 1.0
     rm = jnp.asarray(rm, dtype=jnp.bfloat16)
 
-    sums, count_sums = correlate(blocks, pt, ptr, rm, fm, fmr)
+    sums, count_sums = correlate(chunk_blocks[0], pt, ptr, rm, fm, fmr)
+    sums = [sums] + [correlate(blk, pt, ptr, rm)[0] for blk in chunk_blocks[1:]]
+    sums = jnp.concatenate(sums, axis=0)
     conj_sign = jnp.array([1.0, -1.0], jnp.float32)[None, :, None]
     vis = unskew(sums, conj_sign)
     local_baselines = NBASE // devices

time: 156 us -> 167 us (1.071)
  waiting for transfers between devices: 51.8 us -> 35.7 us
  starting transfers between devices: 11.5 us -> 22.3 us
  Pallas kernels: 48.4 us -> 56.8 us
  matrix products: 14.6 us -> 21.4 us
    all_to_all x1 -> x4, waiting for transfers between devices: 43.3 us -> 27.1 us  [body(): turned = lax.all_to_all(spectra, ('wide', 'tm'), 0, 0, tiled=True)]
    all_to_all x1 -> x4, starting transfers between devices: 7.3 us -> 16.7 us  [body(): turned = lax.all_to_all(spectra, ('wide', 'tm'), 0, 0, tiled=True)]
    pallas_call x1 -> x4, Pallas kernels: 48.4 us -> 56.8 us  [correlate(): pl.pallas_call(functools.partial(correlate_kernel, with_counts=with_count...]
    dot_general x1 -> x4, matrix products: 7.99 us -> 14.7 us  [body(): lax.dot_general(table[j], flattened, NT, preferred_element_type=jnp.float32)]
    reshape x1 -> x4, local copies, waits for them, and re-layouts: 2.3 us -> 4.1 us  [body(): spectra.astype(jnp.bfloat16)]
  transfers between devices with their start and end apart: 2 -> 5, of which waited for: 2 -> 4; matrix products, arithmetic and copies ran while one was open for 8% -> 17% of each run, Pallas kernels for 0% -> 26%
where the time goes in v3:
time: 167 us; the launch traced here: 166 us
  Pallas kernels  56.8 us (34%)
  waiting for transfers between devices  35.7 us (21%)
  starting transfers between devices  22.3 us (13%)
  matrix products  21.4 us (13%)
  local copies, waits for them, and re-layouts  17.9 us (11%)
  other arithmetic  11.2 us (7%)
    pallas_call x4, Pallas kernels, correlate(): pl.pallas_call(functools.partial(correlate_kernel, with_counts=with_count...  56.8 us
    all_to_all x4, waiting for transfers between devices, body(): turned = lax.all_to_all(spectra, ('wide', 'tm'), 0, 0, tiled=True)  27.1 us
    all_to_all x4, starting transfers between devices, body(): turned = lax.all_to_all(spectra, ('wide', 'tm'), 0, 0, tiled=True)  16.7 us
    dot_general x4, matrix products, body(): lax.dot_general(table[j], flattened, NT, preferred_element_type=jnp.float32)  14.7 us
    all_to_all x1, waiting for transfers between devices, body(): received = lax.all_to_all(send, ('wide', 'tm'), 0, 0, tiled=True)  8.64 us
    dot_general x1, matrix products, body(): lax.dot_general(stacked_in, delay, (((0,), (0,)), ((), ())), precision=la...  6.76 us
    all_to_all x1, starting transfers between devices, body(): received = lax.all_to_all(send, ('wide', 'tm'), 0, 0, tiled=True)  5.65 us
    concatenate x6, other arithmetic, unskew(): jnp.concatenate([forward[..., :1], lower[..., :FEEDS - 1]], axis=-1)  4.17 us
  transfers between devices with their start and end apart: 5, of which 4 were waited for; matrix products, arithmetic and copies ran while one was open for 17% of the time, Pallas kernels for 26%

profile of v3, /device:TPU:0, one launch (start us, length us, event | category | flops | bytes accessed | tf_op | source)
XLA Modules:
  0.0 165.9 jit_solution(2405525822908911068)
XLA Ops:
  0.0 3.9 %convolution_convert_fusion.3 = bf16[256,1024]{1,0:T(8,128)(2,1)S(1)} fusion(bf16[256,2048]{1,0:T(8,128)(2,1)} %constant.47, bf16[1024,2048]{1,0:T(8,128)(2,1)} %bitcast.192), kind=kOutput, calls=%fused_computation.11 | convolution fusion | flops 1074003968 | bytes 5767168 | tf_op jit(solution)/shard_map/dot_general | solution.py:167
  3.9 1.0 reshape.310
  4.9 7.3 %all-to-all-start = ((bf16[32,4,16,128]{3,2,1,0:T(8,128)(2,1)}), bf16[32,4,16,128]{3,2,1,0:T(8,128)(2,1)S(1)}, u32[]{:S(2)}, u32[]{:S(2)}) async-start(bf16[32,4,16,128]{3,2,1,0:T(8,128)(2,1)} %reshape.310), calls=%async_computation | async-start | bytes 1048576 | tf_op jit(solution)/shard_map/all_to_all | solution.py:169
  12.2 3.5 %convolution_convert_fusion.2 = bf16[256,1024]{1,0:T(8,128)(2,1)S(1)} fusion(bf16[256,2048]{1,0:T(8,128)(2,1)S(1)} %copy-done.11, bf16[1024,2048]{1,0:T(8,128)(2,1)} %bitcast.193), kind=kOutput, calls=%fused_computation.10 | convolution fusion | flops 1074003968 | bytes 5767168 | tf_op jit(solution)/shard_map/dot_general | solution.py:167
  15.7 1.0 reshape.313
  16.7 3.9 %convolution_convert_fusion.1 = bf16[256,1024]{1,0:T(8,128)(2,1)S(1)} fusion(bf16[256,2048]{1,0:T(8,128)(2,1)} %constant.51, bf16[1024,2048]{1,0:T(8,128)(2,1)} %bitcast.194), kind=kOutput, calls=%fused_computation.9 | convolution fusion | flops 1074003968 | bytes 5767168 | tf_op jit(solution)/shard_map/dot_general | solution.py:167
  20.6 7.2 %all-to-all-done = bf16[32,4,16,128]{3,2,1,0:T(8,128)(2,1)S(1)} async-done(((bf16[32,4,16,128]{3,2,1,0:T(8,128)(2,1)}), bf16[32,4,16,128]{3,2,1,0:T(8,128)(2,1)S(1)}, u32[]{:S(2)}, u32[]{:S(2)}) %all-to-all-start) | async-done | bytes 524320 | tf_op jit(solution)/shard_map/all_to_all | solution.py:169
  27.8 3.1 %all-to-all-start.1 = ((bf16[32,4,16,128]{3,2,1,0:T(8,128)(2,1)}), bf16[32,4,16,128]{3,2,1,0:T(8,128)(2,1)S(1)}, u32[]{:S(2)}, u32[]{:S(2)}) async-start(bf16[32,4,16,128]{3,2,1,0:T(8,128)(2,1)} %reshape.313), calls=%async_computation.1 | async-start | bytes 1048576 | tf_op jit(solution)/shard_map/all_to_all | solution.py:169
  30.9 1.0 reshape.315
  32.1 3.5 %convolution_convert_fusion = bf16[256,1024]{1,0:T(8,128)(2,1)S(1)} fusion(bf16[256,2048]{1,0:T(8,128)(2,1)S(1)} %copy-done.10, bf16[1024,2048]{1,0:T(8,128)(2,1)} %bitcast.195), kind=kOutput, calls=%fused_computation.8 | convolution fusion | flops 1074003968 | bytes 5767168 | tf_op jit(solution)/shard_map/dot_general | solution.py:167
  35.6 10.8 %all-to-all-done.1 = bf16[32,4,16,128]{3,2,1,0:T(8,128)(2,1)S(1)} async-done(((bf16[32,4,16,128]{3,2,1,0:T(8,128)(2,1)}), bf16[32,4,16,128]{3,2,1,0:T(8,128)(2,1)S(1)}, u32[]{:S(2)}, u32[]{:S(2)}) %all-to-all-start.1) | async-done | bytes 524320 | tf_op jit(solution)/shard_map/all_to_all | solution.py:169
  46.4 3.1 %all-to-all-start.2 = ((bf16[32,4,16,128]{3,2,1,0:T(8,128)(2,1)}), bf16[32,4,16,128]{3,2,1,0:T(8,128)(2,1)S(1)}, u32[]{:S(2)}, u32[]{:S(2)}) async-start(bf16[32,4,16,128]{3,2,1,0:T(8,128)(2,1)} %reshape.315), calls=%async_computation.2 | async-start | bytes 1048576 | tf_op jit(solution)/shard_map/all_to_all | solution.py:169
  49.7 1.0 reshape.317
  50.8 1.4 fusion.2
  52.2 1.2 broadcast_select_fusion
  53.3 2.6 %compare_select_fusion = (bf16[8,1024,128]{2,1,0:T(8,128)(2,1)}, bf16[8,1024,128]{2,1,0:T(8,128)(2,1)}) fusion(s32[8,128]{1,0:T(8,128)S(1)} %multiply_add_fusion, s32[1024]{0:T(1024)S(1)} %bitcast.151, bf16[8,128]{1,0:T(8,128)(2,1)S(1)} %convert_bitcast_fusion, s32[1024]{0:T(1024)S(1)} %copy-done.8), kind=kLoop, calls=%fused_computation.4 | loop fusion | flops 4194304 | bytes 4208640 | tf_op jit(solution)/shard_map/jit(_where)/select_n | solution.py:179
  55.9 9.1 %all-to-all-done.2 = bf16[32,4,16,128]{3,2,1,0:T(8,128)(2,1)S(1)} async-done(((bf16[32,4,16,128]{3,2,1,0:T(8,128)(2,1)}), bf16[32,4,16,128]{3,2,1,0:T(8,128)(2,1)S(1)}, u32[]{:S(2)}, u32[]{:S(2)}) %all-to-all-start.2) | async-done | bytes 524320 | tf_op jit(solution)/shard_map/all_to_all | solution.py:169
  65.0 3.3 %all-to-all-start.3 = ((bf16[32,4,16,128]{3,2,1,0:T(8,128)(2,1)}), bf16[32,4,16,128]{3,2,1,0:T(8,128)(2,1)S(1)}, u32[]{:S(2)}, u32[]{:S(2)}) async-start(bf16[32,4,16,128]{3,2,1,0:T(8,128)(2,1)} %reshape.317), calls=%async_computation.3 | async-start | bytes 1048576 | tf_op jit(solution)/shard_map/all_to_all | solution.py:169
  68.3 13.9 %shard_map.74 = f32[4,2,16,256]{3,2,1,0:T(8,128)} custom-call(bf16[8,4,4,16,128]{4,3,2,1,0:T(8,128)(2,1)} %bitcast.144, bf16[8,1024,128]{2,1,0:T(8,128)(2,1)} %get-tuple-element.50.refs_1_, bf16[8,1024,128]{2,1,0:T(8,128)(2,1)} %get-tuple-element.49.refs_2_, bf16[64,64]{1,0:T(8,128)(2,1)} %constant.43.clone.refs_3_), custom_call_target="tpu_custom_call" | custom-call | flops 1778384896 | bytes 4849664 | tf_op jit(solution)/shard_map/pallas_call | solution.py:128
  82.2 13.9 %shard_map.75 = f32[4,2,16,256]{3,2,1,0:T(8,128)} custom-call(bf16[8,4,4,16,128]{4,3,2,1,0:T(8,128)(2,1)} %bitcast.145, bf16[8,1024,128]{2,1,0:T(8,128)(2,1)} %get-tuple-element.50.refs_1_, bf16[8,1024,128]{2,1,0:T(8,128)(2,1)} %get-tuple-element.49.refs_2_, bf16[64,64]{1,0:T(8,128)(2,1)} %constant.43.clone.refs_3_), custom_call_target="tpu_custom_call" | custom-call | flops 1778384896 | bytes 4849664 | tf_op jit(solution)/shard_map/pallas_call | solution.py:128
  96.1 15.1 %shard_map.73 = (f32[4,2,16,256]{3,2,1,0:T(8,128)}, f32[16,256]{1,0:T(8,128)}) custom-call(bf16[8,4,4,16,128]{4,3,2,1,0:T(8,128)(2,1)} %bitcast.143, bf16[8,1024,128]{2,1,0:T(8,128)(2,1)} %get-tuple-element.50.refs_1_, bf16[8,1024,128]{2,1,0:T(8,128)(2,1)} %get-tuple-element.49.refs_2_, bf16[64,64]{1,0:T(8,128)(2,1)} %constant.43.clone.refs_3_, ...), custom_call_target="tpu_custom_call" | custom-call | flops 1778384896 | bytes 4849664 | tf_op jit(solution)/shard_map/pallas_call | solution.py:128
  111.2 0.9 fusion.8
  112.1 1.0 fusion.6
  113.1 0.8 copy-done.3
  113.9 13.9 %shard_map.76 = f32[4,2,16,256]{3,2,1,0:T(8,128)} custom-call(bf16[8,4,4,16,128]{4,3,2,1,0:T(8,128)(2,1)} %bitcast.146, bf16[8,1024,128]{2,1,0:T(8,128)(2,1)} %get-tuple-element.50.refs_1_, bf16[8,1024,128]{2,1,0:T(8,128)(2,1)} %get-tuple-element.49.refs_2_, bf16[64,64]{1,0:T(8,128)(2,1)} %constant.43.clone.refs_3_), custom_call_target="tpu_custom_call" | custom-call | flops 1778384896 | bytes 4849664 | tf_op jit(solution)/shard_map/pallas_call | solution.py:128
  127.8 0.9 pad_maximum_fusion
  135.5 1.2 copy.126
  136.7 5.6 %all-to-all-start.4 = ((f32[32,16,2,128]{3,2,1,0:T(2,128)}), f32[32,16,2,128]{3,2,1,0:T(2,128)S(1)}, u32[]{:S(2)}, u32[]{:S(2)}) async-start(f32[32,16,2,128]{3,2,1,0:T(2,128)} %copy.126), calls=%async_computation.4 | async-start | bytes 1048576 | tf_op jit(solution)/shard_map/all_to_all | solution.py:204
  142.3 1.5 fusion.7
  149.3 8.6 %all-to-all-done.4 = f32[32,16,2,128]{3,2,1,0:T(2,128)S(1)} async-done(((f32[32,16,2,128]{3,2,1,0:T(2,128)}), f32[32,16,2,128]{3,2,1,0:T(2,128)S(1)}, u32[]{:S(2)}, u32[]{:S(2)}) %all-to-all-start.4) | async-done | bytes 524320 | tf_op jit(solution)/shard_map/all_to_all | solution.py:204
  157.9 6.8 %convolution_multiply_fusion = f32[128,2,512]{2,0,1:T(8,128)S(1)} fusion(f32[1024,128,1]{1,0,2:T(8,128)S(1)} %bitcast.142, f32[2,512,1024]{2,1,0:T(8,128)} %constant.55, f32[128]{0:T(128)S(1)} %multiply_rsqrt_fusion), kind=kOutput, calls=%fused_computation.12 | convolution fusion | flops 1610743808 | bytes 5243392 | tf_op jit(solution)/shard_map/dot_general | solution.py:212
  164.7 1.2 copy.128
  (122 shorter events, 12.3 us)
Async XLA Ops:
  0.0 12.2 %copy-start.11 = (bf16[256,2048]{1,0:T(8,128)(2,1)S(1)}, bf16[256,2048]{1,0:T(8,128)(2,1)}, u32[]{:S(2)}) copy-start(bf16[256,2048]{1,0:T(8,128)(2,1)} %constant.49) | copy-start | bytes 3145732
  4.9 22.9 %all-to-all-start = ((bf16[32,4,16,128]{3,2,1,0:T(8,128)(2,1)}), bf16[32,4,16,128]{3,2,1,0:T(8,128)(2,1)S(1)}, u32[]{:S(2)}, u32[]{:S(2)}) async-start(bf16[32,4,16,128]{3,2,1,0:T(8,128)(2,1)} %reshape.310), calls=%async_computation | async-start | bytes 1048576 | tf_op jit(solution)/shard_map/all_to_all | solution.py:169
  16.7 15.3 %copy-start.9 = (s32[1024]{0:T(1024)S(1)}, s32[1024]{0:T(1024)}, u32[]{:S(2)}) copy-start(s32[1024]{0:T(1024)} %param.9) | copy-start | bytes 12292
  16.7 15.4 %copy-start.10 = (bf16[256,2048]{1,0:T(8,128)(2,1)S(1)}, bf16[256,2048]{1,0:T(8,128)(2,1)}, u32[]{:S(2)}) copy-start(bf16[256,2048]{1,0:T(8,128)(2,1)} %constant.53) | copy-start | bytes 3145732
  27.8 7.8 %copy-start = (bf16[32,4,16,128]{3,2,1,0:T(8,128)(2,1)}, bf16[32,4,16,128]{3,2,1,0:T(8,128)(2,1)S(1)}, u32[]{:S(2)}) copy-start(bf16[32,4,16,128]{3,2,1,0:T(8,128)(2,1)S(1)} %all-to-all-done) | copy-start | bytes 1572868
  27.8 18.6 %all-to-all-start.1 = ((bf16[32,4,16,128]{3,2,1,0:T(8,128)(2,1)}), bf16[32,4,16,128]{3,2,1,0:T(8,128)(2,1)S(1)}, u32[]{:S(2)}, u32[]{:S(2)}) async-start(bf16[32,4,16,128]{3,2,1,0:T(8,128)(2,1)} %reshape.313), calls=%async_computation.1 | async-start | bytes 1048576 | tf_op jit(solution)/shard_map/all_to_all | solution.py:169
  32.1 17.4 %copy-start.8 = (s32[1024]{0:T(1024)S(1)}, s32[1024]{0:T(1024)}, u32[]{:S(2)}) copy-start(s32[1024]{0:T(1024)} %param.8) | copy-start | bytes 12292
  46.4 21.9 %copy-start.1 = (bf16[32,4,16,128]{3,2,1,0:T(8,128)(2,1)}, bf16[32,4,16,128]{3,2,1,0:T(8,128)(2,1)S(1)}, u32[]{:S(2)}) copy-start(bf16[32,4,16,128]{3,2,1,0:T(8,128)(2,1)S(1)} %all-to-all-done.1) | copy-start | bytes 1572868
  46.4 18.6 %all-to-all-start.2 = ((bf16[32,4,16,128]{3,2,1,0:T(8,128)(2,1)}), bf16[32,4,16,128]{3,2,1,0:T(8,128)(2,1)S(1)}, u32[]{:S(2)}, u32[]{:S(2)}) async-start(bf16[32,4,16,128]{3,2,1,0:T(8,128)(2,1)} %reshape.315), calls=%async_computation.2 | async-start | bytes 1048576 | tf_op jit(solution)/shard_map/all_to_all | solution.py:169
  65.0 17.2 %copy-start.2 = (bf16[32,4,16,128]{3,2,1,0:T(8,128)(2,1)}, bf16[32,4,16,128]{3,2,1,0:T(8,128)(2,1)S(1)}, u32[]{:S(2)}) copy-start(bf16[32,4,16,128]{3,2,1,0:T(8,128)(2,1)S(1)} %all-to-all-done.2) | copy-start | bytes 1572868
  65.0 48.0 %all-to-all-start.3 = ((bf16[32,4,16,128]{3,2,1,0:T(8,128)(2,1)}), bf16[32,4,16,128]{3,2,1,0:T(8,128)(2,1)S(1)}, u32[]{:S(2)}, u32[]{:S(2)}) async-start(bf16[32,4,16,128]{3,2,1,0:T(8,128)(2,1)} %reshape.317), calls=%async_computation.3 | async-start | bytes 1048576 | tf_op jit(solution)/shard_map/all_to_all | solution.py:169
  111.2 16.6 %copy-start.4 = (f32[4,2,16,256]{3,2,1,0:T(8,128)S(1)}, f32[4,2,16,256]{3,2,1,0:T(8,128)}, u32[]{:S(2)}) copy-start(f32[4,2,16,256]{3,2,1,0:T(8,128)} %shard_map.74) | copy-start | bytes 393220
  111.2 16.6 %copy-start.5 = (f32[4,2,16,256]{3,2,1,0:T(8,128)S(1)}, f32[4,2,16,256]{3,2,1,0:T(8,128)}, u32[]{:S(2)}) copy-start(f32[4,2,16,256]{3,2,1,0:T(8,128)} %shard_map.75) | copy-start | bytes 393220
  111.2 16.6 %copy-start.6 = (f32[4,2,16,256]{3,2,1,0:T(8,128)S(1)}, f32[4,2,16,256]{3,2,1,0:T(8,128)}, u32[]{:S(2)}) copy-start(f32[4,2,16,256]{3,2,1,0:T(8,128)} %get-tuple-element.7) | copy-start | bytes 393220
  113.1 0.8 copy-start.3
  113.9 20.4 %copy-start.7 = (f32[2]{0:T(128)S(1)}, f32[2]{0:T(128)}, u32[]{:S(2)}) copy-start(f32[2]{0:T(128)} %constant.44.clone) | copy-start | bytes 28
  136.7 21.2 %all-to-all-start.4 = ((f32[32,16,2,128]{3,2,1,0:T(2,128)}), f32[32,16,2,128]{3,2,1,0:T(2,128)S(1)}, u32[]{:S(2)}, u32[]{:S(2)}) async-start(f32[32,16,2,128]{3,2,1,0:T(2,128)} %copy.126), calls=%async_computation.4 | async-start | bytes 1048576 | tf_op jit(solution)/shard_map/all_to_all | solution.py:204

commit v4 on v3

--- a/solution.py
+++ b/solution.py
@@ -162,14 +162,13 @@
     table = table.reshape(devices, chunks, chunk_channels * 2, length).transpose(1, 0, 2, 3)
     table = jnp.asarray(table.reshape(chunks, devices * chunk_channels * 2, length), dtype=jnp.bfloat16)
     flattened = samples.reshape(frames_here * inputs_here, length)
-    chunk_blocks = []
-    for j in range(chunks):
-        spectra = lax.dot_general(table[j], flattened, NT, preferred_element_type=jnp.float32)
-        spectra = spectra.astype(jnp.bfloat16).reshape(devices, chunk_channels, 2 * frames_here, inputs_here)
-        turned = lax.all_to_all(spectra, ("wide", "tm"), 0, 0, tiled=True)
-        chunk_blocks.append(
-            turned.reshape(wide_parts, tm_parts, chunk_channels, 2 * frames_here, inputs_here)
-        )
+    spectra = lax.dot_general(
+        table.reshape(chunks * devices * chunk_channels * 2, length), flattened, NT,
+        preferred_element_type=jnp.float32,
+    )
+    spectra = spectra.astype(jnp.bfloat16).reshape(
+        chunks, devices, chunk_channels, 2 * frames_here, inputs_here
+    )
 
     inputs_all = wide_parts * inputs_here
     flags = input_flags.astype(jnp.bfloat16)
@@ -194,8 +193,18 @@
         rm[partner, r] = -1.0 if part_at[r] == 0 else 1.0
     rm = jnp.asarray(rm, dtype=jnp.bfloat16)
 
-    sums, count_sums = correlate(chunk_blocks[0], pt, ptr, rm, fm, fmr)
-    sums = [sums] + [correlate(blk, pt, ptr, rm)[0] for blk in chunk_blocks[1:]]
+    sums = []
+    for j in range(chunks):
+        spectra_j = spectra[j]
+        if j >= 2:
+            spectra_j, _ = lax.optimization_barrier((spectra_j, sums[j - 2]))
+        turned = lax.all_to_all(spectra_j, ("wide", "tm"), 0, 0, tiled=True)
+        blk = turned.reshape(wide_parts, tm_parts, chunk_channels, 2 * frames_here, inputs_here)
+        if j == 0:
+            first, count_sums = correlate(blk, pt, ptr, rm, fm, fmr)
+            sums.append(first)
+        else:
+            sums.append(correlate(blk, pt, ptr, rm)[0])
     sums = jnp.concatenate(sums, axis=0)
     conj_sign = jnp.array([1.0, -1.0], jnp.float32)[None, :, None]
     vis = unskew(sums, conj_sign)

time: 167 us -> 153 us (0.916)
  waiting for transfers between devices: 35.7 us -> 23.2 us
  matrix products: 21.4 us -> 14.7 us
  starting transfers between devices: 22.3 us -> 27.9 us
    all_to_all x4, waiting for transfers between devices: 27.1 us -> 14.5 us  [body(): turned = lax.all_to_all(spectra_j, ('wide', 'tm'), 0, 0, tiled=True)]
    dot_general x4 -> x1, matrix products: 14.7 us -> 7.99 us  [body(): lax.dot_general(table.reshape(chunks * devices * chunk_channels * 2, leng...]
    all_to_all x4, starting transfers between devices: 16.7 us -> 22.1 us  [body(): turned = lax.all_to_all(spectra_j, ('wide', 'tm'), 0, 0, tiled=True)]
    squeeze x0 -> x4, local copies, waits for them, and re-layouts: none -> 4.13 us  [body(): spectra_j = spectra[j]]
    reshape x4 -> x0, local copies, waits for them, and re-layouts: 4.1 us -> none  [body(): spectra.astype(jnp.bfloat16)]
  transfers between devices with their start and end apart: 5 -> 5, of which waited for: 4 -> 2; matrix products, arithmetic and copies ran while one was open for 17% -> 11% of each run, Pallas kernels for 26% -> 28%
where the time goes in v4:
time: 153 us; the launch traced here: 152 us
  Pallas kernels  56.8 us (37%)
  starting transfers between devices  27.9 us (18%)
  waiting for transfers between devices  23.2 us (15%)
  local copies, waits for them, and re-layouts  17.8 us (12%)
  matrix products  14.7 us (10%)
  other arithmetic  11.1 us (7%)
    pallas_call x4, Pallas kernels, correlate(): pl.pallas_call(functools.partial(correlate_kernel, with_counts=with_count...  56.8 us
    all_to_all x4, starting transfers between devices, body(): turned = lax.all_to_all(spectra_j, ('wide', 'tm'), 0, 0, tiled=True)  22.1 us
    all_to_all x4, waiting for transfers between devices, body(): turned = lax.all_to_all(spectra_j, ('wide', 'tm'), 0, 0, tiled=True)  14.5 us
    all_to_all x1, waiting for transfers between devices, body(): received = lax.all_to_all(send, ('wide', 'tm'), 0, 0, tiled=True)  8.71 us
    dot_general x1, matrix products, body(): lax.dot_general(table.reshape(chunks * devices * chunk_channels * 2, leng...  7.99 us
    dot_general x1, matrix products, body(): lax.dot_general(stacked_in, delay, (((0,), (0,)), ((), ())), precision=la...  6.66 us
    all_to_all x1, starting transfers between devices, body(): received = lax.all_to_all(send, ('wide', 'tm'), 0, 0, tiled=True)  5.83 us
    squeeze x4, local copies, waits for them, and re-layouts, body(): spectra_j = spectra[j]  4.13 us
  transfers between devices with their start and end apart: 5, of which 2 were waited for; matrix products, arithmetic and copies ran while one was open for 11% of the time, Pallas kernels for 28%

profile of v4, /device:TPU:0, one launch (start us, length us, event | category | flops | bytes accessed | tf_op | source)
XLA Modules:
  0.0 152.0 jit_solution(13457503529683238108)
XLA Ops:
  0.0 8.0 %convolution_convert_fusion = bf16[1024,1024]{1,0:T(8,128)(2,1)S(1)} fusion(bf16[1024,2048]{1,0:T(8,128)(2,1)} %constant.46, bf16[1024,2048]{1,0:T(8,128)(2,1)} %bitcast.186), kind=kOutput, calls=%fused_computation.8 | convolution fusion | flops 4296015872 | bytes 10485760 | tf_op jit(solution)/shard_map/dot_general | solution.py:165
  8.2 1.0 squeeze.97
  9.2 7.3 %all-to-all-start.1 = ((bf16[32,4,16,128]{3,2,1,0:T(8,128)(2,1)}), bf16[32,4,16,128]{3,2,1,0:T(8,128)(2,1)S(1)}, u32[]{:S(2)}, u32[]{:S(2)}) async-start(bf16[32,4,16,128]{3,2,1,0:T(8,128)(2,1)} %squeeze.97), calls=%async_computation.1 | async-start | bytes 1048576 | tf_op jit(solution)/shard_map/all_to_all | solution.py:201
  16.5 1.0 squeeze.96
  17.6 14.5 %all-to-all-done.1 = bf16[32,4,16,128]{3,2,1,0:T(8,128)(2,1)S(1)} async-done(((bf16[32,4,16,128]{3,2,1,0:T(8,128)(2,1)}), bf16[32,4,16,128]{3,2,1,0:T(8,128)(2,1)S(1)}, u32[]{:S(2)}, u32[]{:S(2)}) %all-to-all-start.1) | async-done | bytes 524320 | tf_op jit(solution)/shard_map/all_to_all | solution.py:201
  32.1 3.1 %all-to-all-start = ((bf16[32,4,16,128]{3,2,1,0:T(8,128)(2,1)}), bf16[32,4,16,128]{3,2,1,0:T(8,128)(2,1)S(1)}, u32[]{:S(2)}, u32[]{:S(2)}) async-start(bf16[32,4,16,128]{3,2,1,0:T(8,128)(2,1)} %squeeze.96), calls=%async_computation | async-start | bytes 1048576 | tf_op jit(solution)/shard_map/all_to_all | solution.py:201
  35.2 1.0 squeeze.99
  36.4 2.6 %compare_select_fusion = (bf16[8,1024,128]{2,1,0:T(8,128)(2,1)}, bf16[8,1024,128]{2,1,0:T(8,128)(2,1)}) fusion(s32[8,128]{1,0:T(8,128)S(1)} %multiply_add_fusion, s32[1024]{0:T(1024)S(1)} %bitcast.144, bf16[8,128]{1,0:T(8,128)(2,1)S(1)} %convert_bitcast_fusion, s32[1024]{0:T(1024)S(1)} %copy-done.8), kind=kLoop, calls=%fused_computation.4 | loop fusion | flops 4194304 | bytes 4208640 | tf_op jit(solution)/shard_map/jit(_where)/select_n | solution.py:178
  39.0 13.9 %shard_map.74 = f32[4,2,16,256]{3,2,1,0:T(8,128)} custom-call(bf16[8,4,4,16,128]{4,3,2,1,0:T(8,128)(2,1)} %bitcast.140, bf16[8,1024,128]{2,1,0:T(8,128)(2,1)} %get-tuple-element.58.refs_1_, bf16[8,1024,128]{2,1,0:T(8,128)(2,1)} %get-tuple-element.57.refs_2_, bf16[64,64]{1,0:T(8,128)(2,1)} %constant.43.clone.refs_3_), custom_call_target="tpu_custom_call" | custom-call | flops 1778384896 | bytes 4849664 | tf_op jit(solution)/shard_map/pallas_call | solution.py:128
  52.9 6.0 %all-to-all-start.3 = ((bf16[32,4,16,128]{3,2,1,0:T(8,128)(2,1)}), bf16[32,4,16,128]{3,2,1,0:T(8,128)(2,1)S(1)}, u32[]{:S(2)}, u32[]{:S(2)}) async-start(bf16[32,4,16,128]{3,2,1,0:T(8,128)(2,1)} %squeeze.99), calls=%async_computation.3 | async-start | bytes 1048576 | tf_op jit(solution)/shard_map/all_to_all | solution.py:201
  59.0 1.0 squeeze.98
  60.2 1.4 fusion.2
  61.6 1.1 broadcast_select_fusion
  62.7 15.1 %shard_map.73 = (f32[4,2,16,256]{3,2,1,0:T(8,128)}, f32[16,256]{1,0:T(8,128)}) custom-call(bf16[8,4,4,16,128]{4,3,2,1,0:T(8,128)(2,1)} %bitcast.138, bf16[8,1024,128]{2,1,0:T(8,128)(2,1)} %get-tuple-element.58.refs_1_, bf16[8,1024,128]{2,1,0:T(8,128)(2,1)} %get-tuple-element.57.refs_2_, bf16[64,64]{1,0:T(8,128)(2,1)} %constant.43.clone.refs_3_, ...), custom_call_target="tpu_custom_call" | custom-call | flops 1778384896 | bytes 4849664 | tf_op jit(solution)/shard_map/pallas_call | solution.py:128
  77.8 5.7 %all-to-all-start.2 = ((bf16[32,4,16,128]{3,2,1,0:T(8,128)(2,1)}), bf16[32,4,16,128]{3,2,1,0:T(8,128)(2,1)S(1)}, u32[]{:S(2)}, u32[]{:S(2)}) async-start(bf16[32,4,16,128]{3,2,1,0:T(8,128)(2,1)} %squeeze.98), calls=%async_computation.2 | async-start | bytes 1048576 | tf_op jit(solution)/shard_map/all_to_all | solution.py:201
  83.6 0.9 fusion.9
  84.5 1.0 fusion.7
  85.4 13.9 %shard_map.76 = f32[4,2,16,256]{3,2,1,0:T(8,128)} custom-call(bf16[8,4,4,16,128]{4,3,2,1,0:T(8,128)(2,1)} %bitcast.137, bf16[8,1024,128]{2,1,0:T(8,128)(2,1)} %get-tuple-element.58.refs_1_, bf16[8,1024,128]{2,1,0:T(8,128)(2,1)} %get-tuple-element.57.refs_2_, bf16[64,64]{1,0:T(8,128)(2,1)} %constant.43.clone.refs_3_), custom_call_target="tpu_custom_call" | custom-call | flops 1778384896 | bytes 4849664 | tf_op jit(solution)/shard_map/pallas_call | solution.py:128
  99.4 0.8 copy-done.2
  100.2 13.9 %shard_map.75 = f32[4,2,16,256]{3,2,1,0:T(8,128)} custom-call(bf16[8,4,4,16,128]{4,3,2,1,0:T(8,128)(2,1)} %bitcast.139, bf16[8,1024,128]{2,1,0:T(8,128)(2,1)} %get-tuple-element.58.refs_1_, bf16[8,1024,128]{2,1,0:T(8,128)(2,1)} %get-tuple-element.57.refs_2_, bf16[64,64]{1,0:T(8,128)(2,1)} %constant.43.clone.refs_3_), custom_call_target="tpu_custom_call" | custom-call | flops 1778384896 | bytes 4849664 | tf_op jit(solution)/shard_map/pallas_call | solution.py:128
  114.1 0.9 pad_maximum_fusion
  121.5 1.2 copy.126
  122.7 5.8 %all-to-all-start.4 = ((f32[32,16,2,128]{3,2,1,0:T(2,128)}), f32[32,16,2,128]{3,2,1,0:T(2,128)S(1)}, u32[]{:S(2)}, u32[]{:S(2)}) async-start(f32[32,16,2,128]{3,2,1,0:T(2,128)} %copy.126), calls=%async_computation.4 | async-start | bytes 1048576 | tf_op jit(solution)/shard_map/all_to_all | solution.py:213
  128.6 1.5 %fusion.8 = (f32[1,1]{1,0:T(1,128)}, f32[1,1]{1,0:T(1,128)}, f32[1,1]{1,0:T(1,128)}, f32[1,1]{1,0:T(1,128)}, f32[1,1]{1,0:T(1,128)}, /*index=5*/f32[1,1]{1,0:T(1,128)}) fusion(f32[16,256]{1,0:T(8,128)} %get-tuple-element.12), kind=kLoop, calls=%fused_computation.76 | loop fusion | bytes 48 | tf_op jit(solution)/shard_map/slice | solution.py:146
  131.7 0.7 pad_maximum_fusion.2
  132.4 0.7 pad_maximum_fusion.3
  133.1 0.6 pad_maximum_fusion.4
  133.7 0.8 pad_maximum_fusion.5
  134.5 0.7 pad_maximum_fusion.6
  135.4 8.7 %all-to-all-done.4 = f32[32,16,2,128]{3,2,1,0:T(2,128)S(1)} async-done(((f32[32,16,2,128]{3,2,1,0:T(2,128)}), f32[32,16,2,128]{3,2,1,0:T(2,128)S(1)}, u32[]{:S(2)}, u32[]{:S(2)}) %all-to-all-start.4) | async-done | bytes 524320 | tf_op jit(solution)/shard_map/all_to_all | solution.py:213
  144.1 6.7 %convolution_multiply_fusion = f32[128,2,512]{2,0,1:T(8,128)S(1)} fusion(f32[1024,128,1]{1,0,2:T(8,128)S(1)} %bitcast.136, f32[2,512,1024]{2,1,0:T(8,128)} %constant.48, f32[128]{0:T(128)S(1)} %multiply_rsqrt_fusion), kind=kOutput, calls=%fused_computation.9 | convolution fusion | flops 1610743808 | bytes 5243392 | tf_op jit(solution)/shard_map/dot_general | solution.py:221
  150.8 1.2 copy.128
  (116 shorter events, 8.7 us)
Async XLA Ops:
  8.0 28.2 %copy-start.8 = (s32[1024]{0:T(1024)S(1)}, s32[1024]{0:T(1024)}, u32[]{:S(2)}) copy-start(s32[1024]{0:T(1024)} %param.8) | copy-start | bytes 12292
  8.0 28.4 %copy-start.9 = (s32[1024]{0:T(1024)S(1)}, s32[1024]{0:T(1024)}, u32[]{:S(2)}) copy-start(s32[1024]{0:T(1024)} %param.9) | copy-start | bytes 12292
  9.2 22.9 %all-to-all-start.1 = ((bf16[32,4,16,128]{3,2,1,0:T(8,128)(2,1)}), bf16[32,4,16,128]{3,2,1,0:T(8,128)(2,1)S(1)}, u32[]{:S(2)}, u32[]{:S(2)}) async-start(bf16[32,4,16,128]{3,2,1,0:T(8,128)(2,1)} %squeeze.97), calls=%async_computation.1 | async-start | bytes 1048576 | tf_op jit(solution)/shard_map/all_to_all | solution.py:201
  32.1 6.9 %copy-start.3 = (bf16[32,4,16,128]{3,2,1,0:T(8,128)(2,1)}, bf16[32,4,16,128]{3,2,1,0:T(8,128)(2,1)S(1)}, u32[]{:S(2)}) copy-start(bf16[32,4,16,128]{3,2,1,0:T(8,128)(2,1)S(1)} %all-to-all-done.1) | copy-start | bytes 1572868
  32.1 20.8 %all-to-all-start = ((bf16[32,4,16,128]{3,2,1,0:T(8,128)(2,1)}), bf16[32,4,16,128]{3,2,1,0:T(8,128)(2,1)S(1)}, u32[]{:S(2)}, u32[]{:S(2)}) async-start(bf16[32,4,16,128]{3,2,1,0:T(8,128)(2,1)} %squeeze.96), calls=%async_computation | async-start | bytes 1048576 | tf_op jit(solution)/shard_map/all_to_all | solution.py:201
  52.9 9.8 %copy-start.1 = (bf16[32,4,16,128]{3,2,1,0:T(8,128)(2,1)}, bf16[32,4,16,128]{3,2,1,0:T(8,128)(2,1)S(1)}, u32[]{:S(2)}) copy-start(bf16[32,4,16,128]{3,2,1,0:T(8,128)(2,1)S(1)} %all-to-all-done) | copy-start | bytes 1572868
  52.9 24.9 %all-to-all-start.3 = ((bf16[32,4,16,128]{3,2,1,0:T(8,128)(2,1)}), bf16[32,4,16,128]{3,2,1,0:T(8,128)(2,1)S(1)}, u32[]{:S(2)}, u32[]{:S(2)}) async-start(bf16[32,4,16,128]{3,2,1,0:T(8,128)(2,1)} %squeeze.99), calls=%async_computation.3 | async-start | bytes 1048576 | tf_op jit(solution)/shard_map/all_to_all | solution.py:201
  77.8 7.6 %copy-start = (bf16[32,4,16,128]{3,2,1,0:T(8,128)(2,1)}, bf16[32,4,16,128]{3,2,1,0:T(8,128)(2,1)S(1)}, u32[]{:S(2)}) copy-start(bf16[32,4,16,128]{3,2,1,0:T(8,128)(2,1)S(1)} %all-to-all-done.3) | copy-start | bytes 1572868
  77.8 21.5 %all-to-all-start.2 = ((bf16[32,4,16,128]{3,2,1,0:T(8,128)(2,1)}), bf16[32,4,16,128]{3,2,1,0:T(8,128)(2,1)S(1)}, u32[]{:S(2)}, u32[]{:S(2)}) async-start(bf16[32,4,16,128]{3,2,1,0:T(8,128)(2,1)} %squeeze.98), calls=%async_computation.2 | async-start | bytes 1048576 | tf_op jit(solution)/shard_map/all_to_all | solution.py:201
  99.3 14.7 %copy-start.4 = (f32[4,2,16,256]{3,2,1,0:T(8,128)S(1)}, f32[4,2,16,256]{3,2,1,0:T(8,128)}, u32[]{:S(2)}) copy-start(f32[4,2,16,256]{3,2,1,0:T(8,128)} %shard_map.74) | copy-start | bytes 393220
  99.3 14.7 %copy-start.5 = (f32[4,2,16,256]{3,2,1,0:T(8,128)S(1)}, f32[4,2,16,256]{3,2,1,0:T(8,128)}, u32[]{:S(2)}) copy-start(f32[4,2,16,256]{3,2,1,0:T(8,128)} %get-tuple-element.9) | copy-start | bytes 393220
  99.3 14.7 %copy-start.6 = (f32[4,2,16,256]{3,2,1,0:T(8,128)S(1)}, f32[4,2,16,256]{3,2,1,0:T(8,128)}, u32[]{:S(2)}) copy-start(f32[4,2,16,256]{3,2,1,0:T(8,128)} %shard_map.76) | copy-start | bytes 393220
  99.4 0.8 copy-start.2
  100.2 20.2 %copy-start.7 = (f32[2]{0:T(128)S(1)}, f32[2]{0:T(128)}, u32[]{:S(2)}) copy-start(f32[2]{0:T(128)} %constant.44.clone) | copy-start | bytes 28
  122.7 21.4 %all-to-all-start.4 = ((f32[32,16,2,128]{3,2,1,0:T(2,128)}), f32[32,16,2,128]{3,2,1,0:T(2,128)S(1)}, u32[]{:S(2)}, u32[]{:S(2)}) async-start(f32[32,16,2,128]{3,2,1,0:T(2,128)} %copy.126), calls=%async_computation.4 | async-start | bytes 1048576 | tf_op jit(solution)/shard_map/all_to_all | solution.py:213

commit v5 on v4

--- a/solution.py
+++ b/solution.py
@@ -162,13 +162,17 @@
     table = table.reshape(devices, chunks, chunk_channels * 2, length).transpose(1, 0, 2, 3)
     table = jnp.asarray(table.reshape(chunks, devices * chunk_channels * 2, length), dtype=jnp.bfloat16)
     flattened = samples.reshape(frames_here * inputs_here, length)
-    spectra = lax.dot_general(
-        table.reshape(chunks * devices * chunk_channels * 2, length), flattened, NT,
-        preferred_element_type=jnp.float32,
-    )
-    spectra = spectra.astype(jnp.bfloat16).reshape(
-        chunks, devices, chunk_channels, 2 * frames_here, inputs_here
-    )
+    chunk_rows = devices * chunk_channels * 2
+    table = table.reshape(chunks * chunk_rows, length)
+
+    def channelize(rows):
+        spectra = lax.dot_general(rows, flattened, NT, preferred_element_type=jnp.float32)
+        return spectra.astype(jnp.bfloat16).reshape(-1, devices, chunk_channels, 2 * frames_here, inputs_here)
+
+    spectra = [channelize(table[:chunk_rows])[0]]
+    if chunks > 1:
+        rest = channelize(table[chunk_rows:])
+        spectra += [rest[j] for j in range(chunks - 1)]
 
     inputs_all = wide_parts * inputs_here
     flags = input_flags.astype(jnp.bfloat16)
@@ -219,7 +223,7 @@
     )
     delay = delay_matrix_const(CH)
     spectra_out = lax.dot_general(
-        stacked_in, delay, (((0,), (0,)), ((), ())), precision=lax.Precision.HIGHEST,
+        stacked_in, delay, (((0,), (0,)), ((), ())), precision=lax.Precision.HIGH,
         preferred_element_type=jnp.float32,
     )
     weight = 1.0 / jnp.sqrt(frames_all * CH * jnp.maximum(local_stack_counts, 1.0))

time: 153 us -> 149 us (0.974)
  waiting for transfers between devices: 23.2 us -> 19.6 us
    all_to_all x4, waiting for transfers between devices: 14.5 us -> 11 us  [body(): turned = lax.all_to_all(spectra_j, ('wide', 'tm'), 0, 0, tiled=True)]
    dot_general x1, matrix products: 6.66 us -> 4.54 us  [body(): lax.dot_general(stacked_in, delay, (((0,), (0,)), ((), ())), precision=la...]
    dot_general x1 -> x2, matrix products: 7.99 us -> 10.1 us  [channelize(): lax.dot_general(rows, flattened, NT, preferred_element_type=jnp.float32)]
    squeeze x4 -> x3, local copies, waits for them, and re-layouts: 4.13 us -> 3.08 us  [body(): spectra += [rest[j] for j in range(chunks - 1)]]
  transfers between devices with their start and end apart: 5 -> 5, of which waited for: 2 -> 2; matrix products, arithmetic and copies ran while one was open for 11% -> 14% of each run, Pallas kernels for 28% -> 29%
where the time goes in v5:
time: 149 us; the launch traced here: 148 us
  Pallas kernels  56.8 us (38%)
  starting transfers between devices  27.9 us (19%)
  waiting for transfers between devices  19.6 us (13%)
  local copies, waits for them, and re-layouts  17.8 us (12%)
  matrix products  14.6 us (10%)
  other arithmetic  11.2 us (8%)
    pallas_call x4, Pallas kernels, correlate(): pl.pallas_call(functools.partial(correlate_kernel, with_counts=with_count...  56.8 us
    all_to_all x4, starting transfers between devices, body(): turned = lax.all_to_all(spectra_j, ('wide', 'tm'), 0, 0, tiled=True)  22.1 us
    all_to_all x4, waiting for transfers between devices, body(): turned = lax.all_to_all(spectra_j, ('wide', 'tm'), 0, 0, tiled=True)  11 us
    dot_general x2, matrix products, channelize(): lax.dot_general(rows, flattened, NT, preferred_element_type=jnp.float32)  10.1 us
    all_to_all x1, waiting for transfers between devices, body(): received = lax.all_to_all(send, ('wide', 'tm'), 0, 0, tiled=True)  8.64 us
    all_to_all x1, starting transfers between devices, body(): received = lax.all_to_all(send, ('wide', 'tm'), 0, 0, tiled=True)  5.83 us
    dot_general x1, matrix products, body(): lax.dot_general(stacked_in, delay, (((0,), (0,)), ((), ())), precision=la...  4.54 us
    concatenate x6, other arithmetic, unskew(): jnp.concatenate([forward[..., :1], lower[..., :FEEDS - 1]], axis=-1)  4.17 us
  transfers between devices with their start and end apart: 5, of which 2 were waited for; matrix products, arithmetic and copies ran while one was open for 14% of the time, Pallas kernels for 29%

profile of v5, /device:TPU:0, one launch (start us, length us, event | category | flops | bytes accessed | tf_op | source)
XLA Modules:
  0.0 148.4 jit_solution(11850119134291292643)
XLA Ops:
  0.0 6.6 %convolution_convert_fusion = bf16[768,1024]{1,0:T(8,128)(2,1)S(1)} fusion(bf16[768,2048]{1,0:T(8,128)(2,1)} %constant.49, bf16[1024,2048]{1,0:T(8,128)(2,1)} %bitcast.188), kind=kOutput, calls=%fused_computation.8 | convolution fusion | flops 3222011904 | bytes 8912896 | tf_op jit(solution)/shard_map/dot_general | solution.py:169
  6.7 1.0 squeeze.93
  7.8 7.3 %all-to-all-start.1 = ((bf16[32,4,16,128]{3,2,1,0:T(8,128)(2,1)}), bf16[32,4,16,128]{3,2,1,0:T(8,128)(2,1)S(1)}, u32[]{:S(2)}, u32[]{:S(2)}) async-start(bf16[32,4,16,128]{3,2,1,0:T(8,128)(2,1)} %squeeze.93), calls=%async_computation.1 | async-start | bytes 1048576 | tf_op jit(solution)/shard_map/all_to_all | solution.py:205
  15.1 3.5 %convolution_convert_fusion.1 = bf16[256,1024]{1,0:T(8,128)(2,1)S(1)} fusion(bf16[256,2048]{1,0:T(8,128)(2,1)S(1)} %copy-done.10, bf16[1024,2048]{1,0:T(8,128)(2,1)} %bitcast.189), kind=kOutput, calls=%fused_computation.9 | convolution fusion | flops 1074003968 | bytes 5767168 | tf_op jit(solution)/shard_map/dot_general | solution.py:169
  18.6 1.0 squeeze_reshape.3
  19.6 11.0 %all-to-all-done.1 = bf16[32,4,16,128]{3,2,1,0:T(8,128)(2,1)S(1)} async-done(((bf16[32,4,16,128]{3,2,1,0:T(8,128)(2,1)}), bf16[32,4,16,128]{3,2,1,0:T(8,128)(2,1)S(1)}, u32[]{:S(2)}, u32[]{:S(2)}) %all-to-all-start.1) | async-done | bytes 524320 | tf_op jit(solution)/shard_map/all_to_all | solution.py:205
  30.6 3.1 %all-to-all-start = ((bf16[32,4,16,128]{3,2,1,0:T(8,128)(2,1)}), bf16[32,4,16,128]{3,2,1,0:T(8,128)(2,1)S(1)}, u32[]{:S(2)}, u32[]{:S(2)}) async-start(bf16[32,4,16,128]{3,2,1,0:T(8,128)(2,1)} %squeeze_reshape.3), calls=%async_computation | async-start | bytes 1048576 | tf_op jit(solution)/shard_map/all_to_all | solution.py:205
  33.7 1.0 squeeze.95
  34.9 2.6 %compare_select_fusion = (bf16[8,1024,128]{2,1,0:T(8,128)(2,1)}, bf16[8,1024,128]{2,1,0:T(8,128)(2,1)}) fusion(s32[8,128]{1,0:T(8,128)S(1)} %multiply_add_fusion, s32[1024]{0:T(1024)S(1)} %bitcast.146, bf16[8,128]{1,0:T(8,128)(2,1)S(1)} %convert_bitcast_fusion, s32[1024]{0:T(1024)S(1)} %copy-done.8), kind=kLoop, calls=%fused_computation.4 | loop fusion | flops 4194304 | bytes 4208640 | tf_op jit(solution)/shard_map/jit(_where)/select_n | solution.py:182
  37.5 13.9 %shard_map.74 = f32[4,2,16,256]{3,2,1,0:T(8,128)} custom-call(bf16[8,4,4,16,128]{4,3,2,1,0:T(8,128)(2,1)} %bitcast.142, bf16[8,1024,128]{2,1,0:T(8,128)(2,1)} %get-tuple-element.57.refs_1_, bf16[8,1024,128]{2,1,0:T(8,128)(2,1)} %get-tuple-element.56.refs_2_, bf16[64,64]{1,0:T(8,128)(2,1)} %constant.43.clone.refs_3_), custom_call_target="tpu_custom_call" | custom-call | flops 1778384896 | bytes 4849664 | tf_op jit(solution)/shard_map/pallas_call | solution.py:128
  51.4 6.0 %all-to-all-start.3 = ((bf16[32,4,16,128]{3,2,1,0:T(8,128)(2,1)}), bf16[32,4,16,128]{3,2,1,0:T(8,128)(2,1)S(1)}, u32[]{:S(2)}, u32[]{:S(2)}) async-start(bf16[32,4,16,128]{3,2,1,0:T(8,128)(2,1)} %squeeze.95), calls=%async_computation.3 | async-start | bytes 1048576 | tf_op jit(solution)/shard_map/all_to_all | solution.py:205
  57.5 1.0 squeeze.94
  58.7 1.4 fusion.2
  60.1 1.2 broadcast_select_fusion
  61.3 15.1 %shard_map.73 = (f32[4,2,16,256]{3,2,1,0:T(8,128)}, f32[16,256]{1,0:T(8,128)}) custom-call(bf16[8,4,4,16,128]{4,3,2,1,0:T(8,128)(2,1)} %bitcast.140, bf16[8,1024,128]{2,1,0:T(8,128)(2,1)} %get-tuple-element.57.refs_1_, bf16[8,1024,128]{2,1,0:T(8,128)(2,1)} %get-tuple-element.56.refs_2_, bf16[64,64]{1,0:T(8,128)(2,1)} %constant.43.clone.refs_3_, ...), custom_call_target="tpu_custom_call" | custom-call | flops 1778384896 | bytes 4849664 | tf_op jit(solution)/shard_map/pallas_call | solution.py:128
  76.3 5.7 %all-to-all-start.2 = ((bf16[32,4,16,128]{3,2,1,0:T(8,128)(2,1)}), bf16[32,4,16,128]{3,2,1,0:T(8,128)(2,1)S(1)}, u32[]{:S(2)}, u32[]{:S(2)}) async-start(bf16[32,4,16,128]{3,2,1,0:T(8,128)(2,1)} %squeeze.94), calls=%async_computation.2 | async-start | bytes 1048576 | tf_op jit(solution)/shard_map/all_to_all | solution.py:205
  82.1 0.9 fusion.9
  83.0 1.0 fusion.7
  83.9 13.9 %shard_map.76 = f32[4,2,16,256]{3,2,1,0:T(8,128)} custom-call(bf16[8,4,4,16,128]{4,3,2,1,0:T(8,128)(2,1)} %bitcast.139, bf16[8,1024,128]{2,1,0:T(8,128)(2,1)} %get-tuple-element.57.refs_1_, bf16[8,1024,128]{2,1,0:T(8,128)(2,1)} %get-tuple-element.56.refs_2_, bf16[64,64]{1,0:T(8,128)(2,1)} %constant.43.clone.refs_3_), custom_call_target="tpu_custom_call" | custom-call | flops 1778384896 | bytes 4849664 | tf_op jit(solution)/shard_map/pallas_call | solution.py:128
  97.9 0.8 copy-done.2
  98.7 13.9 %shard_map.75 = f32[4,2,16,256]{3,2,1,0:T(8,128)} custom-call(bf16[8,4,4,16,128]{4,3,2,1,0:T(8,128)(2,1)} %bitcast.141, bf16[8,1024,128]{2,1,0:T(8,128)(2,1)} %get-tuple-element.57.refs_1_, bf16[8,1024,128]{2,1,0:T(8,128)(2,1)} %get-tuple-element.56.refs_2_, bf16[64,64]{1,0:T(8,128)(2,1)} %constant.43.clone.refs_3_), custom_call_target="tpu_custom_call" | custom-call | flops 1778384896 | bytes 4849664 | tf_op jit(solution)/shard_map/pallas_call | solution.py:128
  112.6 0.9 pad_maximum_fusion
  120.1 1.2 copy.126
  121.3 5.8 %all-to-all-start.4 = ((f32[32,16,2,128]{3,2,1,0:T(2,128)}), f32[32,16,2,128]{3,2,1,0:T(2,128)S(1)}, u32[]{:S(2)}, u32[]{:S(2)}) async-start(f32[32,16,2,128]{3,2,1,0:T(2,128)} %copy.126), calls=%async_computation.4 | async-start | bytes 1048576 | tf_op jit(solution)/shard_map/all_to_all | solution.py:217
  127.1 1.5 %fusion.8 = (f32[1,1]{1,0:T(1,128)}, f32[1,1]{1,0:T(1,128)}, f32[1,1]{1,0:T(1,128)}, f32[1,1]{1,0:T(1,128)}, f32[1,1]{1,0:T(1,128)}, /*index=5*/f32[1,1]{1,0:T(1,128)}) fusion(f32[16,256]{1,0:T(8,128)} %get-tuple-element.12), kind=kLoop, calls=%fused_computation.77 | loop fusion | bytes 48 | tf_op jit(solution)/shard_map/slice | solution.py:146
  129.6 0.7 pad_maximum_fusion.1
  131.0 0.7 pad_maximum_fusion.3
  131.7 0.7 pad_maximum_fusion.4
  133.0 0.8 pad_maximum_fusion.6
  134.0 8.6 %all-to-all-done.4 = f32[32,16,2,128]{3,2,1,0:T(2,128)S(1)} async-done(((f32[32,16,2,128]{3,2,1,0:T(2,128)}), f32[32,16,2,128]{3,2,1,0:T(2,128)S(1)}, u32[]{:S(2)}, u32[]{:S(2)}) %all-to-all-start.4) | async-done | bytes 524320 | tf_op jit(solution)/shard_map/all_to_all | solution.py:217
  142.7 4.5 %convolution_multiply_fusion = f32[128,2,512]{2,0,1:T(8,128)S(1)} fusion(f32[1024,128,1]{1,0,2:T(8,128)S(1)} %bitcast.138, f32[2,512,1024]{2,1,0:T(8,128)} %constant.51, f32[128]{0:T(128)S(1)} %multiply_rsqrt_fusion), kind=kOutput, calls=%fused_computation.10 | convolution fusion | flops 805437440 | bytes 5243392 | tf_op jit(solution)/shard_map/dot_general | solution.py:225
  147.2 1.2 copy.128
  (119 shorter events, 9.3 us)
Async XLA Ops:
  6.6 8.5 %copy-start.10 = (bf16[256,2048]{1,0:T(8,128)(2,1)S(1)}, bf16[256,2048]{1,0:T(8,128)(2,1)}, u32[]{:S(2)}) copy-start(bf16[256,2048]{1,0:T(8,128)(2,1)} %constant.47) | copy-start | bytes 3145732
  7.8 22.9 %all-to-all-start.1 = ((bf16[32,4,16,128]{3,2,1,0:T(8,128)(2,1)}), bf16[32,4,16,128]{3,2,1,0:T(8,128)(2,1)S(1)}, u32[]{:S(2)}, u32[]{:S(2)}) async-start(bf16[32,4,16,128]{3,2,1,0:T(8,128)(2,1)} %squeeze.93), calls=%async_computation.1 | async-start | bytes 1048576 | tf_op jit(solution)/shard_map/all_to_all | solution.py:205
  15.1 19.6 %copy-start.8 = (s32[1024]{0:T(1024)S(1)}, s32[1024]{0:T(1024)}, u32[]{:S(2)}) copy-start(s32[1024]{0:T(1024)} %param.8) | copy-start | bytes 12292
  15.1 19.8 %copy-start.9 = (s32[1024]{0:T(1024)S(1)}, s32[1024]{0:T(1024)}, u32[]{:S(2)}) copy-start(s32[1024]{0:T(1024)} %param.9) | copy-start | bytes 12292
  30.6 6.9 %copy-start.3 = (bf16[32,4,16,128]{3,2,1,0:T(8,128)(2,1)}, bf16[32,4,16,128]{3,2,1,0:T(8,128)(2,1)S(1)}, u32[]{:S(2)}) copy-start(bf16[32,4,16,128]{3,2,1,0:T(8,128)(2,1)S(1)} %all-to-all-done.1) | copy-start | bytes 1572868
  30.6 20.8 %all-to-all-start = ((bf16[32,4,16,128]{3,2,1,0:T(8,128)(2,1)}), bf16[32,4,16,128]{3,2,1,0:T(8,128)(2,1)S(1)}, u32[]{:S(2)}, u32[]{:S(2)}) async-start(bf16[32,4,16,128]{3,2,1,0:T(8,128)(2,1)} %squeeze_reshape.3), calls=%async_computation | async-start | bytes 1048576 | tf_op jit(solution)/shard_map/all_to_all | solution.py:205
  51.4 9.8 %copy-start.1 = (bf16[32,4,16,128]{3,2,1,0:T(8,128)(2,1)}, bf16[32,4,16,128]{3,2,1,0:T(8,128)(2,1)S(1)}, u32[]{:S(2)}) copy-start(bf16[32,4,16,128]{3,2,1,0:T(8,128)(2,1)S(1)} %all-to-all-done) | copy-start | bytes 1572868
  51.4 24.9 %all-to-all-start.3 = ((bf16[32,4,16,128]{3,2,1,0:T(8,128)(2,1)}), bf16[32,4,16,128]{3,2,1,0:T(8,128)(2,1)S(1)}, u32[]{:S(2)}, u32[]{:S(2)}) async-start(bf16[32,4,16,128]{3,2,1,0:T(8,128)(2,1)} %squeeze.95), calls=%async_computation.3 | async-start | bytes 1048576 | tf_op jit(solution)/shard_map/all_to_all | solution.py:205
  76.3 7.6 %copy-start = (bf16[32,4,16,128]{3,2,1,0:T(8,128)(2,1)}, bf16[32,4,16,128]{3,2,1,0:T(8,128)(2,1)S(1)}, u32[]{:S(2)}) copy-start(bf16[32,4,16,128]{3,2,1,0:T(8,128)(2,1)S(1)} %all-to-all-done.3) | copy-start | bytes 1572868
  76.3 21.5 %all-to-all-start.2 = ((bf16[32,4,16,128]{3,2,1,0:T(8,128)(2,1)}), bf16[32,4,16,128]{3,2,1,0:T(8,128)(2,1)S(1)}, u32[]{:S(2)}, u32[]{:S(2)}) async-start(bf16[32,4,16,128]{3,2,1,0:T(8,128)(2,1)} %squeeze.94), calls=%async_computation.2 | async-start | bytes 1048576 | tf_op jit(solution)/shard_map/all_to_all | solution.py:205
  97.8 14.7 %copy-start.4 = (f32[4,2,16,256]{3,2,1,0:T(8,128)S(1)}, f32[4,2,16,256]{3,2,1,0:T(8,128)}, u32[]{:S(2)}) copy-start(f32[4,2,16,256]{3,2,1,0:T(8,128)} %shard_map.74) | copy-start | bytes 393220
  97.9 14.7 %copy-start.5 = (f32[4,2,16,256]{3,2,1,0:T(8,128)S(1)}, f32[4,2,16,256]{3,2,1,0:T(8,128)}, u32[]{:S(2)}) copy-start(f32[4,2,16,256]{3,2,1,0:T(8,128)} %get-tuple-element.9) | copy-start | bytes 393220
  97.9 14.7 %copy-start.6 = (f32[4,2,16,256]{3,2,1,0:T(8,128)S(1)}, f32[4,2,16,256]{3,2,1,0:T(8,128)}, u32[]{:S(2)}) copy-start(f32[4,2,16,256]{3,2,1,0:T(8,128)} %shard_map.76) | copy-start | bytes 393220
  97.9 0.8 copy-start.2
  98.7 20.2 %copy-start.7 = (f32[2]{0:T(128)S(1)}, f32[2]{0:T(128)}, u32[]{:S(2)}) copy-start(f32[2]{0:T(128)} %constant.44.clone) | copy-start | bytes 28
  121.3 21.4 %all-to-all-start.4 = ((f32[32,16,2,128]{3,2,1,0:T(2,128)}), f32[32,16,2,128]{3,2,1,0:T(2,128)S(1)}, u32[]{:S(2)}, u32[]{:S(2)}) async-start(f32[32,16,2,128]{3,2,1,0:T(2,128)} %copy.126), calls=%async_computation.4 | async-start | bytes 1048576 | tf_op jit(solution)/shard_map/all_to_all | solution.py:217

commit v6 on v5

--- a/solution.py
+++ b/solution.py
@@ -67,9 +67,9 @@
 
 def correlate_kernel(*refs, with_counts):
     if with_counts:
-        x_ref, pt_ref, ptr_ref, rm_ref, fm_ref, fmr_ref, o_ref, n_ref = refs
+        x_ref, pt_ref, j_ref, rm_ref, fm_ref, fmr_ref, o_ref, n_ref = refs
     else:
-        x_ref, pt_ref, ptr_ref, rm_ref, o_ref = refs
+        x_ref, pt_ref, j_ref, rm_ref, o_ref = refs
     wide_parts = x_ref.shape[0]
     row_at = lax.broadcasted_iota(jnp.int32, (FEEDS, FEEDS), 0)
     col_at = lax.broadcasted_iota(jnp.int32, (FEEDS, FEEDS), 1)
@@ -84,15 +84,19 @@
             diag_pairs(fm_ref[...], fmr_ref[...], upper, write_count)
 
     g = None
-    gr = None
     for w in range(wide_parts):
         xw = x_ref[w].reshape(-1, x_ref.shape[-1])
         gw = lax.dot_general(pt_ref[w], xw, NT, preferred_element_type=jnp.float32)
-        grw = lax.dot_general(ptr_ref[w], xw, NT, preferred_element_type=jnp.float32)
         g = gw if g is None else g + gw
-        gr = grw if gr is None else gr + grw
     g = g.astype(jnp.bfloat16)
-    gr = gr.astype(jnp.bfloat16)
+    flip = j_ref[...]
+    gr = jnp.concatenate(
+        [
+            jnp.dot(flip, g[b * FEEDS:(b + 1) * FEEDS], preferred_element_type=jnp.float32)
+            for b in range(CYL)
+        ],
+        axis=0,
+    ).astype(jnp.bfloat16)
     yr = jnp.dot(gr, rm_ref[...], preferred_element_type=jnp.float32).astype(jnp.bfloat16)
     for part, right in enumerate((gr, yr)):
         def write_vis(slot, value, part=part):
@@ -101,18 +105,18 @@
         diag_pairs(g, right, upper, write_vis)
 
 
-def correlate(blocks, pt, ptr, rm, fm=None, fmr=None):
+def correlate(blocks, pt, flip, rm, fm=None, fmr=None):
     wide_parts, tm_parts, local_channels, rows_each, inputs_each = blocks.shape
     with_counts = fm is not None
     in_specs = [
         pl.BlockSpec((wide_parts, tm_parts, None, rows_each, inputs_each), lambda c: (0, 0, c, 0, 0)),
         pl.BlockSpec(pt.shape, lambda c: (0, 0, 0)),
-        pl.BlockSpec(ptr.shape, lambda c: (0, 0, 0)),
+        pl.BlockSpec(flip.shape, lambda c: (0, 0)),
         pl.BlockSpec(rm.shape, lambda c: (0, 0)),
     ]
     out_specs = [pl.BlockSpec((1, 2, CYL * CYL, FEEDS), lambda c: (c, 0, 0, 0))]
     out_shape = [jax.ShapeDtypeStruct((local_channels, 2, CYL * CYL, FEEDS), jnp.float32)]
-    operands = [blocks, pt, ptr, rm]
+    operands = [blocks, pt, flip, rm]
     if with_counts:
         in_specs += [pl.BlockSpec(fm.shape, lambda c: (0, 0)), pl.BlockSpec(fmr.shape, lambda c: (0, 0))]
         out_specs.append(pl.BlockSpec((CYL * CYL, FEEDS), lambda c: (0, 0)))
@@ -121,10 +125,11 @@
     positions = CYL * FEEDS
     rows = tm_parts * rows_each
     flops = local_channels * (
-        2 * 2 * positions * wide_parts * inputs_each * rows + 2 * positions * rows * rows
+        2 * positions * wide_parts * inputs_each * rows + 2 * positions * FEEDS * rows
+        + 2 * positions * rows * rows
         + 20 * 2 * FEEDS * FEEDS * rows
     )
-    bytes_accessed = blocks.size * 2 + pt.size * 4 + local_channels * 2 * CYL * CYL * FEEDS * 4
+    bytes_accessed = blocks.size * 2 + pt.size * 2 + local_channels * 2 * CYL * CYL * FEEDS * 4
     return pl.pallas_call(
         functools.partial(correlate_kernel, with_counts=with_counts),
         grid=(local_channels,),
@@ -184,7 +189,7 @@
     fm = jnp.sum(pt_full.astype(jnp.float32), axis=1).astype(jnp.bfloat16)[:, None] * first_lane
     fmr = jnp.sum(ptr_full.astype(jnp.float32), axis=1).astype(jnp.bfloat16)[:, None] * first_lane
     pt = pt_full.reshape(CYL * FEEDS, wide_parts, inputs_here).transpose(1, 0, 2)
-    ptr = ptr_full.reshape(CYL * FEEDS, wide_parts, inputs_here).transpose(1, 0, 2)
+    flip = jnp.asarray(np.eye(FEEDS, dtype=np.float32)[::-1], dtype=jnp.bfloat16)
 
     rows = tm_parts * 2 * frames_here
     r_at = np.arange(rows)
@@ -205,10 +210,10 @@
         turned = lax.all_to_all(spectra_j, ("wide", "tm"), 0, 0, tiled=True)
         blk = turned.reshape(wide_parts, tm_parts, chunk_channels, 2 * frames_here, inputs_here)
         if j == 0:
-            first, count_sums = correlate(blk, pt, ptr, rm, fm, fmr)
+            first, count_sums = correlate(blk, pt, flip, rm, fm, fmr)
             sums.append(first)
         else:
-            sums.append(correlate(blk, pt, ptr, rm)[0])
+            sums.append(correlate(blk, pt, flip, rm)[0])
     sums = jnp.concatenate(sums, axis=0)
     conj_sign = jnp.array([1.0, -1.0], jnp.float32)[None, :, None]
     vis = unskew(sums, conj_sign)

time: 149 us -> 153 us (1.027)
  Pallas kernels: 56.8 us -> 60.8 us
    pallas_call x4, Pallas kernels: 56.8 us -> 60.8 us  [correlate(): pl.pallas_call(functools.partial(correlate_kernel, with_counts=with_count...]
  transfers between devices with their start and end apart: 5 -> 5, of which waited for: 2 -> 2; matrix products, arithmetic and copies ran while one was open for 14% -> 13% of each run, Pallas kernels for 29% -> 30%
where the time goes in v6:
time: 153 us; the launch traced here: 152 us
  Pallas kernels  60.8 us (40%)
  starting transfers between devices  27.9 us (18%)
  waiting for transfers between devices  19.7 us (13%)
  local copies, waits for them, and re-layouts  17.8 us (12%)
  matrix products  14.6 us (10%)
  other arithmetic  10.5 us (7%)
    pallas_call x4, Pallas kernels, correlate(): pl.pallas_call(functools.partial(correlate_kernel, with_counts=with_count...  60.8 us
    all_to_all x4, starting transfers between devices, body(): turned = lax.all_to_all(spectra_j, ('wide', 'tm'), 0, 0, tiled=True)  22.1 us
    all_to_all x4, waiting for transfers between devices, body(): turned = lax.all_to_all(spectra_j, ('wide', 'tm'), 0, 0, tiled=True)  11 us
    dot_general x2, matrix products, channelize(): lax.dot_general(rows, flattened, NT, preferred_element_type=jnp.float32)  10.1 us
    all_to_all x1, waiting for transfers between devices, body(): received = lax.all_to_all(send, ('wide', 'tm'), 0, 0, tiled=True)  8.71 us
    all_to_all x1, starting transfers between devices, body(): received = lax.all_to_all(send, ('wide', 'tm'), 0, 0, tiled=True)  5.83 us
    dot_general x1, matrix products, body(): lax.dot_general(stacked_in, delay, (((0,), (0,)), ((), ())), precision=la...  4.53 us
    concatenate x6, other arithmetic, unskew(): jnp.concatenate([forward[..., :1], lower[..., :FEEDS - 1]], axis=-1)  4.11 us
  transfers between devices with their start and end apart: 5, of which 2 were waited for; matrix products, arithmetic and copies ran while one was open for 13% of the time, Pallas kernels for 30%

profile of v6, /device:TPU:0, one launch (start us, length us, event | category | flops | bytes accessed | tf_op | source)
XLA Modules:
  0.0 151.8 jit_solution(943050612944227095)
XLA Ops:
  0.0 6.6 %convolution_convert_fusion = bf16[768,1024]{1,0:T(8,128)(2,1)S(1)} fusion(bf16[768,2048]{1,0:T(8,128)(2,1)} %constant.51, bf16[1024,2048]{1,0:T(8,128)(2,1)} %bitcast.187), kind=kOutput, calls=%fused_computation.7 | convolution fusion | flops 3222011904 | bytes 8912896 | tf_op jit(solution)/shard_map/dot_general | solution.py:174
  6.7 1.0 squeeze.93
  7.8 7.3 %all-to-all-start.1 = ((bf16[32,4,16,128]{3,2,1,0:T(8,128)(2,1)}), bf16[32,4,16,128]{3,2,1,0:T(8,128)(2,1)S(1)}, u32[]{:S(2)}, u32[]{:S(2)}) async-start(bf16[32,4,16,128]{3,2,1,0:T(8,128)(2,1)} %squeeze.93), calls=%async_computation.1 | async-start | bytes 1048576 | tf_op jit(solution)/shard_map/all_to_all | solution.py:210
  15.1 3.5 %convolution_convert_fusion.1 = bf16[256,1024]{1,0:T(8,128)(2,1)S(1)} fusion(bf16[256,2048]{1,0:T(8,128)(2,1)S(1)} %copy-done.10, bf16[1024,2048]{1,0:T(8,128)(2,1)} %bitcast.188), kind=kOutput, calls=%fused_computation.8 | convolution fusion | flops 1074003968 | bytes 5767168 | tf_op jit(solution)/shard_map/dot_general | solution.py:174
  18.6 1.0 squeeze_reshape.3
  19.6 11.0 %all-to-all-done.1 = bf16[32,4,16,128]{3,2,1,0:T(8,128)(2,1)S(1)} async-done(((bf16[32,4,16,128]{3,2,1,0:T(8,128)(2,1)}), bf16[32,4,16,128]{3,2,1,0:T(8,128)(2,1)S(1)}, u32[]{:S(2)}, u32[]{:S(2)}) %all-to-all-start.1) | async-done | bytes 524320 | tf_op jit(solution)/shard_map/all_to_all | solution.py:210
  30.6 3.1 %all-to-all-start = ((bf16[32,4,16,128]{3,2,1,0:T(8,128)(2,1)}), bf16[32,4,16,128]{3,2,1,0:T(8,128)(2,1)S(1)}, u32[]{:S(2)}, u32[]{:S(2)}) async-start(bf16[32,4,16,128]{3,2,1,0:T(8,128)(2,1)} %squeeze_reshape.3), calls=%async_computation | async-start | bytes 1048576 | tf_op jit(solution)/shard_map/all_to_all | solution.py:210
  33.7 1.0 squeeze.95
  34.7 1.9 %compare_select_fusion.refs_1_ = bf16[8,1024,128]{2,1,0:T(8,128)(2,1)} fusion(s32[8,128]{1,0:T(8,128)S(1)} %multiply_add_fusion, s32[1024]{0:T(1024)S(1)} %copy-done.8, bf16[8,128]{1,0:T(8,128)(2,1)S(1)} %convert_bitcast_fusion), kind=kLoop, calls=%fused_computation.4 | loop fusion | flops 2097152 | bytes 2107392 | tf_op jit(solution)/shard_map/jit(_where)/select_n | solution.py:186
  36.6 14.9 %shard_map.83 = f32[4,2,16,256]{3,2,1,0:T(8,128)} custom-call(bf16[8,4,4,16,128]{4,3,2,1,0:T(8,128)(2,1)} %bitcast.142, bf16[8,1024,128]{2,1,0:T(8,128)(2,1)} %compare_select_fusion.refs_1_, bf16[256,256]{1,0:T(8,128)(2,1)} %constant.44.clone.refs_2_, bf16[64,64]{1,0:T(8,128)(2,1)} %constant.45.clone.refs_3_), custom_call_target="tpu_custom_call" | custom-call | flops 1375731712 | bytes 2752512 | tf_op jit(solution)/shard_map/pallas_call | solution.py:133
  51.5 6.0 %all-to-all-start.3 = ((bf16[32,4,16,128]{3,2,1,0:T(8,128)(2,1)}), bf16[32,4,16,128]{3,2,1,0:T(8,128)(2,1)S(1)}, u32[]{:S(2)}, u32[]{:S(2)}) async-start(bf16[32,4,16,128]{3,2,1,0:T(8,128)(2,1)} %squeeze.95), calls=%async_computation.3 | async-start | bytes 1048576 | tf_op jit(solution)/shard_map/all_to_all | solution.py:210
  57.6 1.0 squeeze.94
  59.0 1.4 fusion.2
  60.4 1.2 broadcast_select_fusion
  61.6 16.0 %shard_map.82 = (f32[4,2,16,256]{3,2,1,0:T(8,128)}, f32[16,256]{1,0:T(8,128)}) custom-call(bf16[8,4,4,16,128]{4,3,2,1,0:T(8,128)(2,1)} %bitcast.140, bf16[8,1024,128]{2,1,0:T(8,128)(2,1)} %compare_select_fusion.refs_1_, bf16[256,256]{1,0:T(8,128)(2,1)} %constant.44.clone.refs_2_, bf16[64,64]{1,0:T(8,128)(2,1)} %constant.45.clone.refs_3_, ...), custom_call_target="tpu_custom_call" | custom-call | flops 1375731712 | bytes 2752512 | tf_op jit(solution)/shard_map/pallas_call | solution.py:133
  77.6 5.7 %all-to-all-start.2 = ((bf16[32,4,16,128]{3,2,1,0:T(8,128)(2,1)}), bf16[32,4,16,128]{3,2,1,0:T(8,128)(2,1)S(1)}, u32[]{:S(2)}, u32[]{:S(2)}) async-start(bf16[32,4,16,128]{3,2,1,0:T(8,128)(2,1)} %squeeze.94), calls=%async_computation.2 | async-start | bytes 1048576 | tf_op jit(solution)/shard_map/all_to_all | solution.py:210
  83.3 0.9 fusion.9
  84.2 1.0 fusion.7
  85.2 15.0 %shard_map.85 = f32[4,2,16,256]{3,2,1,0:T(8,128)} custom-call(bf16[8,4,4,16,128]{4,3,2,1,0:T(8,128)(2,1)} %bitcast.139, bf16[8,1024,128]{2,1,0:T(8,128)(2,1)} %compare_select_fusion.refs_1_, bf16[256,256]{1,0:T(8,128)(2,1)} %constant.44.clone.refs_2_, bf16[64,64]{1,0:T(8,128)(2,1)} %constant.45.clone.refs_3_), custom_call_target="tpu_custom_call" | custom-call | flops 1375731712 | bytes 2752512 | tf_op jit(solution)/shard_map/pallas_call | solution.py:133
  100.2 0.8 copy-done.2
  101.0 14.9 %shard_map.84 = f32[4,2,16,256]{3,2,1,0:T(8,128)} custom-call(bf16[8,4,4,16,128]{4,3,2,1,0:T(8,128)(2,1)} %bitcast.141, bf16[8,1024,128]{2,1,0:T(8,128)(2,1)} %compare_select_fusion.refs_1_, bf16[256,256]{1,0:T(8,128)(2,1)} %constant.44.clone.refs_2_, bf16[64,64]{1,0:T(8,128)(2,1)} %constant.45.clone.refs_3_), custom_call_target="tpu_custom_call" | custom-call | flops 1375731712 | bytes 2752512 | tf_op jit(solution)/shard_map/pallas_call | solution.py:133
  115.9 1.0 pad_maximum_fusion
  123.4 1.2 copy.127
  124.6 5.8 %all-to-all-start.4 = ((f32[32,16,2,128]{3,2,1,0:T(2,128)}), f32[32,16,2,128]{3,2,1,0:T(2,128)S(1)}, u32[]{:S(2)}, u32[]{:S(2)}) async-start(f32[32,16,2,128]{3,2,1,0:T(2,128)} %copy.127), calls=%async_computation.4 | async-start | bytes 1048576 | tf_op jit(solution)/shard_map/all_to_all | solution.py:222
  130.5 1.5 %fusion.8 = (f32[1,1]{1,0:T(1,128)}, f32[1,1]{1,0:T(1,128)}, f32[1,1]{1,0:T(1,128)}, f32[1,1]{1,0:T(1,128)}, f32[1,1]{1,0:T(1,128)}, /*index=5*/f32[1,1]{1,0:T(1,128)}) fusion(f32[16,256]{1,0:T(8,128)} %get-tuple-element.12), kind=kLoop, calls=%fused_computation.76 | loop fusion | bytes 48 | tf_op jit(solution)/shard_map/slice | solution.py:151
  133.6 0.7 pad_maximum_fusion.2
  134.3 0.7 pad_maximum_fusion.3
  135.6 0.8 pad_maximum_fusion.5
  136.4 0.7 pad_maximum_fusion.6
  137.3 8.7 %all-to-all-done.4 = f32[32,16,2,128]{3,2,1,0:T(2,128)S(1)} async-done(((f32[32,16,2,128]{3,2,1,0:T(2,128)}), f32[32,16,2,128]{3,2,1,0:T(2,128)S(1)}, u32[]{:S(2)}, u32[]{:S(2)}) %all-to-all-start.4) | async-done | bytes 524320 | tf_op jit(solution)/shard_map/all_to_all | solution.py:222
  146.0 4.5 %convolution_multiply_fusion = f32[128,2,512]{2,0,1:T(8,128)S(1)} fusion(f32[1024,128,1]{1,0,2:T(8,128)S(1)} %bitcast.138, f32[2,512,1024]{2,1,0:T(8,128)} %constant.53, f32[128]{0:T(128)S(1)} %multiply_rsqrt_fusion), kind=kOutput, calls=%fused_computation.9 | convolution fusion | flops 805437440 | bytes 5243392 | tf_op jit(solution)/shard_map/dot_general | solution.py:230
  150.6 1.2 copy.129
  (119 shorter events, 9.3 us)
Async XLA Ops:
  6.6 8.5 %copy-start.10 = (bf16[256,2048]{1,0:T(8,128)(2,1)S(1)}, bf16[256,2048]{1,0:T(8,128)(2,1)}, u32[]{:S(2)}) copy-start(bf16[256,2048]{1,0:T(8,128)(2,1)} %constant.49) | copy-start | bytes 3145732
  7.8 22.9 %all-to-all-start.1 = ((bf16[32,4,16,128]{3,2,1,0:T(8,128)(2,1)}), bf16[32,4,16,128]{3,2,1,0:T(8,128)(2,1)S(1)}, u32[]{:S(2)}, u32[]{:S(2)}) async-start(bf16[32,4,16,128]{3,2,1,0:T(8,128)(2,1)} %squeeze.93), calls=%async_computation.1 | async-start | bytes 1048576 | tf_op jit(solution)/shard_map/all_to_all | solution.py:210
  15.1 19.6 %copy-start.9 = (s32[1024]{0:T(1024)S(1)}, s32[1024]{0:T(1024)}, u32[]{:S(2)}) copy-start(s32[1024]{0:T(1024)} %param.10) | copy-start | bytes 12292
  15.1 19.6 %copy-start.8 = (s32[1024]{0:T(1024)S(1)}, s32[1024]{0:T(1024)}, u32[]{:S(2)}) copy-start(s32[1024]{0:T(1024)} %param.9) | copy-start | bytes 12292
  30.6 6.0 %copy-start.3 = (bf16[32,4,16,128]{3,2,1,0:T(8,128)(2,1)}, bf16[32,4,16,128]{3,2,1,0:T(8,128)(2,1)S(1)}, u32[]{:S(2)}) copy-start(bf16[32,4,16,128]{3,2,1,0:T(8,128)(2,1)S(1)} %all-to-all-done.1) | copy-start | bytes 1572868
  30.6 20.9 %all-to-all-start = ((bf16[32,4,16,128]{3,2,1,0:T(8,128)(2,1)}), bf16[32,4,16,128]{3,2,1,0:T(8,128)(2,1)S(1)}, u32[]{:S(2)}, u32[]{:S(2)}) async-start(bf16[32,4,16,128]{3,2,1,0:T(8,128)(2,1)} %squeeze_reshape.3), calls=%async_computation | async-start | bytes 1048576 | tf_op jit(solution)/shard_map/all_to_all | solution.py:210
  51.5 10.0 %copy-start.1 = (bf16[32,4,16,128]{3,2,1,0:T(8,128)(2,1)}, bf16[32,4,16,128]{3,2,1,0:T(8,128)(2,1)S(1)}, u32[]{:S(2)}) copy-start(bf16[32,4,16,128]{3,2,1,0:T(8,128)(2,1)S(1)} %all-to-all-done) | copy-start | bytes 1572868
  51.5 26.1 %all-to-all-start.3 = ((bf16[32,4,16,128]{3,2,1,0:T(8,128)(2,1)}), bf16[32,4,16,128]{3,2,1,0:T(8,128)(2,1)S(1)}, u32[]{:S(2)}, u32[]{:S(2)}) async-start(bf16[32,4,16,128]{3,2,1,0:T(8,128)(2,1)} %squeeze.95), calls=%async_computation.3 | async-start | bytes 1048576 | tf_op jit(solution)/shard_map/all_to_all | solution.py:210
  77.6 7.6 %copy-start = (bf16[32,4,16,128]{3,2,1,0:T(8,128)(2,1)}, bf16[32,4,16,128]{3,2,1,0:T(8,128)(2,1)S(1)}, u32[]{:S(2)}) copy-start(bf16[32,4,16,128]{3,2,1,0:T(8,128)(2,1)S(1)} %all-to-all-done.3) | copy-start | bytes 1572868
  77.6 22.6 %all-to-all-start.2 = ((bf16[32,4,16,128]{3,2,1,0:T(8,128)(2,1)}), bf16[32,4,16,128]{3,2,1,0:T(8,128)(2,1)S(1)}, u32[]{:S(2)}, u32[]{:S(2)}) async-start(bf16[32,4,16,128]{3,2,1,0:T(8,128)(2,1)} %squeeze.94), calls=%async_computation.2 | async-start | bytes 1048576 | tf_op jit(solution)/shard_map/all_to_all | solution.py:210
  85.2 30.7 %copy-start.4 = (f32[4,2,16,256]{3,2,1,0:T(8,128)S(1)}, f32[4,2,16,256]{3,2,1,0:T(8,128)}, u32[]{:S(2)}) copy-start(f32[4,2,16,256]{3,2,1,0:T(8,128)} %shard_map.83) | copy-start | bytes 393220
  85.2 30.7 %copy-start.5 = (f32[4,2,16,256]{3,2,1,0:T(8,128)S(1)}, f32[4,2,16,256]{3,2,1,0:T(8,128)}, u32[]{:S(2)}) copy-start(f32[4,2,16,256]{3,2,1,0:T(8,128)} %get-tuple-element.9) | copy-start | bytes 393220
  100.2 15.7 %copy-start.6 = (f32[4,2,16,256]{3,2,1,0:T(8,128)S(1)}, f32[4,2,16,256]{3,2,1,0:T(8,128)}, u32[]{:S(2)}) copy-start(f32[4,2,16,256]{3,2,1,0:T(8,128)} %shard_map.85) | copy-start | bytes 393220
  100.2 0.8 copy-start.2
  101.0 21.2 %copy-start.7 = (f32[2]{0:T(128)S(1)}, f32[2]{0:T(128)}, u32[]{:S(2)}) copy-start(f32[2]{0:T(128)} %constant.46.clone) | copy-start | bytes 28
  124.6 21.4 %all-to-all-start.4 = ((f32[32,16,2,128]{3,2,1,0:T(2,128)}), f32[32,16,2,128]{3,2,1,0:T(2,128)S(1)}, u32[]{:S(2)}, u32[]{:S(2)}) async-start(f32[32,16,2,128]{3,2,1,0:T(2,128)} %copy.127), calls=%async_computation.4 | async-start | bytes 1048576 | tf_op jit(solution)/shard_map/all_to_all | solution.py:222

commit v7 on v5

--- a/solution.py
+++ b/solution.py
@@ -157,7 +157,7 @@
     frames_all = frames_here * tm_parts
     local_channels = CH // devices
     table = channel_table_const(NSAMP, CH, CHAN_LO)
-    chunks = math.gcd(4, local_channels)
+    chunks = math.gcd(2, local_channels)
     chunk_channels = local_channels // chunks
     table = table.reshape(devices, chunks, chunk_channels * 2, length).transpose(1, 0, 2, 3)
     table = jnp.asarray(table.reshape(chunks, devices * chunk_channels * 2, length), dtype=jnp.bfloat16)

time: 149 us -> 140 us (0.940)
  starting transfers between devices: 27.9 us -> 16.9 us
  waiting for transfers between devices: 19.6 us -> 28.9 us
  Pallas kernels: 56.8 us -> 51.1 us
  local copies, waits for them, and re-layouts: 17.8 us -> 13.1 us
  other arithmetic: 11.2 us -> 14.2 us
    all_to_all x4 -> x2, starting transfers between devices: 22.1 us -> 11.1 us  [body(): turned = lax.all_to_all(spectra_j, ('wide', 'tm'), 0, 0, tiled=True)]
    all_to_all x4 -> x2, waiting for transfers between devices: 11 us -> 19.8 us  [body(): turned = lax.all_to_all(spectra_j, ('wide', 'tm'), 0, 0, tiled=True)]
    pallas_call x4 -> x2, Pallas kernels: 56.8 us -> 51.1 us  [correlate(): pl.pallas_call(functools.partial(correlate_kernel, with_counts=with_count...]
    squeeze x3 -> x0, local copies, waits for them, and re-layouts: 3.08 us -> none  [body(): spectra += [rest[j] for j in range(chunks - 1)]]
    concatenate x1 -> x2, other arithmetic: 0.94 us -> 3.86 us  [body(): sums = jnp.concatenate(sums, axis=0)]
  transfers between devices with their start and end apart: 5 -> 3, of which waited for: 2 -> 2; matrix products, arithmetic and copies ran while one was open for 14% -> 13% of each run, Pallas kernels for 29% -> 18%
where the time goes in v7:
time: 140 us
  Pallas kernels  51.1 us (36%)
  waiting for transfers between devices  28.9 us (21%)
  starting transfers between devices  16.9 us (12%)
  matrix products  14.8 us (11%)
  other arithmetic  14.2 us (10%)
  local copies, waits for them, and re-layouts  13.1 us (9%)
    pallas_call x2, Pallas kernels, correlate(): pl.pallas_call(functools.partial(correlate_kernel, with_counts=with_count...  51.1 us
    all_to_all x2, waiting for transfers between devices, body(): turned = lax.all_to_all(spectra_j, ('wide', 'tm'), 0, 0, tiled=True)  19.8 us
    all_to_all x2, starting transfers between devices, body(): turned = lax.all_to_all(spectra_j, ('wide', 'tm'), 0, 0, tiled=True)  11.1 us
    dot_general x2, matrix products, channelize(): lax.dot_general(rows, flattened, NT, preferred_element_type=jnp.float32)  10.4 us
    all_to_all x1, waiting for transfers between devices, body(): received = lax.all_to_all(send, ('wide', 'tm'), 0, 0, tiled=True)  9.14 us
    all_to_all x1, starting transfers between devices, body(): received = lax.all_to_all(send, ('wide', 'tm'), 0, 0, tiled=True)  5.84 us
    dot_general x1, matrix products, body(): lax.dot_general(stacked_in, delay, (((0,), (0,)), ((), ())), precision=la...  4.45 us
    concatenate x6, other arithmetic, unskew(): jnp.concatenate([forward[..., :1], lower[..., :FEEDS - 1]], axis=-1)  4.3 us
  transfers between devices with their start and end apart: 3, of which 2 were waited for; matrix products, arithmetic and copies ran while one was open for 13% of the time, Pallas kernels for 18%

profile of v7, /device:TPU:0, one launch (start us, length us, event | category | flops | bytes accessed | tf_op | source)
XLA Modules:
  0.0 139.5 jit_solution(13292756763417414043)
XLA Ops:
  0.0 5.2 %convolution_convert_fusion = bf16[512,1024]{1,0:T(8,128)(2,1)S(1)} fusion(bf16[512,2048]{1,0:T(8,128)(2,1)} %constant.49, bf16[1024,2048]{1,0:T(8,128)(2,1)} %bitcast.184), kind=kOutput, calls=%fused_computation.38 | convolution fusion | flops 2148007936 | bytes 7340032 | tf_op jit(solution)/shard_map/dot_general | solution.py:169
  5.2 1.3 squeeze_reshape.7
  6.5 7.3 %all-to-all-start.1 = ((bf16[32,8,16,128]{3,2,1,0:T(8,128)(2,1)}), bf16[32,8,16,128]{3,2,1,0:T(8,128)(2,1)S(1)}, u32[]{:S(2)}, u32[]{:S(2)}) async-start(bf16[32,8,16,128]{3,2,1,0:T(8,128)(2,1)} %squeeze_reshape.7), calls=%async_computation.1 | async-start | bytes 2097152 | tf_op jit(solution)/shard_map/all_to_all | solution.py:205
  13.8 5.2 %convolution_convert_fusion.1 = bf16[512,1024]{1,0:T(8,128)(2,1)S(1)} fusion(bf16[512,2048]{1,0:T(8,128)(2,1)} %constant.47, bf16[1024,2048]{1,0:T(8,128)(2,1)} %bitcast.185), kind=kOutput, calls=%fused_computation.39 | convolution fusion | flops 2148007936 | bytes 7340032 | tf_op jit(solution)/shard_map/dot_general | solution.py:169
  19.0 1.3 squeeze_reshape.6
  20.3 19.8 %all-to-all-done.1 = bf16[32,8,16,128]{3,2,1,0:T(8,128)(2,1)S(1)} async-done(((bf16[32,8,16,128]{3,2,1,0:T(8,128)(2,1)}), bf16[32,8,16,128]{3,2,1,0:T(8,128)(2,1)S(1)}, u32[]{:S(2)}, u32[]{:S(2)}) %all-to-all-start.1) | async-done | bytes 1048608 | tf_op jit(solution)/shard_map/all_to_all | solution.py:205
  40.0 3.8 %all-to-all-start = ((bf16[32,8,16,128]{3,2,1,0:T(8,128)(2,1)}), bf16[32,8,16,128]{3,2,1,0:T(8,128)(2,1)S(1)}, u32[]{:S(2)}, u32[]{:S(2)}) async-start(bf16[32,8,16,128]{3,2,1,0:T(8,128)(2,1)} %squeeze_reshape.6), calls=%async_computation | async-start | bytes 2097152 | tf_op jit(solution)/shard_map/all_to_all | solution.py:205
  44.3 1.4 %fusion.2 = (bf16[1024]{0:T(1024)(128)(2,1)S(1)}, bf16[1024]{0:T(1024)(128)(2,1)S(1)}) fusion(s32[1024]{0:T(1024)S(1)} %bitcast.142, bf16[1024]{0:T(1024)(128)(2,1)S(1)} %convert_element_type.41, s32[1024]{0:T(1024)S(1)} %copy-done.5), kind=kLoop, calls=%fused_computation.6 | loop fusion | flops 6289408 | bytes 14336 | tf_op jit(solution)/shard_map/reduce_sum | solution.py:185
  45.7 1.1 broadcast_select_fusion
  46.9 2.5 %compare_select_fusion = (bf16[8,1024,128]{2,1,0:T(8,128)(2,1)}, bf16[8,1024,128]{2,1,0:T(8,128)(2,1)}) fusion(s32[8,128]{1,0:T(8,128)S(1)} %multiply_add_fusion, s32[1024]{0:T(1024)S(1)} %bitcast.143, bf16[8,128]{1,0:T(8,128)(2,1)S(1)} %convert_bitcast_fusion, s32[1024]{0:T(1024)S(1)} %copy-done.5), kind=kLoop, calls=%fused_computation.4 | loop fusion | flops 4194304 | bytes 4208640 | tf_op jit(solution)/shard_map/jit(_where)/select_n | solution.py:182
  49.4 24.9 %shard_map.74 = f32[8,2,16,256]{3,2,1,0:T(8,128)} custom-call(bf16[8,4,8,16,128]{4,3,2,1,0:T(8,128)(2,1)} %bitcast.137, bf16[8,1024,128]{2,1,0:T(8,128)(2,1)} %get-tuple-element.50.refs_1_, bf16[8,1024,128]{2,1,0:T(8,128)(2,1)} %get-tuple-element.49.refs_2_, bf16[64,64]{1,0:T(8,128)(2,1)} %constant.43.clone.refs_3_), custom_call_target="tpu_custom_call" | custom-call | flops 3556769792 | bytes 5505024 | tf_op jit(solution)/shard_map/pallas_call | solution.py:128
  74.3 1.0 copy-done.2
  75.3 26.2 %shard_map.73 = (f32[8,2,16,256]{3,2,1,0:T(8,128)}, f32[16,256]{1,0:T(8,128)}) custom-call(bf16[8,4,8,16,128]{4,3,2,1,0:T(8,128)(2,1)} %bitcast.138, bf16[8,1024,128]{2,1,0:T(8,128)(2,1)} %get-tuple-element.50.refs_1_, bf16[8,1024,128]{2,1,0:T(8,128)(2,1)} %get-tuple-element.49.refs_2_, bf16[64,64]{1,0:T(8,128)(2,1)} %constant.43.clone.refs_3_, ...), custom_call_target="tpu_custom_call" | custom-call | flops 3556769792 | bytes 5505024 | tf_op jit(solution)/shard_map/pallas_call | solution.py:128
  101.5 2.0 %pad_maximum_fusion = (f32[16,2,1,256]{3,2,1,0:T(1,128)S(1)}, f32[16,2,1,256]{3,2,1,0:T(1,128)S(1)}, f32[16,2,1,256]{3,2,1,0:T(1,128)S(1)}, f32[16,2,1,256]{3,2,...) fusion(f32[8,2,16,256]{3,2,1,0:T(8,128)S(1)} %copy-done, ...), kind=kLoop, calls=%fused_computation.75 | loop fusion | flops 73728 | bytes 819200 | tf_op jit(solution)/shard_map/concatenate | solution.py:212
  103.9 1.9 %fusion.4 = (f32[16,2,1,256]{3,2,1,0:T(1,128)S(1)}, f32[16,2,1,256]{3,2,1,0:T(1,128)S(1)}, f32[16,2,1,256]{3,2,1,0:T(1,128)S(1)}, f32[16,2,1,256]{3,2,1,0:T(1,12...) fusion(f32[8,2,16,256]{3,2,1,0:T(8,128)} %get-tuple-element.7, ...), kind=kLoop, calls=%fused_computation.60 | loop fusion | flops 57344 | bytes 753664 | tf_op jit(solution)/shard_map/concatenate | solution.py:212
  105.8 0.3 rev.69
  106.2 0.3 rev.72
  107.3 0.3 rev.75
  107.7 0.3 rev.67
  111.1 0.3 copy.125
  111.5 1.2 copy.126
  112.7 5.8 %all-to-all-start.2 = ((f32[32,16,2,128]{3,2,1,0:T(2,128)}), f32[32,16,2,128]{3,2,1,0:T(2,128)S(1)}, u32[]{:S(2)}, u32[]{:S(2)}) async-start(f32[32,16,2,128]{3,2,1,0:T(2,128)} %copy.126), calls=%async_computation.2 | async-start | bytes 1048576 | tf_op jit(solution)/shard_map/all_to_all | solution.py:217
  118.5 0.7 fusion.21
  120.2 0.8 pad_maximum_fusion.1
  121.0 0.7 pad_maximum_fusion.2
  121.7 0.6 pad_maximum_fusion.3
  122.3 0.8 pad_maximum_fusion.4
  123.1 0.7 pad_maximum_fusion.5
  123.8 0.7 pad_maximum_fusion.6
  124.7 9.1 %all-to-all-done.2 = f32[32,16,2,128]{3,2,1,0:T(2,128)S(1)} async-done(((f32[32,16,2,128]{3,2,1,0:T(2,128)}), f32[32,16,2,128]{3,2,1,0:T(2,128)S(1)}, u32[]{:S(2)}, u32[]{:S(2)}) %all-to-all-start.2) | async-done | bytes 524320 | tf_op jit(solution)/shard_map/all_to_all | solution.py:217
  133.9 4.5 %convolution_multiply_fusion = f32[128,2,512]{2,0,1:T(8,128)S(1)} fusion(f32[1024,128,1]{1,0,2:T(8,128)S(1)} %bitcast.136, f32[2,512,1024]{2,1,0:T(8,128)} %constant.51, f32[128]{0:T(128)S(1)} %multiply_rsqrt_fusion), kind=kOutput, calls=%fused_computation.40 | convolution fusion | flops 805437440 | bytes 5243392 | tf_op jit(solution)/shard_map/dot_general | solution.py:225
  138.3 1.2 copy.128
  (102 shorter events, 6.0 us)
Async XLA Ops:
  6.5 33.5 %all-to-all-start.1 = ((bf16[32,8,16,128]{3,2,1,0:T(8,128)(2,1)}), bf16[32,8,16,128]{3,2,1,0:T(8,128)(2,1)S(1)}, u32[]{:S(2)}, u32[]{:S(2)}) async-start(bf16[32,8,16,128]{3,2,1,0:T(8,128)(2,1)} %squeeze_reshape.7), calls=%async_computation.1 | async-start | bytes 2097152 | tf_op jit(solution)/shard_map/all_to_all | solution.py:205
  19.0 24.9 %copy-start.5 = (s32[1024]{0:T(1024)S(1)}, s32[1024]{0:T(1024)}, u32[]{:S(2)}) copy-start(s32[1024]{0:T(1024)} %param.8) | copy-start | bytes 12292
  19.0 25.1 %copy-start.6 = (s32[1024]{0:T(1024)S(1)}, s32[1024]{0:T(1024)}, u32[]{:S(2)}) copy-start(s32[1024]{0:T(1024)} %param.9) | copy-start | bytes 12292
  40.0 9.4 %copy-start.1 = (bf16[32,8,16,128]{3,2,1,0:T(8,128)(2,1)}, bf16[32,8,16,128]{3,2,1,0:T(8,128)(2,1)S(1)}, u32[]{:S(2)}) copy-start(bf16[32,8,16,128]{3,2,1,0:T(8,128)(2,1)S(1)} %all-to-all-done.1) | copy-start | bytes 3145732
  40.0 34.3 %all-to-all-start = ((bf16[32,8,16,128]{3,2,1,0:T(8,128)(2,1)}), bf16[32,8,16,128]{3,2,1,0:T(8,128)(2,1)S(1)}, u32[]{:S(2)}, u32[]{:S(2)}) async-start(bf16[32,8,16,128]{3,2,1,0:T(8,128)(2,1)} %squeeze_reshape.6), calls=%async_computation | async-start | bytes 2097152 | tf_op jit(solution)/shard_map/all_to_all | solution.py:205
  74.3 1.0 copy-start.2
  75.3 26.2 %copy-start = (f32[8,2,16,256]{3,2,1,0:T(8,128)S(1)}, f32[8,2,16,256]{3,2,1,0:T(8,128)}, u32[]{:S(2)}) copy-start(f32[8,2,16,256]{3,2,1,0:T(8,128)} %shard_map.74) | copy-start | bytes 786436
  101.5 6.2 %copy-start.3 = (f32[16,256]{1,0:T(8,128)S(1)}, f32[16,256]{1,0:T(8,128)}, u32[]{:S(2)}) copy-start(f32[16,256]{1,0:T(8,128)} %get-tuple-element.8) | copy-start | bytes 49156
  101.5 8.8 %copy-start.4 = (f32[2]{0:T(128)S(1)}, f32[2]{0:T(128)}, u32[]{:S(2)}) copy-start(f32[2]{0:T(128)} %constant.44.clone) | copy-start | bytes 28
  112.7 21.2 %all-to-all-start.2 = ((f32[32,16,2,128]{3,2,1,0:T(2,128)}), f32[32,16,2,128]{3,2,1,0:T(2,128)S(1)}, u32[]{:S(2)}, u32[]{:S(2)}) async-start(f32[32,16,2,128]{3,2,1,0:T(2,128)} %copy.126), calls=%async_computation.2 | async-start | bytes 1048576 | tf_op jit(solution)/shard_map/all_to_all | solution.py:217

commit v8 on v7

--- a/solution.py
+++ b/solution.py
@@ -202,6 +202,8 @@
         spectra_j = spectra[j]
         if j >= 2:
             spectra_j, _ = lax.optimization_barrier((spectra_j, sums[j - 2]))
+        elif j == 1:
+            spectra_j, pt, ptr, fm, fmr = lax.optimization_barrier((spectra_j, pt, ptr, fm, fmr))
         turned = lax.all_to_all(spectra_j, ("wide", "tm"), 0, 0, tiled=True)
         blk = turned.reshape(wide_parts, tm_parts, chunk_channels, 2 * frames_here, inputs_here)
         if j == 0:

time: 140 us -> 138 us (0.986)
  waiting for transfers between devices: 28.9 us -> 22.9 us
  local copies, waits for them, and re-layouts: 13.1 us -> 15.8 us
    all_to_all x2, waiting for transfers between devices: 19.8 us -> 14.4 us  [body(): turned = lax.all_to_all(spectra_j, ('wide', 'tm'), 0, 0, tiled=True)]
  transfers between devices with their start and end apart: 3 -> 3, of which waited for: 2 -> 2; matrix products, arithmetic and copies ran while one was open for 13% -> 15% of each run, Pallas kernels for 18% -> 19%
where the time goes in v8:
time: 138 us; the launch traced here: 137 us
  Pallas kernels  51.2 us (37%)
  waiting for transfers between devices  22.9 us (17%)
  starting transfers between devices  16.8 us (12%)
  local copies, waits for them, and re-layouts  15.8 us (11%)
  other arithmetic  15 us (11%)
  matrix products  14.9 us (11%)
    pallas_call x2, Pallas kernels, correlate(): pl.pallas_call(functools.partial(correlate_kernel, with_counts=with_count...  51.2 us
    all_to_all x2, waiting for transfers between devices, body(): turned = lax.all_to_all(spectra_j, ('wide', 'tm'), 0, 0, tiled=True)  14.4 us
    all_to_all x2, starting transfers between devices, body(): turned = lax.all_to_all(spectra_j, ('wide', 'tm'), 0, 0, tiled=True)  11.1 us
    dot_general x2, matrix products, channelize(): lax.dot_general(rows, flattened, NT, preferred_element_type=jnp.float32)  10.4 us
    all_to_all x1, waiting for transfers between devices, body(): received = lax.all_to_all(send, ('wide', 'tm'), 0, 0, tiled=True)  8.56 us
    all_to_all x1, starting transfers between devices, body(): received = lax.all_to_all(send, ('wide', 'tm'), 0, 0, tiled=True)  5.68 us
    concatenate x2, other arithmetic, body(): sums = jnp.concatenate(sums, axis=0)  4.69 us
    dot_general x1, matrix products, body(): lax.dot_general(stacked_in, delay, (((0,), (0,)), ((), ())), precision=la...  4.55 us
  transfers between devices with their start and end apart: 3, of which 2 were waited for; matrix products, arithmetic and copies ran while one was open for 15% of the time, Pallas kernels for 19%

profile of v8, /device:TPU:0, one launch (start us, length us, event | category | flops | bytes accessed | tf_op | source)
XLA Modules:
  0.0 137.1 jit_solution(12718560233518530744)
XLA Ops:
  0.0 5.2 %convolution_convert_fusion.1 = bf16[512,1024]{1,0:T(8,128)(2,1)S(1)} fusion(bf16[512,2048]{1,0:T(8,128)(2,1)} %constant.47, bf16[1024,2048]{1,0:T(8,128)(2,1)} %bitcast.184), kind=kOutput, calls=%fused_computation.39 | convolution fusion | flops 2148007936 | bytes 7340032 | tf_op jit(solution)/shard_map/dot_general | solution.py:169
  5.2 1.3 squeeze_reshape.6
  6.5 7.3 %all-to-all-start = ((bf16[32,8,16,128]{3,2,1,0:T(8,128)(2,1)}), bf16[32,8,16,128]{3,2,1,0:T(8,128)(2,1)S(1)}, u32[]{:S(2)}, u32[]{:S(2)}) async-start(bf16[32,8,16,128]{3,2,1,0:T(8,128)(2,1)} %squeeze_reshape.6), calls=%async_computation | async-start | bytes 2097152 | tf_op jit(solution)/shard_map/all_to_all | solution.py:207
  14.0 5.2 %convolution_convert_fusion = bf16[512,1024]{1,0:T(8,128)(2,1)S(1)} fusion(bf16[512,2048]{1,0:T(8,128)(2,1)} %constant.49, bf16[1024,2048]{1,0:T(8,128)(2,1)} %bitcast.185), kind=kOutput, calls=%fused_computation.38 | convolution fusion | flops 2148007936 | bytes 7340032 | tf_op jit(solution)/shard_map/dot_general | solution.py:169
  19.2 1.3 squeeze_reshape.7
  20.5 1.4 %fusion.2 = (bf16[1024]{0:T(1024)(128)(2,1)S(1)}, bf16[1024]{0:T(1024)(128)(2,1)S(1)}) fusion(s32[1024]{0:T(1024)S(1)} %bitcast.142, bf16[1024]{0:T(1024)(128)(2,1)S(1)} %convert_element_type.41, s32[1024]{0:T(1024)S(1)} %copy-done.4), kind=kLoop, calls=%fused_computation.6 | loop fusion | flops 6289408 | bytes 14336 | tf_op jit(solution)/shard_map/reduce_sum | solution.py:185
  22.0 1.1 broadcast_select_fusion
  23.1 2.6 %compare_select_fusion = (bf16[8,1024,128]{2,1,0:T(8,128)(2,1)}, bf16[8,1024,128]{2,1,0:T(8,128)(2,1)}) fusion(s32[8,128]{1,0:T(8,128)S(1)} %multiply_add_fusion, s32[1024]{0:T(1024)S(1)} %bitcast.143, bf16[8,128]{1,0:T(8,128)(2,1)S(1)} %convert_bitcast_fusion, s32[1024]{0:T(1024)S(1)} %copy-done.4), kind=kLoop, calls=%fused_computation.4 | loop fusion | flops 4194304 | bytes 4208640 | tf_op jit(solution)/shard_map/jit(_where)/select_n | solution.py:182
  25.7 14.4 %all-to-all-done = bf16[32,8,16,128]{3,2,1,0:T(8,128)(2,1)S(1)} async-done(((bf16[32,8,16,128]{3,2,1,0:T(8,128)(2,1)}), bf16[32,8,16,128]{3,2,1,0:T(8,128)(2,1)S(1)}, u32[]{:S(2)}, u32[]{:S(2)}) %all-to-all-start) | async-done | bytes 1048608 | tf_op jit(solution)/shard_map/all_to_all | solution.py:207
  40.0 3.8 %all-to-all-start.1 = ((bf16[32,8,16,128]{3,2,1,0:T(8,128)(2,1)}), bf16[32,8,16,128]{3,2,1,0:T(8,128)(2,1)S(1)}, u32[]{:S(2)}, u32[]{:S(2)}) async-start(bf16[32,8,16,128]{3,2,1,0:T(8,128)(2,1)} %squeeze_reshape.7), calls=%async_computation.1 | async-start | bytes 2097152 | tf_op jit(solution)/shard_map/all_to_all | solution.py:207
  44.1 26.2 %shard_map.73 = (f32[8,2,16,256]{3,2,1,0:T(8,128)}, f32[16,256]{1,0:T(8,128)}) custom-call(bf16[8,4,8,16,128]{4,3,2,1,0:T(8,128)(2,1)} %bitcast.137, bf16[8,1024,128]{2,1,0:T(8,128)(2,1)} %get-tuple-element.12.refs_1_, bf16[8,1024,128]{2,1,0:T(8,128)(2,1)} %get-tuple-element.13.refs_2_, bf16[64,64]{1,0:T(8,128)(2,1)} %constant.43.clone.refs_3_, ...), custom_call_target="tpu_custom_call" | custom-call | flops 3556769792 | bytes 5505024 | tf_op jit(solution)/shard_map/pallas_call | solution.py:128
  70.3 0.9 fusion.22
  71.2 1.0 fusion.20
  72.2 1.0 copy-done.2
  73.2 25.0 %shard_map.74 = f32[8,2,16,256]{3,2,1,0:T(8,128)} custom-call(bf16[8,4,8,16,128]{4,3,2,1,0:T(8,128)(2,1)} %bitcast.138, bf16[8,1024,128]{2,1,0:T(8,128)(2,1)} %get-tuple-element.12.refs_1_, bf16[8,1024,128]{2,1,0:T(8,128)(2,1)} %get-tuple-element.13.refs_2_, bf16[64,64]{1,0:T(8,128)(2,1)} %constant.43.clone.refs_3_), custom_call_target="tpu_custom_call" | custom-call | flops 3556769792 | bytes 5505024 | tf_op jit(solution)/shard_map/pallas_call | solution.py:128
  98.1 2.6 %pad_maximum_fusion = (f32[16,2,1,256]{3,2,1,0:T(1,128)S(1)}, f32[16,2,1,256]{3,2,1,0:T(1,128)S(1)}, f32[16,2,1,256]{3,2,1,0:T(1,128)S(1)}, f32[16,2,1,256]{3,2,...) fusion(f32[8,2,16,256]{3,2,1,0:T(8,128)} %shard_map.74, ...), kind=kLoop, calls=%fused_computation.75 | loop fusion | flops 73728 | bytes 819200 | tf_op jit(solution)/shard_map/concatenate | solution.py:214
  100.8 0.3 rev.68
  101.2 0.3 rev.69
  101.5 2.1 %fusion.4 = (f32[16,2,1,256]{3,2,1,0:T(1,128)S(1)}, f32[16,2,1,256]{3,2,1,0:T(1,128)S(1)}, f32[16,2,1,256]{3,2,1,0:T(1,128)S(1)}, f32[16,2,1,256]{3,2,1,0:T(1,12...) fusion(f32[8,2,16,256]{3,2,1,0:T(8,128)S(1)} %copy-done, ...), kind=kLoop, calls=%fused_computation.60 | loop fusion | flops 57344 | bytes 753664 | tf_op jit(solution)/shard_map/concatenate | solution.py:214
  108.5 0.3 copy.125
  108.9 1.2 copy.126
  110.1 5.7 %all-to-all-start.2 = ((f32[32,16,2,128]{3,2,1,0:T(2,128)}), f32[32,16,2,128]{3,2,1,0:T(2,128)S(1)}, u32[]{:S(2)}, u32[]{:S(2)}) async-start(f32[32,16,2,128]{3,2,1,0:T(2,128)} %copy.126), calls=%async_computation.2 | async-start | bytes 1048576 | tf_op jit(solution)/shard_map/all_to_all | solution.py:219
  115.8 1.5 %fusion.21 = (f32[1,1]{1,0:T(1,128)}, f32[1,1]{1,0:T(1,128)}, f32[1,1]{1,0:T(1,128)}, f32[1,1]{1,0:T(1,128)}, f32[1,1]{1,0:T(1,128)}, /*index=5*/f32[1,1]{1,0:T(1,128)}) fusion(f32[16,256]{1,0:T(8,128)} %get-tuple-element.14), kind=kLoop, calls=%fused_computation.120 | loop fusion | bytes 48 | tf_op jit(solution)/shard_map/slice | solution.py:146
  118.3 0.7 pad_maximum_fusion.1
  119.0 0.6 pad_maximum_fusion.2
  119.7 0.8 pad_maximum_fusion.3
  120.4 0.7 pad_maximum_fusion.4
  121.1 0.7 pad_maximum_fusion.5
  121.8 0.7 pad_maximum_fusion.6
  122.8 8.6 %all-to-all-done.2 = f32[32,16,2,128]{3,2,1,0:T(2,128)S(1)} async-done(((f32[32,16,2,128]{3,2,1,0:T(2,128)}), f32[32,16,2,128]{3,2,1,0:T(2,128)S(1)}, u32[]{:S(2)}, u32[]{:S(2)}) %all-to-all-start.2) | async-done | bytes 524320 | tf_op jit(solution)/shard_map/all_to_all | solution.py:219
  131.3 4.5 %convolution_multiply_fusion = f32[128,2,512]{2,0,1:T(8,128)S(1)} fusion(f32[1024,128,1]{1,0,2:T(8,128)S(1)} %bitcast.136, f32[2,512,1024]{2,1,0:T(8,128)} %constant.51, f32[128]{0:T(128)S(1)} %multiply_rsqrt_fusion), kind=kOutput, calls=%fused_computation.40 | convolution fusion | flops 805437440 | bytes 5243392 | tf_op jit(solution)/shard_map/dot_general | solution.py:227
  135.9 1.2 copy.128
  (100 shorter events, 6.6 us)
Async XLA Ops:
  5.2 8.6 %copy-start.4 = (s32[1024]{0:T(1024)S(1)}, s32[1024]{0:T(1024)}, u32[]{:S(2)}) copy-start(s32[1024]{0:T(1024)} %param.8) | copy-start | bytes 12292
  5.2 8.8 %copy-start.5 = (s32[1024]{0:T(1024)S(1)}, s32[1024]{0:T(1024)}, u32[]{:S(2)}) copy-start(s32[1024]{0:T(1024)} %param.9) | copy-start | bytes 12292
  6.5 33.5 %all-to-all-start = ((bf16[32,8,16,128]{3,2,1,0:T(8,128)(2,1)}), bf16[32,8,16,128]{3,2,1,0:T(8,128)(2,1)S(1)}, u32[]{:S(2)}, u32[]{:S(2)}) async-start(bf16[32,8,16,128]{3,2,1,0:T(8,128)(2,1)} %squeeze_reshape.6), calls=%async_computation | async-start | bytes 2097152 | tf_op jit(solution)/shard_map/all_to_all | solution.py:207
  40.0 4.0 %copy-start.1 = (bf16[32,8,16,128]{3,2,1,0:T(8,128)(2,1)}, bf16[32,8,16,128]{3,2,1,0:T(8,128)(2,1)S(1)}, u32[]{:S(2)}) copy-start(bf16[32,8,16,128]{3,2,1,0:T(8,128)(2,1)S(1)} %all-to-all-done) | copy-start | bytes 3145732
  40.0 32.1 %all-to-all-start.1 = ((bf16[32,8,16,128]{3,2,1,0:T(8,128)(2,1)}), bf16[32,8,16,128]{3,2,1,0:T(8,128)(2,1)S(1)}, u32[]{:S(2)}, u32[]{:S(2)}) async-start(bf16[32,8,16,128]{3,2,1,0:T(8,128)(2,1)} %squeeze_reshape.7), calls=%async_computation.1 | async-start | bytes 2097152 | tf_op jit(solution)/shard_map/all_to_all | solution.py:207
  72.2 1.0 copy-start.2
  73.2 25.0 %copy-start = (f32[8,2,16,256]{3,2,1,0:T(8,128)S(1)}, f32[8,2,16,256]{3,2,1,0:T(8,128)}, u32[]{:S(2)}) copy-start(f32[8,2,16,256]{3,2,1,0:T(8,128)} %get-tuple-element.10) | copy-start | bytes 786436
  98.1 9.5 %copy-start.3 = (f32[2]{0:T(128)S(1)}, f32[2]{0:T(128)}, u32[]{:S(2)}) copy-start(f32[2]{0:T(128)} %constant.44.clone) | copy-start | bytes 28
  110.1 21.2 %all-to-all-start.2 = ((f32[32,16,2,128]{3,2,1,0:T(2,128)}), f32[32,16,2,128]{3,2,1,0:T(2,128)S(1)}, u32[]{:S(2)}, u32[]{:S(2)}) async-start(f32[32,16,2,128]{3,2,1,0:T(2,128)} %copy.126), calls=%async_computation.2 | async-start | bytes 1048576 | tf_op jit(solution)/shard_map/all_to_all | solution.py:219

commit v9 on v8

--- a/solution.py
+++ b/solution.py
@@ -136,17 +136,17 @@
 
 
 def unskew(sums, sign):
-    pieces = {}
-    for a in range(CYL):
-        for b in range(a, CYL):
-            forward = jnp.flip(sums[..., a * CYL + b, :], axis=-1)
-            pieces[(a, b)] = forward
-            if a < b:
-                lower = sums[..., b * CYL + a, :]
-                backward = jnp.concatenate([forward[..., :1], lower[..., : FEEDS - 1]], axis=-1)
-                pieces[(b, a)] = backward * sign
-    stacked = jnp.stack([pieces[(a, b)] for a in range(CYL) for b in range(CYL)], axis=-2)
-    return stacked * pair_keep().reshape(CYL * CYL, FEEDS)
+    lead = sums.shape[:-2]
+    grid = sums.reshape(lead + (CYL, CYL, FEEDS))
+    forward = jnp.flip(grid, axis=-1)
+    shifted = jnp.roll(grid, 1, axis=-1)
+    first_of_pair = jnp.swapaxes(forward, -3, -2)[..., :1]
+    k_at = lax.broadcasted_iota(jnp.int32, (CYL, CYL, FEEDS), 2)
+    a_at = lax.broadcasted_iota(jnp.int32, (CYL, CYL, FEEDS), 0)
+    b_at = lax.broadcasted_iota(jnp.int32, (CYL, CYL, FEEDS), 1)
+    backward = jnp.where(k_at == 0, first_of_pair, shifted) * sign
+    joined = jnp.where(a_at <= b_at, forward, backward) * pair_keep()
+    return joined.reshape(lead + (CYL * CYL, FEEDS))
 
 
 def body(samples, feed_input_wiring, input_flags):
@@ -212,7 +212,7 @@
         else:
             sums.append(correlate(blk, pt, ptr, rm)[0])
     sums = jnp.concatenate(sums, axis=0)
-    conj_sign = jnp.array([1.0, -1.0], jnp.float32)[None, :, None]
+    conj_sign = jnp.array([1.0, -1.0], jnp.float32)[None, :, None, None, None]
     vis = unskew(sums, conj_sign)
     local_baselines = NBASE // devices
     send = vis.reshape(local_channels, 2, devices, local_baselines).transpose(2, 0, 1, 3)

time: 138 us -> 129 us (0.935)
  other arithmetic: 15 us -> 6.8 us
  local copies, waits for them, and re-layouts: 15.8 us -> 8.73 us
  waiting for transfers between devices: 22.9 us -> 29.8 us
    all_to_all x1, waiting for transfers between devices: 8.56 us -> 15.4 us  [body(): received = lax.all_to_all(send, ('wide', 'tm'), 0, 0, tiled=True)]
    concatenate x6 -> x0, other arithmetic: 4.25 us -> none  [unskew(): jnp.concatenate([forward[..., :1], lower[..., :FEEDS - 1]], axis=-1)]
    slice x15 -> x5, local copies, waits for them, and re-layouts: 4.41 us -> 0.44 us  [the longest x2 0.27 us: unskew(): shifted = jnp.roll(grid, 1, axis=-1)]
    concatenate x2 -> x1, other arithmetic: 4.69 us -> 0.99 us  [body(): sums = jnp.concatenate(sums, axis=0)]
    rev x20 -> x2, local copies, waits for them, and re-layouts: 3.65 us -> 0.89 us  [unskew(): forward = jnp.flip(grid, axis=-1)]
  transfers between devices with their start and end apart: 3 -> 3, of which waited for: 2 -> 2; matrix products, arithmetic and copies ran while one was open for 15% -> 9% of each run, Pallas kernels for 19% -> 20%
where the time goes in v9:
time: 129 us; the launch traced here: 128 us
  Pallas kernels  51.1 us (40%)
  waiting for transfers between devices  29.8 us (23%)
  starting transfers between devices  16.7 us (13%)
  matrix products  14.9 us (12%)
  local copies, waits for them, and re-layouts  8.73 us (7%)
  other arithmetic  6.8 us (5%)
    pallas_call x2, Pallas kernels, correlate(): pl.pallas_call(functools.partial(correlate_kernel, with_counts=with_count...  51.1 us
    all_to_all x1, waiting for transfers between devices, body(): received = lax.all_to_all(send, ('wide', 'tm'), 0, 0, tiled=True)  15.4 us
    all_to_all x2, waiting for transfers between devices, body(): turned = lax.all_to_all(spectra_j, ('wide', 'tm'), 0, 0, tiled=True)  14.4 us
    all_to_all x2, starting transfers between devices, body(): turned = lax.all_to_all(spectra_j, ('wide', 'tm'), 0, 0, tiled=True)  11.1 us
    dot_general x2, matrix products, channelize(): lax.dot_general(rows, flattened, NT, preferred_element_type=jnp.float32)  10.4 us
    all_to_all x1, starting transfers between devices, body(): received = lax.all_to_all(send, ('wide', 'tm'), 0, 0, tiled=True)  5.65 us
    dot_general x1, matrix products, body(): lax.dot_general(stacked_in, delay, (((0,), (0,)), ((), ())), precision=la...  4.54 us
  transfers between devices with their start and end apart: 3, of which 2 were waited for; matrix products, arithmetic and copies ran while one was open for 9% of the time, Pallas kernels for 20%

profile of v9, /device:TPU:0, one launch (start us, length us, event | category | flops | bytes accessed | tf_op | source)
XLA Modules:
  0.0 128.4 jit_solution(8074333040943845397)
XLA Ops:
  0.0 5.2 %convolution_convert_fusion.1 = bf16[512,1024]{1,0:T(8,128)(2,1)S(1)} fusion(bf16[512,2048]{1,0:T(8,128)(2,1)} %constant.47, bf16[1024,2048]{1,0:T(8,128)(2,1)} %bitcast.43), kind=kOutput, calls=%fused_computation.9 | convolution fusion | flops 2148007936 | bytes 7340032 | tf_op jit(solution)/shard_map/dot_general | solution.py:169
  5.2 1.3 squeeze_reshape.6
  6.5 7.3 %all-to-all-start = ((bf16[32,8,16,128]{3,2,1,0:T(8,128)(2,1)}), bf16[32,8,16,128]{3,2,1,0:T(8,128)(2,1)S(1)}, u32[]{:S(2)}, u32[]{:S(2)}) async-start(bf16[32,8,16,128]{3,2,1,0:T(8,128)(2,1)} %squeeze_reshape.6), calls=%async_computation | async-start | bytes 2097152 | tf_op jit(solution)/shard_map/all_to_all | solution.py:207
  13.8 5.2 %convolution_convert_fusion = bf16[512,1024]{1,0:T(8,128)(2,1)S(1)} fusion(bf16[512,2048]{1,0:T(8,128)(2,1)} %constant.49, bf16[1024,2048]{1,0:T(8,128)(2,1)} %bitcast.44), kind=kOutput, calls=%fused_computation.8 | convolution fusion | flops 2148007936 | bytes 7340032 | tf_op jit(solution)/shard_map/dot_general | solution.py:169
  19.0 1.3 squeeze_reshape.7
  20.3 0.2 rev.12
  20.5 1.4 %fusion.2 = (bf16[1024]{0:T(1024)(128)(2,1)S(1)}, bf16[1024]{0:T(1024)(128)(2,1)S(1)}) fusion(s32[1024]{0:T(1024)S(1)} %bitcast.38, bf16[1024]{0:T(1024)(128)(2,1)S(1)} %convert_element_type.35, s32[1024]{0:T(1024)S(1)} %copy-done.3), kind=kLoop, calls=%fused_computation.6 | loop fusion | flops 6289408 | bytes 14336 | tf_op jit(solution)/shard_map/reduce_sum | solution.py:185
  21.9 1.1 broadcast_select_fusion
  23.1 2.5 %compare_select_fusion = (bf16[8,1024,128]{2,1,0:T(8,128)(2,1)}, bf16[8,1024,128]{2,1,0:T(8,128)(2,1)}) fusion(s32[8,128]{1,0:T(8,128)S(1)} %multiply_add_fusion, s32[1024]{0:T(1024)S(1)} %bitcast.39, bf16[8,128]{1,0:T(8,128)(2,1)S(1)} %convert_bitcast_fusion, s32[1024]{0:T(1024)S(1)} %copy-done.3), kind=kLoop, calls=%fused_computation.4 | loop fusion | flops 4194304 | bytes 4208640 | tf_op jit(solution)/shard_map/jit(_where)/select_n | solution.py:182
  25.6 14.4 %all-to-all-done = bf16[32,8,16,128]{3,2,1,0:T(8,128)(2,1)S(1)} async-done(((bf16[32,8,16,128]{3,2,1,0:T(8,128)(2,1)}), bf16[32,8,16,128]{3,2,1,0:T(8,128)(2,1)S(1)}, u32[]{:S(2)}, u32[]{:S(2)}) %all-to-all-start) | async-done | bytes 1048608 | tf_op jit(solution)/shard_map/all_to_all | solution.py:207
  40.0 3.8 %all-to-all-start.1 = ((bf16[32,8,16,128]{3,2,1,0:T(8,128)(2,1)}), bf16[32,8,16,128]{3,2,1,0:T(8,128)(2,1)S(1)}, u32[]{:S(2)}, u32[]{:S(2)}) async-start(bf16[32,8,16,128]{3,2,1,0:T(8,128)(2,1)} %squeeze_reshape.7), calls=%async_computation.1 | async-start | bytes 2097152 | tf_op jit(solution)/shard_map/all_to_all | solution.py:207
  43.9 26.2 %shard_map.73 = (f32[8,2,16,256]{3,2,1,0:T(8,128)}, f32[16,256]{1,0:T(8,128)}) custom-call(bf16[8,4,8,16,128]{4,3,2,1,0:T(8,128)(2,1)} %bitcast.33, bf16[8,1024,128]{2,1,0:T(8,128)(2,1)} %get-tuple-element.12.refs_1_, bf16[8,1024,128]{2,1,0:T(8,128)(2,1)} %get-tuple-element.13.refs_2_, bf16[64,64]{1,0:T(8,128)(2,1)} %constant.43.clone.refs_3_, ...), custom_call_target="tpu_custom_call" | custom-call | flops 3556769792 | bytes 5505024 | tf_op jit(solution)/shard_map/pallas_call | solution.py:128
  70.1 1.0 copy-done.1
  71.0 24.9 %shard_map.74 = f32[8,2,16,256]{3,2,1,0:T(8,128)} custom-call(bf16[8,4,8,16,128]{4,3,2,1,0:T(8,128)(2,1)} %bitcast.34, bf16[8,1024,128]{2,1,0:T(8,128)(2,1)} %get-tuple-element.12.refs_1_, bf16[8,1024,128]{2,1,0:T(8,128)(2,1)} %get-tuple-element.13.refs_2_, bf16[64,64]{1,0:T(8,128)(2,1)} %constant.43.clone.refs_3_), custom_call_target="tpu_custom_call" | custom-call | flops 3556769792 | bytes 5505024 | tf_op jit(solution)/shard_map/pallas_call | solution.py:128
  96.0 1.0 pad_maximum_fusion
  97.0 0.1 reshape.85
  97.1 0.7 rev.13
  97.8 0.2 slice.45
  98.1 0.2 rev.14
  98.3 0.1 slice.48
  98.3 0.1 copy.42
  98.5 0.1 slice.44
  98.5 0.9 copy.45
  99.4 0.1 fusion.9
  99.5 0.5 fusion.6
  100.0 0.2 reshape_reshape.6
  100.2 1.2 copy.40
  101.4 5.6 %all-to-all-start.2 = ((f32[32,16,2,128]{3,2,1,0:T(2,128)}), f32[32,16,2,128]{3,2,1,0:T(2,128)S(1)}, u32[]{:S(2)}, u32[]{:S(2)}) async-start(f32[32,16,2,128]{3,2,1,0:T(2,128)} %copy.40), calls=%async_computation.2 | async-start | bytes 1048576 | tf_op jit(solution)/shard_map/all_to_all | solution.py:219
  107.1 0.1 multiply_rsqrt_fusion
  107.2 15.4 %all-to-all-done.2 = f32[32,16,2,128]{3,2,1,0:T(2,128)S(1)} async-done(((f32[32,16,2,128]{3,2,1,0:T(2,128)}), f32[32,16,2,128]{3,2,1,0:T(2,128)S(1)}, u32[]{:S(2)}, u32[]{:S(2)}) %all-to-all-start.2) | async-done | bytes 524320 | tf_op jit(solution)/shard_map/all_to_all | solution.py:219
  122.6 4.5 %convolution_multiply_fusion = f32[128,2,512]{2,0,1:T(8,128)S(1)} fusion(f32[1024,128,1]{1,0,2:T(8,128)S(1)} %bitcast.32, f32[2,512,1024]{2,1,0:T(8,128)} %constant.51, f32[128]{0:T(128)S(1)} %multiply_rsqrt_fusion), kind=kOutput, calls=%fused_computation.10 | convolution fusion | flops 805437440 | bytes 5243392 | tf_op jit(solution)/shard_map/dot_general | solution.py:227
  127.2 1.2 copy.43
  (26 shorter events, 0.1 us)
Async XLA Ops:
  6.5 33.5 %all-to-all-start = ((bf16[32,8,16,128]{3,2,1,0:T(8,128)(2,1)}), bf16[32,8,16,128]{3,2,1,0:T(8,128)(2,1)S(1)}, u32[]{:S(2)}, u32[]{:S(2)}) async-start(bf16[32,8,16,128]{3,2,1,0:T(8,128)(2,1)} %squeeze_reshape.6), calls=%async_computation | async-start | bytes 2097152 | tf_op jit(solution)/shard_map/all_to_all | solution.py:207
  19.0 1.3 %copy-start.3 = (s32[1024]{0:T(1024)S(1)}, s32[1024]{0:T(1024)}, u32[]{:S(2)}) copy-start(s32[1024]{0:T(1024)} %param.8) | copy-start | bytes 12292
  19.0 1.5 %copy-start.4 = (s32[1024]{0:T(1024)S(1)}, s32[1024]{0:T(1024)}, u32[]{:S(2)}) copy-start(s32[1024]{0:T(1024)} %param.9) | copy-start | bytes 12292
  40.0 3.9 %copy-start = (bf16[32,8,16,128]{3,2,1,0:T(8,128)(2,1)}, bf16[32,8,16,128]{3,2,1,0:T(8,128)(2,1)S(1)}, u32[]{:S(2)}) copy-start(bf16[32,8,16,128]{3,2,1,0:T(8,128)(2,1)S(1)} %all-to-all-done) | copy-start | bytes 3145732
  40.0 30.1 %all-to-all-start.1 = ((bf16[32,8,16,128]{3,2,1,0:T(8,128)(2,1)}), bf16[32,8,16,128]{3,2,1,0:T(8,128)(2,1)S(1)}, u32[]{:S(2)}, u32[]{:S(2)}) async-start(bf16[32,8,16,128]{3,2,1,0:T(8,128)(2,1)} %squeeze_reshape.7), calls=%async_computation.1 | async-start | bytes 2097152 | tf_op jit(solution)/shard_map/all_to_all | solution.py:207
  70.1 1.0 copy-start.1
  71.0 24.9 %copy-start.2 = (f32[8,2,16,256]{3,2,1,0:T(8,128)S(1)}, f32[8,2,16,256]{3,2,1,0:T(8,128)}, u32[]{:S(2)}) copy-start(f32[8,2,16,256]{3,2,1,0:T(8,128)} %get-tuple-element.10) | copy-start | bytes 786436
  96.0 2.1 %copy-start.5 = (f32[16,256]{1,0:T(8,128)S(1)}, f32[16,256]{1,0:T(8,128)}, u32[]{:S(2)}) copy-start(f32[16,256]{1,0:T(8,128)} %get-tuple-element.14) | copy-start | bytes 49156
  97.0 2.5 %copy-start.6 = (f32[2]{0:T(128)S(1)}, f32[2]{0:T(128)}, u32[]{:S(2)}) copy-start(f32[2]{0:T(128)} %constant.44.clone) | copy-start | bytes 28
  101.4 21.2 %all-to-all-start.2 = ((f32[32,16,2,128]{3,2,1,0:T(2,128)}), f32[32,16,2,128]{3,2,1,0:T(2,128)S(1)}, u32[]{:S(2)}, u32[]{:S(2)}) async-start(f32[32,16,2,128]{3,2,1,0:T(2,128)} %copy.40), calls=%async_computation.2 | async-start | bytes 1048576 | tf_op jit(solution)/shard_map/all_to_all | solution.py:219

commit v10 on v9

--- a/solution.py
+++ b/solution.py
@@ -197,7 +197,15 @@
         rm[partner, r] = -1.0 if part_at[r] == 0 else 1.0
     rm = jnp.asarray(rm, dtype=jnp.bfloat16)
 
+    local_baselines = NBASE // devices
+    conj_sign = jnp.array([1.0, -1.0], jnp.float32)[None, :, None, None, None]
+
+    def send_of(chunk_sums):
+        vis = unskew(chunk_sums, conj_sign)
+        return vis.reshape(chunk_channels, 2, devices, local_baselines).transpose(2, 0, 1, 3)
+
     sums = []
+    received = []
     for j in range(chunks):
         spectra_j = spectra[j]
         if j >= 2:
@@ -206,18 +214,16 @@
             spectra_j, pt, ptr, fm, fmr = lax.optimization_barrier((spectra_j, pt, ptr, fm, fmr))
         turned = lax.all_to_all(spectra_j, ("wide", "tm"), 0, 0, tiled=True)
         blk = turned.reshape(wide_parts, tm_parts, chunk_channels, 2 * frames_here, inputs_here)
+        if j >= 1:
+            blk, send_prev = lax.optimization_barrier((blk, send_of(sums[j - 1])))
+            received.append(lax.all_to_all(send_prev, ("wide", "tm"), 0, 0, tiled=True))
         if j == 0:
             first, count_sums = correlate(blk, pt, ptr, rm, fm, fmr)
             sums.append(first)
         else:
             sums.append(correlate(blk, pt, ptr, rm)[0])
-    sums = jnp.concatenate(sums, axis=0)
-    conj_sign = jnp.array([1.0, -1.0], jnp.float32)[None, :, None, None, None]
-    vis = unskew(sums, conj_sign)
-    local_baselines = NBASE // devices
-    send = vis.reshape(local_channels, 2, devices, local_baselines).transpose(2, 0, 1, 3)
-    received = lax.all_to_all(send, ("wide", "tm"), 0, 0, tiled=True)
-    stacked_in = received.reshape(CH * 2, local_baselines)
+    received.append(lax.all_to_all(send_of(sums[-1]), ("wide", "tm"), 0, 0, tiled=True))
+    stacked_in = jnp.stack(received, axis=1).reshape(CH * 2, local_baselines)
     device_position = lax.axis_index("wide") * tm_parts + lax.axis_index("tm")
     global_stack_counts = unskew(count_sums, 1.0).reshape(NBASE)
     local_stack_counts = lax.dynamic_slice_in_dim(

time: 129 us -> 132 us (1.023)
  starting transfers between devices: 16.7 us -> 22.6 us
  waiting for transfers between devices: 29.8 us -> 24.9 us
  local copies, waits for them, and re-layouts: 8.73 us -> 11.6 us
    all_to_all x1 -> x2, starting transfers between devices: 5.65 us -> 11.7 us  [the longest x1 6.01 us: body(): received.append(lax.all_to_all(send_prev, ('wide', 'tm'), 0, 0, tiled=True))]
    all_to_all x1 -> x2, waiting for transfers between devices: 15.4 us -> 10.5 us  [the longest x1 10.5 us: body(): lax.all_to_all(send_of(sums[-1]), ('wide', 'tm'), 0, 0, tiled=True)]
    reshape x2 -> x3, local copies, waits for them, and re-layouts: 0.16 us -> 2.78 us  [unskew(): grid = sums.reshape(lead + (CYL, CYL, FEEDS))]
  transfers between devices with their start and end apart: 3 -> 4, of which waited for: 2 -> 2; matrix products, arithmetic and copies ran while one was open for 9% -> 14% of each run, Pallas kernels for 20% -> 39%
where the time goes in v10:
time: 132 us
  Pallas kernels  51.1 us (39%)
  waiting for transfers between devices  24.9 us (19%)
  starting transfers between devices  22.6 us (17%)
  matrix products  14.9 us (11%)
  local copies, waits for them, and re-layouts  11.6 us (9%)
  other arithmetic  6.17 us (5%)
    pallas_call x2, Pallas kernels, correlate(): pl.pallas_call(functools.partial(correlate_kernel, with_counts=with_count...  51.1 us
    all_to_all x2, waiting for transfers between devices, body(): turned = lax.all_to_all(spectra_j, ('wide', 'tm'), 0, 0, tiled=True)  14.4 us
    all_to_all x2, starting transfers between devices, body(): turned = lax.all_to_all(spectra_j, ('wide', 'tm'), 0, 0, tiled=True)  10.9 us
    all_to_all x1, waiting for transfers between devices, body(): lax.all_to_all(send_of(sums[-1]), ('wide', 'tm'), 0, 0, tiled=True)  10.5 us
    dot_general x2, matrix products, channelize(): lax.dot_general(rows, flattened, NT, preferred_element_type=jnp.float32)  10.4 us
    all_to_all x1, starting transfers between devices, body(): received.append(lax.all_to_all(send_prev, ('wide', 'tm'), 0, 0, tiled=True))  6.01 us
    all_to_all x1, starting transfers between devices, body(): lax.all_to_all(send_of(sums[-1]), ('wide', 'tm'), 0, 0, tiled=True)  5.67 us
    dot_general x1, matrix products, body(): lax.dot_general(stacked_in, delay, (((0,), (0,)), ((), ())), precision=la...  4.55 us
  transfers between devices with their start and end apart: 4, of which 2 were waited for; matrix products, arithmetic and copies ran while one was open for 14% of the time, Pallas kernels for 39%

profile of v10, /device:TPU:0, one launch (start us, length us, event | category | flops | bytes accessed | tf_op | source)
XLA Modules:
  0.0 131.6 jit_solution(6213587259041534957)
XLA Ops:
  0.0 5.2 %convolution_convert_fusion = bf16[512,1024]{1,0:T(8,128)(2,1)S(1)} fusion(bf16[512,2048]{1,0:T(8,128)(2,1)} %constant.49, bf16[1024,2048]{1,0:T(8,128)(2,1)} %bitcast.58), kind=kOutput, calls=%fused_computation.8 | convolution fusion | flops 2148007936 | bytes 7340032 | tf_op jit(solution)/shard_map/dot_general | solution.py:169
  5.2 1.3 squeeze_reshape.7
  6.5 7.3 %all-to-all-start.1 = ((bf16[32,8,16,128]{3,2,1,0:T(8,128)(2,1)}), bf16[32,8,16,128]{3,2,1,0:T(8,128)(2,1)S(1)}, u32[]{:S(2)}, u32[]{:S(2)}) async-start(bf16[32,8,16,128]{3,2,1,0:T(8,128)(2,1)} %squeeze_reshape.7), calls=%async_computation.1 | async-start | bytes 2097152 | tf_op jit(solution)/shard_map/all_to_all | solution.py:215
  13.8 0.2 rev.15
  14.0 5.2 %convolution_convert_fusion.1 = bf16[512,1024]{1,0:T(8,128)(2,1)S(1)} fusion(bf16[512,2048]{1,0:T(8,128)(2,1)} %constant.47, bf16[1024,2048]{1,0:T(8,128)(2,1)} %bitcast.59), kind=kOutput, calls=%fused_computation.9 | convolution fusion | flops 2148007936 | bytes 7340032 | tf_op jit(solution)/shard_map/dot_general | solution.py:169
  19.2 1.3 squeeze_reshape.6
  20.5 1.4 %fusion.2 = (bf16[1024]{0:T(1024)(128)(2,1)S(1)}, bf16[1024]{0:T(1024)(128)(2,1)S(1)}) fusion(s32[1024]{0:T(1024)S(1)} %bitcast.53, bf16[1024]{0:T(1024)(128)(2,1)S(1)} %convert_element_type.41, s32[1024]{0:T(1024)S(1)} %copy-done.2), kind=kLoop, calls=%fused_computation.6 | loop fusion | flops 6289408 | bytes 14336 | tf_op jit(solution)/shard_map/reduce_sum | solution.py:185
  22.0 1.1 broadcast_select_fusion
  23.1 2.5 %compare_select_fusion = (bf16[8,1024,128]{2,1,0:T(8,128)(2,1)}, bf16[8,1024,128]{2,1,0:T(8,128)(2,1)}) fusion(s32[8,128]{1,0:T(8,128)S(1)} %multiply_add_fusion, s32[1024]{0:T(1024)S(1)} %bitcast.54, bf16[8,128]{1,0:T(8,128)(2,1)S(1)} %convert_bitcast_fusion, s32[1024]{0:T(1024)S(1)} %copy-done.2), kind=kLoop, calls=%fused_computation.4 | loop fusion | flops 4194304 | bytes 4208640 | tf_op jit(solution)/shard_map/jit(_where)/select_n | solution.py:182
  25.6 14.4 %all-to-all-done.1 = bf16[32,8,16,128]{3,2,1,0:T(8,128)(2,1)S(1)} async-done(((bf16[32,8,16,128]{3,2,1,0:T(8,128)(2,1)}), bf16[32,8,16,128]{3,2,1,0:T(8,128)(2,1)S(1)}, u32[]{:S(2)}, u32[]{:S(2)}) %all-to-all-start.1) | async-done | bytes 1048608 | tf_op jit(solution)/shard_map/all_to_all | solution.py:215
  40.0 3.6 %all-to-all-start = ((bf16[32,8,16,128]{3,2,1,0:T(8,128)(2,1)}), bf16[32,8,16,128]{3,2,1,0:T(8,128)(2,1)S(1)}, u32[]{:S(2)}, u32[]{:S(2)}) async-start(bf16[32,8,16,128]{3,2,1,0:T(8,128)(2,1)} %squeeze_reshape.6), calls=%async_computation | async-start | bytes 2097152 | tf_op jit(solution)/shard_map/all_to_all | solution.py:215
  43.7 26.2 %shard_map.73 = (f32[8,2,16,256]{3,2,1,0:T(8,128)}, f32[16,256]{1,0:T(8,128)}) custom-call(bf16[8,4,8,16,128]{4,3,2,1,0:T(8,128)(2,1)} %bitcast.44, bf16[8,1024,128]{2,1,0:T(8,128)(2,1)} %get-tuple-element.16.refs_1_, bf16[8,1024,128]{2,1,0:T(8,128)(2,1)} %get-tuple-element.17.refs_2_, bf16[64,64]{1,0:T(8,128)(2,1)} %constant.43.clone.refs_3_, ...), custom_call_target="tpu_custom_call" | custom-call | flops 3556769792 | bytes 5505024 | tf_op jit(solution)/shard_map/pallas_call | solution.py:128
  69.9 0.7 reshape.91
  70.7 0.2 rev.18
  70.9 1.0 reshape.88
  72.0 0.1 slice.57
  72.1 0.4 rev.16
  72.7 0.5 copy.61
  73.3 0.3 fusion.6
  73.7 1.1 copy.52
  74.8 6.0 %all-to-all-start.2 = ((f32[32,8,2,128]{3,2,1,0:T(2,128)}), f32[32,8,2,128]{3,2,1,0:T(2,128)S(1)}, u32[]{:S(2)}, u32[]{:S(2)}) async-start(f32[32,8,2,128]{3,2,1,0:T(2,128)} %copy.52), calls=%async_computation.2 | async-start | bytes 524288 | tf_op jit(solution)/shard_map/all_to_all | solution.py:219
  80.8 24.9 %shard_map.74 = f32[8,2,16,256]{3,2,1,0:T(8,128)} custom-call(bf16[8,4,8,16,128]{4,3,2,1,0:T(8,128)(2,1)} %bitcast.43, bf16[8,1024,128]{2,1,0:T(8,128)(2,1)} %get-tuple-element.16.refs_1_, bf16[8,1024,128]{2,1,0:T(8,128)(2,1)} %get-tuple-element.17.refs_2_, bf16[64,64]{1,0:T(8,128)(2,1)} %constant.43.clone.refs_3_), custom_call_target="tpu_custom_call" | custom-call | flops 3556769792 | bytes 5505024 | tf_op jit(solution)/shard_map/pallas_call | solution.py:128
  105.8 1.0 reshape.89
  106.9 0.4 rev.17
  107.4 0.5 copy.62
  107.9 0.3 fusion.9
  108.3 0.9 copy.55
  109.2 5.7 %all-to-all-start.3 = ((f32[32,8,2,128]{3,2,1,0:T(2,128)}), f32[32,8,2,128]{3,2,1,0:T(2,128)S(1)}, u32[]{:S(2)}, u32[]{:S(2)}) async-start(f32[32,8,2,128]{3,2,1,0:T(2,128)} %copy.55), calls=%async_computation.3 | async-start | bytes 524288 | tf_op jit(solution)/shard_map/all_to_all | solution.py:225
  115.0 10.5 %all-to-all-done.3 = f32[32,8,2,128]{3,2,1,0:T(2,128)S(1)} async-done(((f32[32,8,2,128]{3,2,1,0:T(2,128)}), f32[32,8,2,128]{3,2,1,0:T(2,128)S(1)}, u32[]{:S(2)}, u32[]{:S(2)}) %all-to-all-start.3) | async-done | bytes 262176 | tf_op jit(solution)/shard_map/all_to_all | solution.py:225
  125.5 0.3 pad_maximum_fusion
  125.8 4.6 %convolution_multiply_fusion = f32[128,2,512]{2,0,1:T(8,128)S(1)} fusion(f32[1024,128,1]{1,0,2:T(8,128)S(1)} %bitcast.40, f32[2,512,1024]{2,1,0:T(8,128)} %constant.51, f32[128]{0:T(128)S(1)} %multiply_rsqrt_fusion), kind=kOutput, calls=%fused_computation.10 | convolution fusion | flops 805437440 | bytes 5243392 | tf_op jit(solution)/shard_map/dot_general | solution.py:233
  130.4 1.2 copy.59
  (33 shorter events, 0.9 us)
Async XLA Ops:
  5.2 8.6 %copy-start.3 = (s32[1024]{0:T(1024)S(1)}, s32[1024]{0:T(1024)}, u32[]{:S(2)}) copy-start(s32[1024]{0:T(1024)} %param.9) | copy-start | bytes 12292
  5.2 8.6 %copy-start.2 = (s32[1024]{0:T(1024)S(1)}, s32[1024]{0:T(1024)}, u32[]{:S(2)}) copy-start(s32[1024]{0:T(1024)} %param.8) | copy-start | bytes 12292
  6.5 33.5 %all-to-all-start.1 = ((bf16[32,8,16,128]{3,2,1,0:T(8,128)(2,1)}), bf16[32,8,16,128]{3,2,1,0:T(8,128)(2,1)S(1)}, u32[]{:S(2)}, u32[]{:S(2)}) async-start(bf16[32,8,16,128]{3,2,1,0:T(8,128)(2,1)} %squeeze_reshape.7), calls=%async_computation.1 | async-start | bytes 2097152 | tf_op jit(solution)/shard_map/all_to_all | solution.py:215
  40.0 3.7 %copy-start.1 = (bf16[32,8,16,128]{3,2,1,0:T(8,128)(2,1)}, bf16[32,8,16,128]{3,2,1,0:T(8,128)(2,1)S(1)}, u32[]{:S(2)}) copy-start(bf16[32,8,16,128]{3,2,1,0:T(8,128)(2,1)S(1)} %all-to-all-done.1) | copy-start | bytes 3145732
  40.0 33.7 %all-to-all-start = ((bf16[32,8,16,128]{3,2,1,0:T(8,128)(2,1)}), bf16[32,8,16,128]{3,2,1,0:T(8,128)(2,1)S(1)}, u32[]{:S(2)}, u32[]{:S(2)}) async-start(bf16[32,8,16,128]{3,2,1,0:T(8,128)(2,1)} %squeeze_reshape.6), calls=%async_computation | async-start | bytes 2097152 | tf_op jit(solution)/shard_map/all_to_all | solution.py:215
  43.7 29.6 %copy-start.4 = (f32[2]{0:T(128)S(1)}, f32[2]{0:T(128)}, u32[]{:S(2)}) copy-start(f32[2]{0:T(128)} %constant.44.clone) | copy-start | bytes 28
  73.7 7.1 %copy-start = (bf16[32,8,16,128]{3,2,1,0:T(8,128)(2,1)}, bf16[32,8,16,128]{3,2,1,0:T(8,128)(2,1)S(1)}, u32[]{:S(2)}) copy-start(bf16[32,8,16,128]{3,2,1,0:T(8,128)(2,1)S(1)} %all-to-all-done) | copy-start | bytes 3145732
  74.8 34.4 %all-to-all-start.2 = ((f32[32,8,2,128]{3,2,1,0:T(2,128)}), f32[32,8,2,128]{3,2,1,0:T(2,128)S(1)}, u32[]{:S(2)}, u32[]{:S(2)}) async-start(f32[32,8,2,128]{3,2,1,0:T(2,128)} %copy.52), calls=%async_computation.2 | async-start | bytes 524288 | tf_op jit(solution)/shard_map/all_to_all | solution.py:219
  109.2 16.3 %all-to-all-start.3 = ((f32[32,8,2,128]{3,2,1,0:T(2,128)}), f32[32,8,2,128]{3,2,1,0:T(2,128)S(1)}, u32[]{:S(2)}, u32[]{:S(2)}) async-start(f32[32,8,2,128]{3,2,1,0:T(2,128)} %copy.55), calls=%async_computation.3 | async-start | bytes 524288 | tf_op jit(solution)/shard_map/all_to_all | solution.py:225

commit v11 on v9

--- a/solution.py
+++ b/solution.py
@@ -216,8 +216,8 @@
     vis = unskew(sums, conj_sign)
     local_baselines = NBASE // devices
     send = vis.reshape(local_channels, 2, devices, local_baselines).transpose(2, 0, 1, 3)
-    received = lax.all_to_all(send, ("wide", "tm"), 0, 0, tiled=True)
-    stacked_in = received.reshape(CH * 2, local_baselines)
+    received = lax.all_to_all(send.astype(jnp.bfloat16), ("wide", "tm"), 0, 0, tiled=True)
+    stacked_in = received.astype(jnp.float32).reshape(CH * 2, local_baselines)
     device_position = lax.axis_index("wide") * tm_parts + lax.axis_index("tm")
     global_stack_counts = unskew(count_sums, 1.0).reshape(NBASE)
     local_stack_counts = lax.dynamic_slice_in_dim(

time: 129 us -> 123 us (0.953)
  waiting for transfers between devices: 29.8 us -> 24.9 us
    all_to_all x1, waiting for transfers between devices: 15.4 us -> 10.5 us  [body(): lax.all_to_all(send.astype(jnp.bfloat16), ('wide', 'tm'), 0, 0, tiled=True)]
  transfers between devices with their start and end apart: 3 -> 3, of which waited for: 2 -> 2; matrix products, arithmetic and copies ran while one was open for 9% -> 10% of each run, Pallas kernels for 20% -> 21%
where the time goes in v11:
time: 123 us; the launch traced here: 122 us
  Pallas kernels  51.1 us (42%)
  waiting for transfers between devices  24.9 us (20%)
  starting transfers between devices  16.7 us (14%)
  matrix products  14.1 us (11%)
  local copies, waits for them, and re-layouts  8.33 us (7%)
  other arithmetic  6.8 us (6%)
    pallas_call x2, Pallas kernels, correlate(): pl.pallas_call(functools.partial(correlate_kernel, with_counts=with_count...  51.1 us
    all_to_all x2, waiting for transfers between devices, body(): turned = lax.all_to_all(spectra_j, ('wide', 'tm'), 0, 0, tiled=True)  14.4 us
    all_to_all x2, starting transfers between devices, body(): turned = lax.all_to_all(spectra_j, ('wide', 'tm'), 0, 0, tiled=True)  11.1 us
    all_to_all x1, waiting for transfers between devices, body(): lax.all_to_all(send.astype(jnp.bfloat16), ('wide', 'tm'), 0, 0, tiled=True)  10.5 us
    dot_general x2, matrix products, channelize(): lax.dot_general(rows, flattened, NT, preferred_element_type=jnp.float32)  10.4 us
    all_to_all x1, starting transfers between devices, body(): lax.all_to_all(send.astype(jnp.bfloat16), ('wide', 'tm'), 0, 0, tiled=True)  5.65 us
    dot_general x1, matrix products, body(): lax.dot_general(stacked_in, delay, (((0,), (0,)), ((), ())), precision=la...  3.68 us
    select_n x1, other arithmetic, body(): jnp.where(wiring_rev[:, None] == source[None, :], flags[None, :], jnp.bfl...  2.54 us
  transfers between devices with their start and end apart: 3, of which 2 were waited for; matrix products, arithmetic and copies ran while one was open for 10% of the time, Pallas kernels for 21%

profile of v11, /device:TPU:0, one launch (start us, length us, event | category | flops | bytes accessed | tf_op | source)
XLA Modules:
  0.0 122.2 jit_solution(13130596161874633818)
XLA Ops:
  0.0 5.2 %convolution_convert_fusion.1 = bf16[512,1024]{1,0:T(8,128)(2,1)S(1)} fusion(bf16[512,2048]{1,0:T(8,128)(2,1)} %constant.47, bf16[1024,2048]{1,0:T(8,128)(2,1)} %bitcast.43), kind=kOutput, calls=%fused_computation.9 | convolution fusion | flops 2148007936 | bytes 7340032 | tf_op jit(solution)/shard_map/dot_general | solution.py:169
  5.2 1.3 %squeeze_reshape.6 = bf16[32,8,16,128]{3,2,1,0:T(8,128)(2,1)} reshape(bf16[512,1024]{1,0:T(8,128)(2,1)S(1)} %convolution_convert_fusion.1) | data formatting | bytes 2097152 | tf_op jit(solution)/shard_map/squeeze;reshape | solution.py:172
  6.5 7.3 %all-to-all-start = ((bf16[32,8,16,128]{3,2,1,0:T(8,128)(2,1)}), bf16[32,8,16,128]{3,2,1,0:T(8,128)(2,1)S(1)}, u32[]{:S(2)}, u32[]{:S(2)}) async-start(bf16[32,8,16,128]{3,2,1,0:T(8,128)(2,1)} %squeeze_reshape.6), calls=%async_computation | async-start | bytes 2097152 | tf_op jit(solution)/shard_map/all_to_all | solution.py:207
  13.8 5.2 %convolution_convert_fusion = bf16[512,1024]{1,0:T(8,128)(2,1)S(1)} fusion(bf16[512,2048]{1,0:T(8,128)(2,1)} %constant.49, bf16[1024,2048]{1,0:T(8,128)(2,1)} %bitcast.44), kind=kOutput, calls=%fused_computation.8 | convolution fusion | flops 2148007936 | bytes 7340032 | tf_op jit(solution)/shard_map/dot_general | solution.py:169
  19.0 1.3 %squeeze_reshape.7 = bf16[32,8,16,128]{3,2,1,0:T(8,128)(2,1)} reshape(bf16[512,1024]{1,0:T(8,128)(2,1)S(1)} %convolution_convert_fusion) | data formatting | bytes 2097152 | tf_op jit(solution)/shard_map/squeeze;reshape | solution.py:175
  20.3 0.2 rev.12
  20.5 1.4 %fusion.2 = (bf16[1024]{0:T(1024)(128)(2,1)S(1)}, bf16[1024]{0:T(1024)(128)(2,1)S(1)}) fusion(s32[1024]{0:T(1024)S(1)} %bitcast.38, bf16[1024]{0:T(1024)(128)(2,1)S(1)} %convert_element_type.45, s32[1024]{0:T(1024)S(1)} %copy-done.3), kind=kLoop, calls=%fused_computation.6 | loop fusion | flops 6289408 | bytes 14336 | tf_op jit(solution)/shard_map/reduce_sum | solution.py:185
  21.9 1.1 broadcast_select_fusion
  23.1 2.5 %compare_select_fusion = (bf16[8,1024,128]{2,1,0:T(8,128)(2,1)}, bf16[8,1024,128]{2,1,0:T(8,128)(2,1)}) fusion(s32[8,128]{1,0:T(8,128)S(1)} %multiply_add_fusion, s32[1024]{0:T(1024)S(1)} %bitcast.39, bf16[8,128]{1,0:T(8,128)(2,1)S(1)} %convert_bitcast_fusion, s32[1024]{0:T(1024)S(1)} %copy-done.3), kind=kLoop, calls=%fused_computation.4 | loop fusion | flops 4194304 | bytes 4208640 | tf_op jit(solution)/shard_map/jit(_where)/select_n | solution.py:182
  25.6 14.4 %all-to-all-done = bf16[32,8,16,128]{3,2,1,0:T(8,128)(2,1)S(1)} async-done(((bf16[32,8,16,128]{3,2,1,0:T(8,128)(2,1)}), bf16[32,8,16,128]{3,2,1,0:T(8,128)(2,1)S(1)}, u32[]{:S(2)}, u32[]{:S(2)}) %all-to-all-start) | async-done | bytes 1048608 | tf_op jit(solution)/shard_map/all_to_all | solution.py:207
  40.0 3.8 %all-to-all-start.1 = ((bf16[32,8,16,128]{3,2,1,0:T(8,128)(2,1)}), bf16[32,8,16,128]{3,2,1,0:T(8,128)(2,1)S(1)}, u32[]{:S(2)}, u32[]{:S(2)}) async-start(bf16[32,8,16,128]{3,2,1,0:T(8,128)(2,1)} %squeeze_reshape.7), calls=%async_computation.1 | async-start | bytes 2097152 | tf_op jit(solution)/shard_map/all_to_all | solution.py:207
  43.9 26.2 %shard_map.73 = (f32[8,2,16,256]{3,2,1,0:T(8,128)}, f32[16,256]{1,0:T(8,128)}) custom-call(bf16[8,4,8,16,128]{4,3,2,1,0:T(8,128)(2,1)} %bitcast.32, bf16[8,1024,128]{2,1,0:T(8,128)(2,1)} %get-tuple-element.12.refs_1_, bf16[8,1024,128]{2,1,0:T(8,128)(2,1)} %get-tuple-element.13.refs_2_, bf16[64,64]{1,0:T(8,128)(2,1)} %constant.43.clone.refs_3_, ...), custom_call_target="tpu_custom_call" | custom-call | flops 3556769792 | bytes 5505024 | tf_op jit(solution)/shard_map/pallas_call | solution.py:128
  70.1 1.0 copy-done.1
  71.0 24.9 %shard_map.74 = f32[8,2,16,256]{3,2,1,0:T(8,128)} custom-call(bf16[8,4,8,16,128]{4,3,2,1,0:T(8,128)(2,1)} %bitcast.33, bf16[8,1024,128]{2,1,0:T(8,128)(2,1)} %get-tuple-element.12.refs_1_, bf16[8,1024,128]{2,1,0:T(8,128)(2,1)} %get-tuple-element.13.refs_2_, bf16[64,64]{1,0:T(8,128)(2,1)} %constant.43.clone.refs_3_), custom_call_target="tpu_custom_call" | custom-call | flops 3556769792 | bytes 5505024 | tf_op jit(solution)/shard_map/pallas_call | solution.py:128
  96.0 1.0 pad_maximum_fusion
  97.0 0.1 reshape.86
  97.1 0.7 rev.13
  97.8 0.2 slice.45
  98.1 0.2 rev.14
  98.3 0.1 slice.48
  98.3 0.1 copy.42
  98.5 0.1 slice.44
  98.5 0.9 copy.45
  99.4 0.1 fusion.10
  99.5 0.5 fusion.7
  100.0 0.1 convert_element_type.50
  100.1 0.9 copy.40
  101.0 5.6 %all-to-all-start.2 = ((bf16[32,16,2,128]{3,2,1,0:T(2,128)(2,1)}), bf16[32,16,2,128]{3,2,1,0:T(2,128)(2,1)S(1)}, u32[]{:S(2)}, u32[]{:S(2)}) async-start(bf16[32,16,2,128]{3,2,1,0:T(2,128)(2,1)} %copy.40), calls=%async_computation.2 | async-start | bytes 524288 | tf_op jit(solution)/shard_map/all_to_all | solution.py:219
  106.7 0.1 multiply_rsqrt_fusion
  106.8 10.5 %all-to-all-done.2 = bf16[32,16,2,128]{3,2,1,0:T(2,128)(2,1)S(1)} async-done(((bf16[32,16,2,128]{3,2,1,0:T(2,128)(2,1)}), bf16[32,16,2,128]{3,2,1,0:T(2,128)(2,1)S(1)}, u32[]{:S(2)}, u32[]{:S(2)}) %all-to-all-start.2) | async-done | bytes 262176 | tf_op jit(solution)/shard_map/all_to_all | solution.py:219
  117.3 3.7 %convolution_multiply_fusion = f32[128,2,512]{2,0,1:T(8,128)S(1)} fusion(bf16[1024,128,1]{1,0,2:T(8,128)(2,1)S(1)} %bitcast.31, f32[2,512,1024]{2,1,0:T(8,128)} %constant.51, f32[128]{0:T(128)S(1)} %multiply_rsqrt_fusion), kind=kOutput, calls=%fused_computation.10 | convolution fusion | flops 805437440 | bytes 4981248 | tf_op jit(solution)/shard_map/dot_general | solution.py:227
  121.0 1.2 copy.43
  (26 shorter events, 0.1 us)
Async XLA Ops:
  6.5 33.5 %all-to-all-start = ((bf16[32,8,16,128]{3,2,1,0:T(8,128)(2,1)}), bf16[32,8,16,128]{3,2,1,0:T(8,128)(2,1)S(1)}, u32[]{:S(2)}, u32[]{:S(2)}) async-start(bf16[32,8,16,128]{3,2,1,0:T(8,128)(2,1)} %squeeze_reshape.6), calls=%async_computation | async-start | bytes 2097152 | tf_op jit(solution)/shard_map/all_to_all | solution.py:207
  19.0 1.3 %copy-start.3 = (s32[1024]{0:T(1024)S(1)}, s32[1024]{0:T(1024)}, u32[]{:S(2)}) copy-start(s32[1024]{0:T(1024)} %param.8) | copy-start | bytes 12292
  19.0 1.5 %copy-start.4 = (s32[1024]{0:T(1024)S(1)}, s32[1024]{0:T(1024)}, u32[]{:S(2)}) copy-start(s32[1024]{0:T(1024)} %param.9) | copy-start | bytes 12292
  40.0 3.9 %copy-start = (bf16[32,8,16,128]{3,2,1,0:T(8,128)(2,1)}, bf16[32,8,16,128]{3,2,1,0:T(8,128)(2,1)S(1)}, u32[]{:S(2)}) copy-start(bf16[32,8,16,128]{3,2,1,0:T(8,128)(2,1)S(1)} %all-to-all-done) | copy-start | bytes 3145732
  40.0 30.1 %all-to-all-start.1 = ((bf16[32,8,16,128]{3,2,1,0:T(8,128)(2,1)}), bf16[32,8,16,128]{3,2,1,0:T(8,128)(2,1)S(1)}, u32[]{:S(2)}, u32[]{:S(2)}) async-start(bf16[32,8,16,128]{3,2,1,0:T(8,128)(2,1)} %squeeze_reshape.7), calls=%async_computation.1 | async-start | bytes 2097152 | tf_op jit(solution)/shard_map/all_to_all | solution.py:207
  70.1 1.0 copy-start.1
  71.0 24.9 %copy-start.2 = (f32[8,2,16,256]{3,2,1,0:T(8,128)S(1)}, f32[8,2,16,256]{3,2,1,0:T(8,128)}, u32[]{:S(2)}) copy-start(f32[8,2,16,256]{3,2,1,0:T(8,128)} %get-tuple-element.10) | copy-start | bytes 786436
  96.0 2.1 %copy-start.5 = (f32[16,256]{1,0:T(8,128)S(1)}, f32[16,256]{1,0:T(8,128)}, u32[]{:S(2)}) copy-start(f32[16,256]{1,0:T(8,128)} %get-tuple-element.14) | copy-start | bytes 49156
  97.0 2.5 %copy-start.6 = (f32[2]{0:T(128)S(1)}, f32[2]{0:T(128)}, u32[]{:S(2)}) copy-start(f32[2]{0:T(128)} %constant.44.clone) | copy-start | bytes 28
  101.0 16.3 %all-to-all-start.2 = ((bf16[32,16,2,128]{3,2,1,0:T(2,128)(2,1)}), bf16[32,16,2,128]{3,2,1,0:T(2,128)(2,1)S(1)}, u32[]{:S(2)}, u32[]{:S(2)}) async-start(bf16[32,16,2,128]{3,2,1,0:T(2,128)(2,1)} %copy.40), calls=%async_computation.2 | async-start | bytes 524288 | tf_op jit(solution)/shard_map/all_to_all | solution.py:219

commit v12 on v11

--- a/solution.py
+++ b/solution.py
@@ -1,6 +1,7 @@
 import functools
 import math
 
+import ml_dtypes
 import numpy as np
 import jax
 import jax.numpy as jnp
@@ -41,7 +42,7 @@
     w[:, 1, 0] = sine
     w[:, 0, 1] = -sine
     w[:, 1, 1] = cosine
-    return jnp.asarray(w.reshape(2 * frequency_channels, 2 * frequency_channels))
+    return w.reshape(2 * frequency_channels, 2 * frequency_channels)
 
 
 def pair_keep():
@@ -217,17 +218,20 @@
     local_baselines = NBASE // devices
     send = vis.reshape(local_channels, 2, devices, local_baselines).transpose(2, 0, 1, 3)
     received = lax.all_to_all(send.astype(jnp.bfloat16), ("wide", "tm"), 0, 0, tiled=True)
-    stacked_in = received.astype(jnp.float32).reshape(CH * 2, local_baselines)
+    stacked_in = received.reshape(CH * 2, local_baselines)
     device_position = lax.axis_index("wide") * tm_parts + lax.axis_index("tm")
     global_stack_counts = unskew(count_sums, 1.0).reshape(NBASE)
     local_stack_counts = lax.dynamic_slice_in_dim(
         global_stack_counts, device_position * local_baselines, local_baselines
     )
     delay = delay_matrix_const(CH)
+    high_np = delay.astype(ml_dtypes.bfloat16)
+    delay_high = jnp.asarray(high_np)
+    delay_low = jnp.asarray((delay - high_np.astype(np.float32)).astype(ml_dtypes.bfloat16))
+    contract = (((0,), (0,)), ((), ()))
     spectra_out = lax.dot_general(
-        stacked_in, delay, (((0,), (0,)), ((), ())), precision=lax.Precision.HIGH,
-        preferred_element_type=jnp.float32,
-    )
+        stacked_in, delay_high, contract, preferred_element_type=jnp.float32
+    ) + lax.dot_general(stacked_in, delay_low, contract, preferred_element_type=jnp.float32)
     weight = 1.0 / jnp.sqrt(frames_all * CH * jnp.maximum(local_stack_counts, 1.0))
     return spectra_out.reshape(local_baselines, 2, CH) * weight[:, None, None]
 

time: 123 us -> 123 us (level)
  matrix products: 14.1 us -> 11.3 us
  other arithmetic: 6.8 us -> 8.83 us
    dot_general x1 -> x2, matrix products: 3.68 us -> 0.93 us  [the longest x1 0.47 us: body(): lax.dot_general(stacked_in, delay_high, contract, preferred_element_type=...]
where the time goes in v12:
time: 123 us; the launch traced here: 122 us
  Pallas kernels  51.1 us (42%)
  waiting for transfers between devices  24.8 us (20%)
  starting transfers between devices  16.7 us (14%)
  matrix products  11.3 us (9%)
  local copies, waits for them, and re-layouts  9.42 us (8%)
  other arithmetic  8.83 us (7%)
    pallas_call x2, Pallas kernels, correlate(): pl.pallas_call(functools.partial(correlate_kernel, with_counts=with_count...  51.1 us
    all_to_all x2, waiting for transfers between devices, body(): turned = lax.all_to_all(spectra_j, ('wide', 'tm'), 0, 0, tiled=True)  14.3 us
    all_to_all x2, starting transfers between devices, body(): turned = lax.all_to_all(spectra_j, ('wide', 'tm'), 0, 0, tiled=True)  11.1 us
    all_to_all x1, waiting for transfers between devices, body(): lax.all_to_all(send.astype(jnp.bfloat16), ('wide', 'tm'), 0, 0, tiled=True)  10.5 us
    dot_general x2, matrix products, channelize(): lax.dot_general(rows, flattened, NT, preferred_element_type=jnp.float32)  10.4 us
    all_to_all x1, starting transfers between devices, body(): lax.all_to_all(send.astype(jnp.bfloat16), ('wide', 'tm'), 0, 0, tiled=True)  5.65 us
    select_n x1, other arithmetic, body(): jnp.where(wiring_rev[:, None] == source[None, :], flags[None, :], jnp.bfl...  2.56 us
  transfers between devices with their start and end apart: 3, of which 2 were waited for; matrix products, arithmetic and copies ran while one was open for 10% of the time, Pallas kernels for 21%

profile of v12, /device:TPU:0, one launch (start us, length us, event | category | flops | bytes accessed | tf_op | source)
XLA Modules:
  0.0 122.5 jit_solution(7493152465187672655)
XLA Ops:
  0.0 5.2 %convolution_convert_fusion.1 = bf16[512,1024]{1,0:T(8,128)(2,1)S(1)} fusion(bf16[512,2048]{1,0:T(8,128)(2,1)} %constant.50, bf16[1024,2048]{1,0:T(8,128)(2,1)} %bitcast.44), kind=kOutput, calls=%fused_computation.9 | convolution fusion | flops 2148007936 | bytes 7340032 | tf_op jit(solution)/shard_map/dot_general | solution.py:170
  5.2 1.3 %squeeze_reshape.6 = bf16[32,8,16,128]{3,2,1,0:T(8,128)(2,1)} reshape(bf16[512,1024]{1,0:T(8,128)(2,1)S(1)} %convolution_convert_fusion.1) | data formatting | bytes 2097152 | tf_op jit(solution)/shard_map/squeeze;reshape | solution.py:173
  6.5 7.3 %all-to-all-start = ((bf16[32,8,16,128]{3,2,1,0:T(8,128)(2,1)}), bf16[32,8,16,128]{3,2,1,0:T(8,128)(2,1)S(1)}, u32[]{:S(2)}, u32[]{:S(2)}) async-start(bf16[32,8,16,128]{3,2,1,0:T(8,128)(2,1)} %squeeze_reshape.6), calls=%async_computation | async-start | bytes 2097152 | tf_op jit(solution)/shard_map/all_to_all | solution.py:208
  13.8 5.2 %convolution_convert_fusion = bf16[512,1024]{1,0:T(8,128)(2,1)S(1)} fusion(bf16[512,2048]{1,0:T(8,128)(2,1)} %constant.52, bf16[1024,2048]{1,0:T(8,128)(2,1)} %bitcast.45), kind=kOutput, calls=%fused_computation.8 | convolution fusion | flops 2148007936 | bytes 7340032 | tf_op jit(solution)/shard_map/dot_general | solution.py:170
  19.0 1.3 %squeeze_reshape.7 = bf16[32,8,16,128]{3,2,1,0:T(8,128)(2,1)} reshape(bf16[512,1024]{1,0:T(8,128)(2,1)S(1)} %convolution_convert_fusion) | data formatting | bytes 2097152 | tf_op jit(solution)/shard_map/squeeze;reshape | solution.py:176
  20.3 0.2 rev.12
  20.5 1.4 %fusion.2 = (bf16[1024]{0:T(1024)(128)(2,1)S(1)}, bf16[1024]{0:T(1024)(128)(2,1)S(1)}) fusion(s32[1024]{0:T(1024)S(1)} %bitcast.39, bf16[1024]{0:T(1024)(128)(2,1)S(1)} %convert_element_type.44, s32[1024]{0:T(1024)S(1)} %copy-done.5), kind=kLoop, calls=%fused_computation.6 | loop fusion | flops 6289408 | bytes 14336 | tf_op jit(solution)/shard_map/reduce_sum | solution.py:186
  22.0 1.1 broadcast_select_fusion
  23.1 2.6 %compare_select_fusion = (bf16[8,1024,128]{2,1,0:T(8,128)(2,1)}, bf16[8,1024,128]{2,1,0:T(8,128)(2,1)}) fusion(s32[8,128]{1,0:T(8,128)S(1)} %multiply_add_fusion, s32[1024]{0:T(1024)S(1)} %bitcast.40, bf16[8,128]{1,0:T(8,128)(2,1)S(1)} %convert_bitcast_fusion, s32[1024]{0:T(1024)S(1)} %copy-done.5), kind=kLoop, calls=%fused_computation.4 | loop fusion | flops 4194304 | bytes 4208640 | tf_op jit(solution)/shard_map/jit(_where)/select_n | solution.py:183
  25.7 14.3 %all-to-all-done = bf16[32,8,16,128]{3,2,1,0:T(8,128)(2,1)S(1)} async-done(((bf16[32,8,16,128]{3,2,1,0:T(8,128)(2,1)}), bf16[32,8,16,128]{3,2,1,0:T(8,128)(2,1)S(1)}, u32[]{:S(2)}, u32[]{:S(2)}) %all-to-all-start) | async-done | bytes 1048608 | tf_op jit(solution)/shard_map/all_to_all | solution.py:208
  40.0 3.8 %all-to-all-start.1 = ((bf16[32,8,16,128]{3,2,1,0:T(8,128)(2,1)}), bf16[32,8,16,128]{3,2,1,0:T(8,128)(2,1)S(1)}, u32[]{:S(2)}, u32[]{:S(2)}) async-start(bf16[32,8,16,128]{3,2,1,0:T(8,128)(2,1)} %squeeze_reshape.7), calls=%async_computation.1 | async-start | bytes 2097152 | tf_op jit(solution)/shard_map/all_to_all | solution.py:208
  43.9 26.2 %shard_map.82 = (f32[8,2,16,256]{3,2,1,0:T(8,128)}, f32[16,256]{1,0:T(8,128)}) custom-call(bf16[8,4,8,16,128]{4,3,2,1,0:T(8,128)(2,1)} %bitcast.33, bf16[8,1024,128]{2,1,0:T(8,128)(2,1)} %get-tuple-element.12.refs_1_, bf16[8,1024,128]{2,1,0:T(8,128)(2,1)} %get-tuple-element.13.refs_2_, bf16[64,64]{1,0:T(8,128)(2,1)} %constant.45.clone.refs_3_, ...), custom_call_target="tpu_custom_call" | custom-call | flops 3556769792 | bytes 5505024 | tf_op jit(solution)/shard_map/pallas_call | solution.py:129
  70.1 1.0 copy-done.3
  71.1 24.9 %shard_map.83 = f32[8,2,16,256]{3,2,1,0:T(8,128)} custom-call(bf16[8,4,8,16,128]{4,3,2,1,0:T(8,128)(2,1)} %bitcast.34, bf16[8,1024,128]{2,1,0:T(8,128)(2,1)} %get-tuple-element.12.refs_1_, bf16[8,1024,128]{2,1,0:T(8,128)(2,1)} %get-tuple-element.13.refs_2_, bf16[64,64]{1,0:T(8,128)(2,1)} %constant.45.clone.refs_3_), custom_call_target="tpu_custom_call" | custom-call | flops 3556769792 | bytes 5505024 | tf_op jit(solution)/shard_map/pallas_call | solution.py:129
  96.0 1.0 pad_maximum_fusion
  97.0 0.1 reshape.87
  97.2 0.7 rev.13
  97.8 0.9 slice.45
  98.8 0.2 rev.14
  99.0 0.1 copy.34
  99.2 0.9 copy.35
  100.1 0.1 fusion.10
  100.2 1.4 %fusion.7 = bf16[16,2,4,4,256]{4,3,2,1,0:T(4,128)(2,1)S(1)} fusion(f32[16,2,4,4,256]{4,3,2,1,0:T(4,128)S(1)} %rev.13, f32[16,2,4,4,255]{4,3,2,1,0:T(4,128)S(1)} %bitcast.29, f32[16,2,4,4,1]{4,3,2,1,0:T(4,128)} %slice.45, f32[4,4,256]{2,1,0:T(4,128)S(1)} %get-tuple-element.20, f32[2]{0:T(128)S(1)} %copy-done.8, f32[16,2,4,4]{3,2,1,0:T(4,128)S(1)} %bitcast.36, ...), kind=kLoop, calls=%fused_computation.16 | loop fusion | flops 786432 | bytes 1333512 | tf_op jit(solution)/shard_map/convert_element_type | solution.py:220
  101.7 0.1 convert_element_type.49
  101.8 0.9 copy.33
  102.7 5.6 %all-to-all-start.2 = ((bf16[32,16,2,128]{3,2,1,0:T(2,128)(2,1)}), bf16[32,16,2,128]{3,2,1,0:T(2,128)(2,1)S(1)}, u32[]{:S(2)}, u32[]{:S(2)}) async-start(bf16[32,16,2,128]{3,2,1,0:T(2,128)(2,1)} %copy.33), calls=%async_computation.2 | async-start | bytes 524288 | tf_op jit(solution)/shard_map/all_to_all | solution.py:220
  108.4 10.5 %all-to-all-done.2 = bf16[32,16,2,128]{3,2,1,0:T(2,128)(2,1)S(1)} async-done(((bf16[32,16,2,128]{3,2,1,0:T(2,128)(2,1)}), bf16[32,16,2,128]{3,2,1,0:T(2,128)(2,1)S(1)}, u32[]{:S(2)}, u32[]{:S(2)}) %all-to-all-start.2) | async-done | bytes 262176 | tf_op jit(solution)/shard_map/all_to_all | solution.py:220
  118.9 0.5 fusion.13
  119.4 1.1 copy-done.1
  120.5 0.5 convolution_add_fusion
  121.0 0.4 reshape.89
  121.4 1.0 broadcast_multiply_fusion
  (32 shorter events, 0.3 us)
Async XLA Ops:
  6.5 33.5 %all-to-all-start = ((bf16[32,8,16,128]{3,2,1,0:T(8,128)(2,1)}), bf16[32,8,16,128]{3,2,1,0:T(8,128)(2,1)S(1)}, u32[]{:S(2)}, u32[]{:S(2)}) async-start(bf16[32,8,16,128]{3,2,1,0:T(8,128)(2,1)} %squeeze_reshape.6), calls=%async_computation | async-start | bytes 2097152 | tf_op jit(solution)/shard_map/all_to_all | solution.py:208
  19.0 1.3 %copy-start.5 = (s32[1024]{0:T(1024)S(1)}, s32[1024]{0:T(1024)}, u32[]{:S(2)}) copy-start(s32[1024]{0:T(1024)} %param.9) | copy-start | bytes 12292
  19.0 1.5 %copy-start.6 = (s32[1024]{0:T(1024)S(1)}, s32[1024]{0:T(1024)}, u32[]{:S(2)}) copy-start(s32[1024]{0:T(1024)} %param.10) | copy-start | bytes 12292
  40.0 3.9 %copy-start.2 = (bf16[32,8,16,128]{3,2,1,0:T(8,128)(2,1)}, bf16[32,8,16,128]{3,2,1,0:T(8,128)(2,1)S(1)}, u32[]{:S(2)}) copy-start(bf16[32,8,16,128]{3,2,1,0:T(8,128)(2,1)S(1)} %all-to-all-done) | copy-start | bytes 3145732
  40.0 30.1 %all-to-all-start.1 = ((bf16[32,8,16,128]{3,2,1,0:T(8,128)(2,1)}), bf16[32,8,16,128]{3,2,1,0:T(8,128)(2,1)S(1)}, u32[]{:S(2)}, u32[]{:S(2)}) async-start(bf16[32,8,16,128]{3,2,1,0:T(8,128)(2,1)} %squeeze_reshape.7), calls=%async_computation.1 | async-start | bytes 2097152 | tf_op jit(solution)/shard_map/all_to_all | solution.py:208
  70.1 1.0 copy-start.3
  71.1 24.9 %copy-start.4 = (f32[8,2,16,256]{3,2,1,0:T(8,128)S(1)}, f32[8,2,16,256]{3,2,1,0:T(8,128)}, u32[]{:S(2)}) copy-start(f32[8,2,16,256]{3,2,1,0:T(8,128)} %get-tuple-element.10) | copy-start | bytes 786436
  96.0 2.8 %copy-start.7 = (f32[16,256]{1,0:T(8,128)S(1)}, f32[16,256]{1,0:T(8,128)}, u32[]{:S(2)}) copy-start(f32[16,256]{1,0:T(8,128)} %get-tuple-element.14) | copy-start | bytes 49156
  97.0 3.2 %copy-start.8 = (f32[2]{0:T(128)S(1)}, f32[2]{0:T(128)}, u32[]{:S(2)}) copy-start(f32[2]{0:T(128)} %constant.46.clone) | copy-start | bytes 28
  99.2 19.8 %copy-start = (bf16[1024,1024]{1,0:T(8,128)(2,1)S(1)}, bf16[1024,1024]{1,0:T(8,128)(2,1)}, u32[]{:S(2)}) copy-start(bf16[1024,1024]{1,0:T(8,128)(2,1)} %constant.47.clone) | copy-start | bytes 6291460
  102.7 16.3 %all-to-all-start.2 = ((bf16[32,16,2,128]{3,2,1,0:T(2,128)(2,1)}), bf16[32,16,2,128]{3,2,1,0:T(2,128)(2,1)S(1)}, u32[]{:S(2)}, u32[]{:S(2)}) async-start(bf16[32,16,2,128]{3,2,1,0:T(2,128)(2,1)} %copy.33), calls=%async_computation.2 | async-start | bytes 524288 | tf_op jit(solution)/shard_map/all_to_all | solution.py:220
  118.9 1.6 %copy-start.1 = (bf16[1024,1024]{1,0:T(8,128)(2,1)S(1)}, bf16[1024,1024]{1,0:T(8,128)(2,1)}, u32[]{:S(2)}) copy-start(bf16[1024,1024]{1,0:T(8,128)(2,1)} %constant.48.clone) | copy-start | bytes 6291460

commit v13 on v11

--- a/solution.py
+++ b/solution.py
@@ -50,19 +50,37 @@
     return 1.0 - same * first
 
 
-def diag_pairs(left, right, upper, write):
+HALF = FEEDS // 2
+
+
+def diag_pairs(left, right, upper, upper_half, write):
     for a in range(CYL):
         for b in range(a, CYL):
+            right_b = right[b * FEEDS:(b + 1) * FEEDS]
+            if a == b:
+                top = lax.dot_general(
+                    left[a * FEEDS:a * FEEDS + HALF], right_b, NT, preferred_element_type=jnp.float32
+                )
+                top = pltpu.roll(top, 0, 1, stride=1, stride_axis=0)
+                bottom = lax.dot_general(
+                    left[a * FEEDS + HALF:(a + 1) * FEEDS], right_b[:HALF], NT,
+                    preferred_element_type=jnp.float32,
+                )
+                bottom = pltpu.roll(bottom, 0, 1, stride=1, stride_axis=0)
+                up_left = jnp.sum(jnp.where(upper_half, top[:, :HALF], 0.0), axis=0, keepdims=True)
+                up_right = jnp.sum(top[:, HALF:], axis=0, keepdims=True) + jnp.sum(
+                    jnp.where(upper_half, bottom, 0.0), axis=0, keepdims=True
+                )
+                write(a * CYL + b, jnp.concatenate([up_left, up_right], axis=1))
+                continue
             tile = lax.dot_general(
-                left[a * FEEDS:(a + 1) * FEEDS], right[b * FEEDS:(b + 1) * FEEDS], NT,
-                preferred_element_type=jnp.float32,
+                left[a * FEEDS:(a + 1) * FEEDS], right_b, NT, preferred_element_type=jnp.float32,
             )
             skewed = pltpu.roll(tile, 0, 1, stride=1, stride_axis=0)
             up = jnp.sum(jnp.where(upper, skewed, 0.0), axis=0, keepdims=True)
             write(a * CYL + b, up)
-            if a < b:
-                total = jnp.sum(skewed, axis=0, keepdims=True)
-                write(b * CYL + a, total - up)
+            total = jnp.sum(skewed, axis=0, keepdims=True)
+            write(b * CYL + a, total - up)
 
 
 def correlate_kernel(*refs, with_counts):
@@ -74,6 +92,7 @@
     row_at = lax.broadcasted_iota(jnp.int32, (FEEDS, FEEDS), 0)
     col_at = lax.broadcasted_iota(jnp.int32, (FEEDS, FEEDS), 1)
     upper = col_at >= row_at
+    upper_half = upper[:HALF, :HALF]
 
     if with_counts:
         @pl.when(pl.program_id(0) == 0)
@@ -81,7 +100,7 @@
             def write_count(slot, value):
                 n_ref[pl.ds(slot, 1), :] = value
 
-            diag_pairs(fm_ref[...], fmr_ref[...], upper, write_count)
+            diag_pairs(fm_ref[...], fmr_ref[...], upper, upper_half, write_count)
 
     g = None
     gr = None
@@ -98,7 +117,7 @@
         def write_vis(slot, value, part=part):
             o_ref[0, part, pl.ds(slot, 1), :] = value
 
-        diag_pairs(g, right, upper, write_vis)
+        diag_pairs(g, right, upper, upper_half, write_vis)
 
 
 def correlate(blocks, pt, ptr, rm, fm=None, fmr=None):

time: 123 us -> 121 us (0.984)
  Pallas kernels: 51.1 us -> 49.8 us
    pallas_call x2, Pallas kernels: 51.1 us -> 49.8 us  [correlate(): pl.pallas_call(functools.partial(correlate_kernel, with_counts=with_count...]
  transfers between devices with their start and end apart: 3 -> 3, of which waited for: 2 -> 3; matrix products, arithmetic and copies ran while one was open for 10% -> 10% of each run, Pallas kernels for 21% -> 21%
where the time goes in v13:
time: 121 us
  Pallas kernels  49.8 us (41%)
  waiting for transfers between devices  25.4 us (21%)
  starting transfers between devices  16.2 us (13%)
  matrix products  14.1 us (12%)
  local copies, waits for them, and re-layouts  8.33 us (7%)
  other arithmetic  6.8 us (6%)
    pallas_call x2, Pallas kernels, correlate(): pl.pallas_call(functools.partial(correlate_kernel, with_counts=with_count...  49.8 us
    all_to_all x2, waiting for transfers between devices, body(): turned = lax.all_to_all(spectra_j, ('wide', 'tm'), 0, 0, tiled=True)  15 us
    all_to_all x2, starting transfers between devices, body(): turned = lax.all_to_all(spectra_j, ('wide', 'tm'), 0, 0, tiled=True)  11.1 us
    all_to_all x1, waiting for transfers between devices, body(): lax.all_to_all(send.astype(jnp.bfloat16), ('wide', 'tm'), 0, 0, tiled=True)  10.5 us
    dot_general x2, matrix products, channelize(): lax.dot_general(rows, flattened, NT, preferred_element_type=jnp.float32)  10.4 us
    all_to_all x1, starting transfers between devices, body(): lax.all_to_all(send.astype(jnp.bfloat16), ('wide', 'tm'), 0, 0, tiled=True)  5.13 us
    dot_general x1, matrix products, body(): lax.dot_general(stacked_in, delay, (((0,), (0,)), ((), ())), precision=la...  3.68 us
    select_n x1, other arithmetic, body(): jnp.where(wiring_rev[:, None] == source[None, :], flags[None, :], jnp.bfl...  2.54 us
  transfers between devices with their start and end apart: 3, of which 3 were waited for; matrix products, arithmetic and copies ran while one was open for 10% of the time, Pallas kernels for 21%

profile of v13, /device:TPU:0, one launch (start us, length us, event | category | flops | bytes accessed | tf_op | source)
XLA Modules:
  0.0 120.9 jit_solution(17793282767966646363)
XLA Ops:
  0.0 5.2 %convolution_convert_fusion.1 = bf16[512,1024]{1,0:T(8,128)(2,1)S(1)} fusion(bf16[512,2048]{1,0:T(8,128)(2,1)} %constant.47, bf16[1024,2048]{1,0:T(8,128)(2,1)} %bitcast.43), kind=kOutput, calls=%fused_computation.9 | convolution fusion | flops 2148007936 | bytes 7340032 | tf_op jit(solution)/shard_map/dot_general | solution.py:188
  5.2 1.3 %squeeze_reshape.6 = bf16[32,8,16,128]{3,2,1,0:T(8,128)(2,1)} reshape(bf16[512,1024]{1,0:T(8,128)(2,1)S(1)} %convolution_convert_fusion.1) | data formatting | bytes 2097152 | tf_op jit(solution)/shard_map/squeeze;reshape | solution.py:191
  6.5 7.3 %all-to-all-start = ((bf16[32,8,16,128]{3,2,1,0:T(8,128)(2,1)}), bf16[32,8,16,128]{3,2,1,0:T(8,128)(2,1)S(1)}, u32[]{:S(2)}, u32[]{:S(2)}) async-start(bf16[32,8,16,128]{3,2,1,0:T(8,128)(2,1)} %squeeze_reshape.6), calls=%async_computation | async-start | bytes 2097152 | tf_op jit(solution)/shard_map/all_to_all | solution.py:226
  13.8 5.2 %convolution_convert_fusion = bf16[512,1024]{1,0:T(8,128)(2,1)S(1)} fusion(bf16[512,2048]{1,0:T(8,128)(2,1)} %constant.49, bf16[1024,2048]{1,0:T(8,128)(2,1)} %bitcast.44), kind=kOutput, calls=%fused_computation.8 | convolution fusion | flops 2148007936 | bytes 7340032 | tf_op jit(solution)/shard_map/dot_general | solution.py:188
  19.0 1.3 %squeeze_reshape.7 = bf16[32,8,16,128]{3,2,1,0:T(8,128)(2,1)} reshape(bf16[512,1024]{1,0:T(8,128)(2,1)S(1)} %convolution_convert_fusion) | data formatting | bytes 2097152 | tf_op jit(solution)/shard_map/squeeze;reshape | solution.py:194
  20.3 0.2 rev.12
  20.5 1.4 %fusion.2 = (bf16[1024]{0:T(1024)(128)(2,1)S(1)}, bf16[1024]{0:T(1024)(128)(2,1)S(1)}) fusion(s32[1024]{0:T(1024)S(1)} %bitcast.38, bf16[1024]{0:T(1024)(128)(2,1)S(1)} %convert_element_type.45, s32[1024]{0:T(1024)S(1)} %copy-done.3), kind=kLoop, calls=%fused_computation.6 | loop fusion | flops 6289408 | bytes 14336 | tf_op jit(solution)/shard_map/reduce_sum | solution.py:204
  21.9 1.1 broadcast_select_fusion
  23.1 2.5 %compare_select_fusion = (bf16[8,1024,128]{2,1,0:T(8,128)(2,1)}, bf16[8,1024,128]{2,1,0:T(8,128)(2,1)}) fusion(s32[8,128]{1,0:T(8,128)S(1)} %multiply_add_fusion, s32[1024]{0:T(1024)S(1)} %bitcast.39, bf16[8,128]{1,0:T(8,128)(2,1)S(1)} %convert_bitcast_fusion, s32[1024]{0:T(1024)S(1)} %copy-done.3), kind=kLoop, calls=%fused_computation.4 | loop fusion | flops 4194304 | bytes 4208640 | tf_op jit(solution)/shard_map/jit(_where)/select_n | solution.py:201
  25.6 14.4 %all-to-all-done = bf16[32,8,16,128]{3,2,1,0:T(8,128)(2,1)S(1)} async-done(((bf16[32,8,16,128]{3,2,1,0:T(8,128)(2,1)}), bf16[32,8,16,128]{3,2,1,0:T(8,128)(2,1)S(1)}, u32[]{:S(2)}, u32[]{:S(2)}) %all-to-all-start) | async-done | bytes 1048608 | tf_op jit(solution)/shard_map/all_to_all | solution.py:226
  40.0 3.8 %all-to-all-start.1 = ((bf16[32,8,16,128]{3,2,1,0:T(8,128)(2,1)}), bf16[32,8,16,128]{3,2,1,0:T(8,128)(2,1)S(1)}, u32[]{:S(2)}, u32[]{:S(2)}) async-start(bf16[32,8,16,128]{3,2,1,0:T(8,128)(2,1)} %squeeze_reshape.7), calls=%async_computation.1 | async-start | bytes 2097152 | tf_op jit(solution)/shard_map/all_to_all | solution.py:226
  43.9 25.4 %shard_map.73 = (f32[8,2,16,256]{3,2,1,0:T(8,128)}, f32[16,256]{1,0:T(8,128)}) custom-call(bf16[8,4,8,16,128]{4,3,2,1,0:T(8,128)(2,1)} %bitcast.32, bf16[8,1024,128]{2,1,0:T(8,128)(2,1)} %get-tuple-element.12.refs_1_, bf16[8,1024,128]{2,1,0:T(8,128)(2,1)} %get-tuple-element.13.refs_2_, bf16[64,64]{1,0:T(8,128)(2,1)} %constant.43.clone.refs_3_, ...), custom_call_target="tpu_custom_call" | custom-call | flops 3556769792 | bytes 5505024 | tf_op jit(solution)/shard_map/pallas_call | solution.py:147
  69.3 0.6 all-to-all-done.1
  69.9 1.0 copy-done.1
  70.8 24.4 %shard_map.74 = f32[8,2,16,256]{3,2,1,0:T(8,128)} custom-call(bf16[8,4,8,16,128]{4,3,2,1,0:T(8,128)(2,1)} %bitcast.33, bf16[8,1024,128]{2,1,0:T(8,128)(2,1)} %get-tuple-element.12.refs_1_, bf16[8,1024,128]{2,1,0:T(8,128)(2,1)} %get-tuple-element.13.refs_2_, bf16[64,64]{1,0:T(8,128)(2,1)} %constant.43.clone.refs_3_), custom_call_target="tpu_custom_call" | custom-call | flops 3556769792 | bytes 5505024 | tf_op jit(solution)/shard_map/pallas_call | solution.py:147
  95.2 1.0 pad_maximum_fusion
  96.2 0.1 reshape.86
  96.4 0.7 rev.13
  97.1 0.2 slice.45
  97.3 0.2 rev.14
  97.5 0.1 slice.48
  97.6 0.1 copy.42
  97.8 0.9 copy.45
  98.6 0.1 fusion.10
  98.7 0.5 fusion.7
  99.2 0.1 convert_element_type.50
  99.4 0.9 copy.40
  100.3 5.1 %all-to-all-start.2 = ((bf16[32,16,2,128]{3,2,1,0:T(2,128)(2,1)}), bf16[32,16,2,128]{3,2,1,0:T(2,128)(2,1)S(1)}, u32[]{:S(2)}, u32[]{:S(2)}) async-start(bf16[32,16,2,128]{3,2,1,0:T(2,128)(2,1)} %copy.40), calls=%async_computation.2 | async-start | bytes 524288 | tf_op jit(solution)/shard_map/all_to_all | solution.py:238
  105.4 0.1 multiply_rsqrt_fusion
  105.5 10.5 %all-to-all-done.2 = bf16[32,16,2,128]{3,2,1,0:T(2,128)(2,1)S(1)} async-done(((bf16[32,16,2,128]{3,2,1,0:T(2,128)(2,1)}), bf16[32,16,2,128]{3,2,1,0:T(2,128)(2,1)S(1)}, u32[]{:S(2)}, u32[]{:S(2)}) %all-to-all-start.2) | async-done | bytes 262176 | tf_op jit(solution)/shard_map/all_to_all | solution.py:238
  116.0 3.7 %convolution_multiply_fusion = f32[128,2,512]{2,0,1:T(8,128)S(1)} fusion(bf16[1024,128,1]{1,0,2:T(8,128)(2,1)S(1)} %bitcast.31, f32[2,512,1024]{2,1,0:T(8,128)} %constant.51, f32[128]{0:T(128)S(1)} %multiply_rsqrt_fusion), kind=kOutput, calls=%fused_computation.10 | convolution fusion | flops 805437440 | bytes 4981248 | tf_op jit(solution)/shard_map/dot_general | solution.py:246
  119.7 1.2 copy.43
  (26 shorter events, 0.2 us)
Async XLA Ops:
  6.5 33.5 %all-to-all-start = ((bf16[32,8,16,128]{3,2,1,0:T(8,128)(2,1)}), bf16[32,8,16,128]{3,2,1,0:T(8,128)(2,1)S(1)}, u32[]{:S(2)}, u32[]{:S(2)}) async-start(bf16[32,8,16,128]{3,2,1,0:T(8,128)(2,1)} %squeeze_reshape.6), calls=%async_computation | async-start | bytes 2097152 | tf_op jit(solution)/shard_map/all_to_all | solution.py:226
  19.0 1.3 %copy-start.3 = (s32[1024]{0:T(1024)S(1)}, s32[1024]{0:T(1024)}, u32[]{:S(2)}) copy-start(s32[1024]{0:T(1024)} %param.8) | copy-start | bytes 12292
  19.0 1.5 %copy-start.4 = (s32[1024]{0:T(1024)S(1)}, s32[1024]{0:T(1024)}, u32[]{:S(2)}) copy-start(s32[1024]{0:T(1024)} %param.9) | copy-start | bytes 12292
  40.0 3.9 %copy-start = (bf16[32,8,16,128]{3,2,1,0:T(8,128)(2,1)}, bf16[32,8,16,128]{3,2,1,0:T(8,128)(2,1)S(1)}, u32[]{:S(2)}) copy-start(bf16[32,8,16,128]{3,2,1,0:T(8,128)(2,1)S(1)} %all-to-all-done) | copy-start | bytes 3145732
  40.0 29.9 %all-to-all-start.1 = ((bf16[32,8,16,128]{3,2,1,0:T(8,128)(2,1)}), bf16[32,8,16,128]{3,2,1,0:T(8,128)(2,1)S(1)}, u32[]{:S(2)}, u32[]{:S(2)}) async-start(bf16[32,8,16,128]{3,2,1,0:T(8,128)(2,1)} %squeeze_reshape.7), calls=%async_computation.1 | async-start | bytes 2097152 | tf_op jit(solution)/shard_map/all_to_all | solution.py:226
  69.9 1.0 copy-start.1
  70.8 24.4 %copy-start.2 = (f32[8,2,16,256]{3,2,1,0:T(8,128)S(1)}, f32[8,2,16,256]{3,2,1,0:T(8,128)}, u32[]{:S(2)}) copy-start(f32[8,2,16,256]{3,2,1,0:T(8,128)} %get-tuple-element.10) | copy-start | bytes 786436
  95.2 2.1 %copy-start.5 = (f32[16,256]{1,0:T(8,128)S(1)}, f32[16,256]{1,0:T(8,128)}, u32[]{:S(2)}) copy-start(f32[16,256]{1,0:T(8,128)} %get-tuple-element.14) | copy-start | bytes 49156
  96.2 2.5 %copy-start.6 = (f32[2]{0:T(128)S(1)}, f32[2]{0:T(128)}, u32[]{:S(2)}) copy-start(f32[2]{0:T(128)} %constant.44.clone) | copy-start | bytes 28
  100.3 15.7 %all-to-all-start.2 = ((bf16[32,16,2,128]{3,2,1,0:T(2,128)(2,1)}), bf16[32,16,2,128]{3,2,1,0:T(2,128)(2,1)S(1)}, u32[]{:S(2)}, u32[]{:S(2)}) async-start(bf16[32,16,2,128]{3,2,1,0:T(2,128)(2,1)} %copy.40), calls=%async_computation.2 | async-start | bytes 524288 | tf_op jit(solution)/shard_map/all_to_all | solution.py:238

commit v14 on v13

--- a/solution.py
+++ b/solution.py
@@ -120,6 +120,24 @@
         diag_pairs(g, right, upper, upper_half, write_vis)
 
 
+def counts_kernel(fm_ref, fmr_ref, n_ref):
+    row_at = lax.broadcasted_iota(jnp.int32, (FEEDS, FEEDS), 0)
+    col_at = lax.broadcasted_iota(jnp.int32, (FEEDS, FEEDS), 1)
+    upper = col_at >= row_at
+
+    def write_count(slot, value):
+        n_ref[pl.ds(slot, 1), :] = value
+
+    diag_pairs(fm_ref[...], fmr_ref[...], upper, upper[:HALF, :HALF], write_count)
+
+
+def stack_counts(fm, fmr):
+    return pl.pallas_call(
+        counts_kernel,
+        out_shape=jax.ShapeDtypeStruct((CYL * CYL, FEEDS), jnp.float32),
+    )(fm, fmr)
+
+
 def correlate(blocks, pt, ptr, rm, fm=None, fmr=None):
     wide_parts, tm_parts, local_channels, rows_each, inputs_each = blocks.shape
     with_counts = fm is not None
@@ -216,20 +234,17 @@
         rm[partner, r] = -1.0 if part_at[r] == 0 else 1.0
     rm = jnp.asarray(rm, dtype=jnp.bfloat16)
 
+    count_sums = stack_counts(fm, fmr)
     sums = []
     for j in range(chunks):
         spectra_j = spectra[j]
         if j >= 2:
             spectra_j, _ = lax.optimization_barrier((spectra_j, sums[j - 2]))
         elif j == 1:
-            spectra_j, pt, ptr, fm, fmr = lax.optimization_barrier((spectra_j, pt, ptr, fm, fmr))
+            spectra_j, pt, ptr, count_sums = lax.optimization_barrier((spectra_j, pt, ptr, count_sums))
         turned = lax.all_to_all(spectra_j, ("wide", "tm"), 0, 0, tiled=True)
         blk = turned.reshape(wide_parts, tm_parts, chunk_channels, 2 * frames_here, inputs_here)
-        if j == 0:
-            first, count_sums = correlate(blk, pt, ptr, rm, fm, fmr)
-            sums.append(first)
-        else:
-            sums.append(correlate(blk, pt, ptr, rm)[0])
+        sums.append(correlate(blk, pt, ptr, rm)[0])
     sums = jnp.concatenate(sums, axis=0)
     conj_sign = jnp.array([1.0, -1.0], jnp.float32)[None, :, None, None, None]
     vis = unskew(sums, conj_sign)

time: 121 us -> 120 us (level)
  waiting for transfers between devices: 25.4 us -> 23.5 us
  Pallas kernels: 49.8 us -> 51.2 us
    pallas_call x0 -> x1, Pallas kernels: none -> 2.5 us  [stack_counts(): pl.pallas_call(counts_kernel, out_shape=jax.ShapeDtypeStruct((CYL * CYL,...]
    all_to_all x2, waiting for transfers between devices: 15 us -> 13 us  [body(): turned = lax.all_to_all(spectra_j, ('wide', 'tm'), 0, 0, tiled=True)]
  transfers between devices with their start and end apart: 3 -> 3, of which waited for: 3 -> 3; matrix products, arithmetic and copies ran while one was open for 10% -> 10% of each run, Pallas kernels for 21% -> 22%
where the time goes in v14:
time: 120 us
  Pallas kernels  51.2 us (43%)
  waiting for transfers between devices  23.5 us (20%)
  starting transfers between devices  15.6 us (13%)
  matrix products  14 us (12%)
  local copies, waits for them, and re-layouts  8.33 us (7%)
  other arithmetic  6.87 us (6%)
    pallas_call x2, Pallas kernels, correlate(): pl.pallas_call(functools.partial(correlate_kernel, with_counts=with_count...  48.7 us
    all_to_all x2, waiting for transfers between devices, body(): turned = lax.all_to_all(spectra_j, ('wide', 'tm'), 0, 0, tiled=True)  13 us
    all_to_all x2, starting transfers between devices, body(): turned = lax.all_to_all(spectra_j, ('wide', 'tm'), 0, 0, tiled=True)  11.1 us
    all_to_all x1, waiting for transfers between devices, body(): lax.all_to_all(send.astype(jnp.bfloat16), ('wide', 'tm'), 0, 0, tiled=True)  10.5 us
    dot_general x2, matrix products, channelize(): lax.dot_general(rows, flattened, NT, preferred_element_type=jnp.float32)  10.4 us
    all_to_all x1, starting transfers between devices, body(): lax.all_to_all(send.astype(jnp.bfloat16), ('wide', 'tm'), 0, 0, tiled=True)  4.5 us
    dot_general x1, matrix products, body(): lax.dot_general(stacked_in, delay, (((0,), (0,)), ((), ())), precision=la...  3.67 us
    select_n x1, other arithmetic, body(): jnp.where(wiring_rev[:, None] == source[None, :], flags[None, :], jnp.bfl...  2.6 us
  transfers between devices with their start and end apart: 3, of which 3 were waited for; matrix products, arithmetic and copies ran while one was open for 10% of the time, Pallas kernels for 22%

profile of v14, /device:TPU:0, one launch (start us, length us, event | category | flops | bytes accessed | tf_op | source)
XLA Modules:
  0.0 119.7 jit_solution(17511041284985751741)
XLA Ops:
  0.0 5.2 %convolution_convert_fusion.1 = bf16[512,1024]{1,0:T(8,128)(2,1)S(1)} fusion(bf16[512,2048]{1,0:T(8,128)(2,1)} %constant.47, bf16[1024,2048]{1,0:T(8,128)(2,1)} %bitcast.43), kind=kOutput, calls=%fused_computation.9 | convolution fusion | flops 2148007936 | bytes 7340032 | tf_op jit(solution)/shard_map/dot_general | solution.py:206
  5.2 1.3 %squeeze_reshape.6 = bf16[32,8,16,128]{3,2,1,0:T(8,128)(2,1)} reshape(bf16[512,1024]{1,0:T(8,128)(2,1)S(1)} %convolution_convert_fusion.1) | data formatting | bytes 2097152 | tf_op jit(solution)/shard_map/squeeze;reshape | solution.py:209
  6.5 7.3 %all-to-all-start = ((bf16[32,8,16,128]{3,2,1,0:T(8,128)(2,1)}), bf16[32,8,16,128]{3,2,1,0:T(8,128)(2,1)S(1)}, u32[]{:S(2)}, u32[]{:S(2)}) async-start(bf16[32,8,16,128]{3,2,1,0:T(8,128)(2,1)} %squeeze_reshape.6), calls=%async_computation | async-start | bytes 2097152 | tf_op jit(solution)/shard_map/all_to_all | solution.py:245
  13.8 5.2 %convolution_convert_fusion = bf16[512,1024]{1,0:T(8,128)(2,1)S(1)} fusion(bf16[512,2048]{1,0:T(8,128)(2,1)} %constant.49, bf16[1024,2048]{1,0:T(8,128)(2,1)} %bitcast.44), kind=kOutput, calls=%fused_computation.8 | convolution fusion | flops 2148007936 | bytes 7340032 | tf_op jit(solution)/shard_map/dot_general | solution.py:206
  19.0 1.3 %squeeze_reshape.7 = bf16[32,8,16,128]{3,2,1,0:T(8,128)(2,1)} reshape(bf16[512,1024]{1,0:T(8,128)(2,1)S(1)} %convolution_convert_fusion) | data formatting | bytes 2097152 | tf_op jit(solution)/shard_map/squeeze;reshape | solution.py:212
  20.3 0.2 rev.12
  20.5 1.4 %fusion.2 = (bf16[1024]{0:T(1024)(128)(2,1)S(1)}, bf16[1024]{0:T(1024)(128)(2,1)S(1)}) fusion(s32[1024]{0:T(1024)S(1)} %bitcast.38, bf16[1024]{0:T(1024)(128)(2,1)S(1)} %convert_element_type.45, s32[1024]{0:T(1024)S(1)} %copy-done.4), kind=kLoop, calls=%fused_computation.6 | loop fusion | flops 6289408 | bytes 14336 | tf_op jit(solution)/shard_map/reduce_sum | solution.py:222
  21.9 1.1 broadcast_select_fusion
  23.1 2.5 %shard_map.74 = f32[16,256]{1,0:T(8,128)} custom-call(bf16[1024,128]{1,0:T(8,128)(2,1)} %get-tuple-element.20.fm_ref, bf16[1024,128]{1,0:T(8,128)(2,1)} %get-tuple-element.19.fmr_ref), custom_call_target="tpu_custom_call" | custom-call | tf_op jit(solution)/shard_map/pallas_call | solution.py:135
  25.6 2.6 %compare_select_fusion = (bf16[8,1024,128]{2,1,0:T(8,128)(2,1)}, bf16[8,1024,128]{2,1,0:T(8,128)(2,1)}) fusion(s32[8,128]{1,0:T(8,128)S(1)} %multiply_add_fusion, s32[1024]{0:T(1024)S(1)} %bitcast.39, bf16[8,128]{1,0:T(8,128)(2,1)S(1)} %convert_bitcast_fusion, s32[1024]{0:T(1024)S(1)} %copy-done.4), kind=kLoop, calls=%fused_computation.4 | loop fusion | flops 4194304 | bytes 4208640 | tf_op jit(solution)/shard_map/jit(_where)/select_n | solution.py:219
  28.2 11.8 %all-to-all-done = bf16[32,8,16,128]{3,2,1,0:T(8,128)(2,1)S(1)} async-done(((bf16[32,8,16,128]{3,2,1,0:T(8,128)(2,1)}), bf16[32,8,16,128]{3,2,1,0:T(8,128)(2,1)S(1)}, u32[]{:S(2)}, u32[]{:S(2)}) %all-to-all-start) | async-done | bytes 1048608 | tf_op jit(solution)/shard_map/all_to_all | solution.py:245
  40.0 3.8 %all-to-all-start.1 = ((bf16[32,8,16,128]{3,2,1,0:T(8,128)(2,1)}), bf16[32,8,16,128]{3,2,1,0:T(8,128)(2,1)S(1)}, u32[]{:S(2)}, u32[]{:S(2)}) async-start(bf16[32,8,16,128]{3,2,1,0:T(8,128)(2,1)} %squeeze_reshape.7), calls=%async_computation.1 | async-start | bytes 2097152 | tf_op jit(solution)/shard_map/all_to_all | solution.py:245
  43.8 0.2 rev.14
  44.1 0.1 copy.42
  44.3 0.1 fusion.10
  44.4 24.3 %shard_map.73 = f32[8,2,16,256]{3,2,1,0:T(8,128)} custom-call(bf16[8,4,8,16,128]{4,3,2,1,0:T(8,128)(2,1)} %bitcast.32, bf16[8,1024,128]{2,1,0:T(8,128)(2,1)} %get-tuple-element.10.refs_1_, bf16[8,1024,128]{2,1,0:T(8,128)(2,1)} %get-tuple-element.11.refs_2_, bf16[64,64]{1,0:T(8,128)(2,1)} %constant.43.clone.refs_3_), custom_call_target="tpu_custom_call" | custom-call | flops 3556769792 | bytes 5505024 | tf_op jit(solution)/shard_map/pallas_call | solution.py:165
  68.7 1.2 all-to-all-done.1
  69.9 1.0 copy-done.1
  70.8 24.4 %shard_map.75 = f32[8,2,16,256]{3,2,1,0:T(8,128)} custom-call(bf16[8,4,8,16,128]{4,3,2,1,0:T(8,128)(2,1)} %bitcast.33, bf16[8,1024,128]{2,1,0:T(8,128)(2,1)} %get-tuple-element.10.refs_1_, bf16[8,1024,128]{2,1,0:T(8,128)(2,1)} %get-tuple-element.11.refs_2_, bf16[64,64]{1,0:T(8,128)(2,1)} %constant.43.clone.refs_3_), custom_call_target="tpu_custom_call" | custom-call | flops 3556769792 | bytes 5505024 | tf_op jit(solution)/shard_map/pallas_call | solution.py:165
  95.2 1.0 pad_maximum_fusion
  96.2 0.1 reshape.86
  96.4 0.7 rev.13
  97.1 0.2 slice.45
  97.3 0.9 copy.45
  98.2 0.5 fusion.7
  98.7 0.1 convert_element_type.50
  98.8 0.9 copy.40
  99.7 4.5 %all-to-all-start.2 = ((bf16[32,16,2,128]{3,2,1,0:T(2,128)(2,1)}), bf16[32,16,2,128]{3,2,1,0:T(2,128)(2,1)S(1)}, u32[]{:S(2)}, u32[]{:S(2)}) async-start(bf16[32,16,2,128]{3,2,1,0:T(2,128)(2,1)} %copy.40), calls=%async_computation.2 | async-start | bytes 524288 | tf_op jit(solution)/shard_map/all_to_all | solution.py:253
  104.3 0.1 multiply_rsqrt_fusion
  104.4 10.5 %all-to-all-done.2 = bf16[32,16,2,128]{3,2,1,0:T(2,128)(2,1)S(1)} async-done(((bf16[32,16,2,128]{3,2,1,0:T(2,128)(2,1)}), bf16[32,16,2,128]{3,2,1,0:T(2,128)(2,1)S(1)}, u32[]{:S(2)}, u32[]{:S(2)}) %all-to-all-start.2) | async-done | bytes 262176 | tf_op jit(solution)/shard_map/all_to_all | solution.py:253
  114.8 3.7 %convolution_multiply_fusion = f32[128,2,512]{2,0,1:T(8,128)S(1)} fusion(bf16[1024,128,1]{1,0,2:T(8,128)(2,1)S(1)} %bitcast.31, f32[2,512,1024]{2,1,0:T(8,128)} %constant.51, f32[128]{0:T(128)S(1)} %multiply_rsqrt_fusion), kind=kOutput, calls=%fused_computation.10 | convolution fusion | flops 805437440 | bytes 4981248 | tf_op jit(solution)/shard_map/dot_general | solution.py:261
  118.5 1.2 %copy.43 = f32[128,2,512]{2,1,0:T(2,128)} copy(f32[128,2,512]{2,0,1:T(8,128)S(1)} %convolution_multiply_fusion) | data formatting | bytes 1048576 | tf_op jit(solution)/shard_map/mul | solution.py:266
  (27 shorter events, 0.2 us)
Async XLA Ops:
  6.5 33.5 %all-to-all-start = ((bf16[32,8,16,128]{3,2,1,0:T(8,128)(2,1)}), bf16[32,8,16,128]{3,2,1,0:T(8,128)(2,1)S(1)}, u32[]{:S(2)}, u32[]{:S(2)}) async-start(bf16[32,8,16,128]{3,2,1,0:T(8,128)(2,1)} %squeeze_reshape.6), calls=%async_computation | async-start | bytes 2097152 | tf_op jit(solution)/shard_map/all_to_all | solution.py:245
  19.0 1.3 %copy-start.4 = (s32[1024]{0:T(1024)S(1)}, s32[1024]{0:T(1024)}, u32[]{:S(2)}) copy-start(s32[1024]{0:T(1024)} %param.8) | copy-start | bytes 12292
  19.0 1.5 %copy-start.5 = (s32[1024]{0:T(1024)S(1)}, s32[1024]{0:T(1024)}, u32[]{:S(2)}) copy-start(s32[1024]{0:T(1024)} %param.9) | copy-start | bytes 12292
  28.2 15.6 %copy-start.3 = (f32[16,256]{1,0:T(8,128)S(1)}, f32[16,256]{1,0:T(8,128)}, u32[]{:S(2)}) copy-start(f32[16,256]{1,0:T(8,128)} %shard_map.74) | copy-start | bytes 49156
  40.0 4.3 %copy-start = (bf16[32,8,16,128]{3,2,1,0:T(8,128)(2,1)}, bf16[32,8,16,128]{3,2,1,0:T(8,128)(2,1)S(1)}, u32[]{:S(2)}) copy-start(bf16[32,8,16,128]{3,2,1,0:T(8,128)(2,1)S(1)} %all-to-all-done) | copy-start | bytes 3145732
  40.0 29.9 %all-to-all-start.1 = ((bf16[32,8,16,128]{3,2,1,0:T(8,128)(2,1)}), bf16[32,8,16,128]{3,2,1,0:T(8,128)(2,1)S(1)}, u32[]{:S(2)}, u32[]{:S(2)}) async-start(bf16[32,8,16,128]{3,2,1,0:T(8,128)(2,1)} %squeeze_reshape.7), calls=%async_computation.1 | async-start | bytes 2097152 | tf_op jit(solution)/shard_map/all_to_all | solution.py:245
  69.9 1.0 copy-start.1
  70.8 24.4 %copy-start.2 = (f32[8,2,16,256]{3,2,1,0:T(8,128)S(1)}, f32[8,2,16,256]{3,2,1,0:T(8,128)}, u32[]{:S(2)}) copy-start(f32[8,2,16,256]{3,2,1,0:T(8,128)} %shard_map.73) | copy-start | bytes 786436
  95.2 3.0 %copy-start.6 = (f32[2]{0:T(128)S(1)}, f32[2]{0:T(128)}, u32[]{:S(2)}) copy-start(f32[2]{0:T(128)} %constant.44.clone) | copy-start | bytes 28
  99.7 15.1 %all-to-all-start.2 = ((bf16[32,16,2,128]{3,2,1,0:T(2,128)(2,1)}), bf16[32,16,2,128]{3,2,1,0:T(2,128)(2,1)S(1)}, u32[]{:S(2)}, u32[]{:S(2)}) async-start(bf16[32,16,2,128]{3,2,1,0:T(2,128)(2,1)} %copy.40), calls=%async_computation.2 | async-start | bytes 524288 | tf_op jit(solution)/shard_map/all_to_all | solution.py:253

commit v15 on v14

--- a/solution.py
+++ b/solution.py
@@ -251,16 +251,15 @@
     local_baselines = NBASE // devices
     send = vis.reshape(local_channels, 2, devices, local_baselines).transpose(2, 0, 1, 3)
     received = lax.all_to_all(send.astype(jnp.bfloat16), ("wide", "tm"), 0, 0, tiled=True)
-    stacked_in = received.astype(jnp.float32).reshape(CH * 2, local_baselines)
+    stacked_in = received.reshape(CH * 2, local_baselines)
     device_position = lax.axis_index("wide") * tm_parts + lax.axis_index("tm")
     global_stack_counts = unskew(count_sums, 1.0).reshape(NBASE)
     local_stack_counts = lax.dynamic_slice_in_dim(
         global_stack_counts, device_position * local_baselines, local_baselines
     )
-    delay = delay_matrix_const(CH)
+    delay = delay_matrix_const(CH).astype(jnp.bfloat16)
     spectra_out = lax.dot_general(
-        stacked_in, delay, (((0,), (0,)), ((), ())), precision=lax.Precision.HIGH,
-        preferred_element_type=jnp.float32,
+        stacked_in, delay, (((0,), (0,)), ((), ())), preferred_element_type=jnp.float32,
     )
     weight = 1.0 / jnp.sqrt(frames_all * CH * jnp.maximum(local_stack_counts, 1.0))
     return spectra_out.reshape(local_baselines, 2, CH) * weight[:, None, None]

time: 120 us -> 119 us (level)
  matrix products: 14 us -> 11.2 us
    dot_general x1, matrix products: 3.67 us -> 0.83 us  [body(): lax.dot_general(stacked_in, delay, (((0,), (0,)), ((), ())), preferred_el...]
  transfers between devices with their start and end apart: 3 -> 3, of which waited for: 3 -> 3; matrix products, arithmetic and copies ran while one was open for 10% -> 10% of each run, Pallas kernels for 22% -> 23%
where the time goes in v15:
time: 119 us
  Pallas kernels  51.2 us (43%)
  waiting for transfers between devices  23.6 us (20%)
  starting transfers between devices  15.6 us (13%)
  matrix products  11.2 us (9%)
  local copies, waits for them, and re-layouts  9.04 us (8%)
  other arithmetic  7.77 us (7%)
    pallas_call x2, Pallas kernels, correlate(): pl.pallas_call(functools.partial(correlate_kernel, with_counts=with_count...  48.7 us
    all_to_all x2, waiting for transfers between devices, body(): turned = lax.all_to_all(spectra_j, ('wide', 'tm'), 0, 0, tiled=True)  13.1 us
    all_to_all x2, starting transfers between devices, body(): turned = lax.all_to_all(spectra_j, ('wide', 'tm'), 0, 0, tiled=True)  11.1 us
    all_to_all x1, waiting for transfers between devices, body(): lax.all_to_all(send.astype(jnp.bfloat16), ('wide', 'tm'), 0, 0, tiled=True)  10.5 us
    dot_general x2, matrix products, channelize(): lax.dot_general(rows, flattened, NT, preferred_element_type=jnp.float32)  10.4 us
    all_to_all x1, starting transfers between devices, body(): lax.all_to_all(send.astype(jnp.bfloat16), ('wide', 'tm'), 0, 0, tiled=True)  4.49 us
    select_n x1, other arithmetic, body(): jnp.where(wiring_rev[:, None] == source[None, :], flags[None, :], jnp.bfl...  2.56 us
    pallas_call x1, Pallas kernels, stack_counts(): pl.pallas_call(counts_kernel, out_shape=jax.ShapeDtypeStruct((CYL * CYL,...  2.5 us
  transfers between devices with their start and end apart: 3, of which 3 were waited for; matrix products, arithmetic and copies ran while one was open for 10% of the time, Pallas kernels for 23%

profile of v15, /device:TPU:0, one launch (start us, length us, event | category | flops | bytes accessed | tf_op | source)
XLA Modules:
  0.0 118.5 jit_solution(17090986429013854317)
XLA Ops:
  0.0 5.2 %convolution_convert_fusion.1 = bf16[512,1024]{1,0:T(8,128)(2,1)S(1)} fusion(bf16[512,2048]{1,0:T(8,128)(2,1)} %constant.47, bf16[1024,2048]{1,0:T(8,128)(2,1)} %bitcast.43), kind=kOutput, calls=%fused_computation.9 | convolution fusion | flops 2148007936 | bytes 7340032 | tf_op jit(solution)/shard_map/dot_general | solution.py:206
  5.2 1.3 %squeeze_reshape.6 = bf16[32,8,16,128]{3,2,1,0:T(8,128)(2,1)} reshape(bf16[512,1024]{1,0:T(8,128)(2,1)S(1)} %convolution_convert_fusion.1) | data formatting | bytes 2097152 | tf_op jit(solution)/shard_map/squeeze;reshape | solution.py:209
  6.5 7.3 %all-to-all-start = ((bf16[32,8,16,128]{3,2,1,0:T(8,128)(2,1)}), bf16[32,8,16,128]{3,2,1,0:T(8,128)(2,1)S(1)}, u32[]{:S(2)}, u32[]{:S(2)}) async-start(bf16[32,8,16,128]{3,2,1,0:T(8,128)(2,1)} %squeeze_reshape.6), calls=%async_computation | async-start | bytes 2097152 | tf_op jit(solution)/shard_map/all_to_all | solution.py:245
  13.8 5.2 %convolution_convert_fusion = bf16[512,1024]{1,0:T(8,128)(2,1)S(1)} fusion(bf16[512,2048]{1,0:T(8,128)(2,1)} %constant.49, bf16[1024,2048]{1,0:T(8,128)(2,1)} %bitcast.44), kind=kOutput, calls=%fused_computation.8 | convolution fusion | flops 2148007936 | bytes 7340032 | tf_op jit(solution)/shard_map/dot_general | solution.py:206
  19.0 1.3 %squeeze_reshape.7 = bf16[32,8,16,128]{3,2,1,0:T(8,128)(2,1)} reshape(bf16[512,1024]{1,0:T(8,128)(2,1)S(1)} %convolution_convert_fusion) | data formatting | bytes 2097152 | tf_op jit(solution)/shard_map/squeeze;reshape | solution.py:212
  20.3 0.2 rev.12
  20.5 1.4 %fusion.2 = (bf16[1024]{0:T(1024)(128)(2,1)S(1)}, bf16[1024]{0:T(1024)(128)(2,1)S(1)}) fusion(s32[1024]{0:T(1024)S(1)} %bitcast.38, bf16[1024]{0:T(1024)(128)(2,1)S(1)} %convert_element_type.47, s32[1024]{0:T(1024)S(1)} %copy-done.5), kind=kLoop, calls=%fused_computation.6 | loop fusion | flops 6289408 | bytes 14336 | tf_op jit(solution)/shard_map/reduce_sum | solution.py:222
  21.9 1.1 broadcast_select_fusion
  23.0 2.5 %shard_map.74 = f32[16,256]{1,0:T(8,128)} custom-call(bf16[1024,128]{1,0:T(8,128)(2,1)} %get-tuple-element.20.fm_ref, bf16[1024,128]{1,0:T(8,128)(2,1)} %get-tuple-element.19.fmr_ref), custom_call_target="tpu_custom_call" | custom-call | tf_op jit(solution)/shard_map/pallas_call | solution.py:135
  25.6 2.6 %compare_select_fusion = (bf16[8,1024,128]{2,1,0:T(8,128)(2,1)}, bf16[8,1024,128]{2,1,0:T(8,128)(2,1)}) fusion(s32[8,128]{1,0:T(8,128)S(1)} %multiply_add_fusion, s32[1024]{0:T(1024)S(1)} %bitcast.39, bf16[8,128]{1,0:T(8,128)(2,1)S(1)} %convert_bitcast_fusion, s32[1024]{0:T(1024)S(1)} %copy-done.5), kind=kLoop, calls=%fused_computation.4 | loop fusion | flops 4194304 | bytes 4208640 | tf_op jit(solution)/shard_map/jit(_where)/select_n | solution.py:219
  28.1 11.9 %all-to-all-done = bf16[32,8,16,128]{3,2,1,0:T(8,128)(2,1)S(1)} async-done(((bf16[32,8,16,128]{3,2,1,0:T(8,128)(2,1)}), bf16[32,8,16,128]{3,2,1,0:T(8,128)(2,1)S(1)}, u32[]{:S(2)}, u32[]{:S(2)}) %all-to-all-start) | async-done | bytes 1048608 | tf_op jit(solution)/shard_map/all_to_all | solution.py:245
  40.0 3.8 %all-to-all-start.1 = ((bf16[32,8,16,128]{3,2,1,0:T(8,128)(2,1)}), bf16[32,8,16,128]{3,2,1,0:T(8,128)(2,1)S(1)}, u32[]{:S(2)}, u32[]{:S(2)}) async-start(bf16[32,8,16,128]{3,2,1,0:T(8,128)(2,1)} %squeeze_reshape.7), calls=%async_computation.1 | async-start | bytes 2097152 | tf_op jit(solution)/shard_map/all_to_all | solution.py:245
  43.8 0.2 rev.14
  44.1 0.1 copy.42
  44.3 0.1 fusion.10
  44.4 24.3 %shard_map.73 = f32[8,2,16,256]{3,2,1,0:T(8,128)} custom-call(bf16[8,4,8,16,128]{4,3,2,1,0:T(8,128)(2,1)} %bitcast.32, bf16[8,1024,128]{2,1,0:T(8,128)(2,1)} %get-tuple-element.10.refs_1_, bf16[8,1024,128]{2,1,0:T(8,128)(2,1)} %get-tuple-element.11.refs_2_, bf16[64,64]{1,0:T(8,128)(2,1)} %constant.43.clone.refs_3_), custom_call_target="tpu_custom_call" | custom-call | flops 3556769792 | bytes 5505024 | tf_op jit(solution)/shard_map/pallas_call | solution.py:165
  68.7 1.2 all-to-all-done.1
  69.9 1.0 copy-done.2
  70.8 24.4 %shard_map.75 = f32[8,2,16,256]{3,2,1,0:T(8,128)} custom-call(bf16[8,4,8,16,128]{4,3,2,1,0:T(8,128)(2,1)} %bitcast.33, bf16[8,1024,128]{2,1,0:T(8,128)(2,1)} %get-tuple-element.10.refs_1_, bf16[8,1024,128]{2,1,0:T(8,128)(2,1)} %get-tuple-element.11.refs_2_, bf16[64,64]{1,0:T(8,128)(2,1)} %constant.43.clone.refs_3_), custom_call_target="tpu_custom_call" | custom-call | flops 3556769792 | bytes 5505024 | tf_op jit(solution)/shard_map/pallas_call | solution.py:165
  95.2 1.0 pad_maximum_fusion
  96.2 0.1 reshape.86
  96.4 0.7 rev.13
  97.1 0.9 slice.45
  98.0 0.9 copy.45
  98.9 1.5 %fusion.7 = bf16[16,2,4,4,256]{4,3,2,1,0:T(4,128)(2,1)S(1)} fusion(f32[16,2,4,4,256]{4,3,2,1,0:T(4,128)S(1)} %rev.13, f32[16,2,4,4,255]{4,3,2,1,0:T(4,128)S(1)} %bitcast.29, f32[16,2,4,4,1]{4,3,2,1,0:T(4,128)} %slice.45, f32[4,4,256]{2,1,0:T(4,128)S(1)} %get-tuple-element.18, f32[2]{0:T(128)S(1)} %copy-done.7, f32[16,2,4,4]{3,2,1,0:T(4,128)S(1)} %bitcast.35, ...), kind=kLoop, calls=%fused_computation.16 | loop fusion | flops 786432 | bytes 1333512 | tf_op jit(solution)/shard_map/convert_element_type | solution.py:253
  100.4 0.1 convert_element_type.52
  100.5 0.9 copy.40
  101.4 4.5 %all-to-all-start.2 = ((bf16[32,16,2,128]{3,2,1,0:T(2,128)(2,1)}), bf16[32,16,2,128]{3,2,1,0:T(2,128)(2,1)S(1)}, u32[]{:S(2)}, u32[]{:S(2)}) async-start(bf16[32,16,2,128]{3,2,1,0:T(2,128)(2,1)} %copy.40), calls=%async_computation.2 | async-start | bytes 524288 | tf_op jit(solution)/shard_map/all_to_all | solution.py:253
  105.9 0.1 multiply_rsqrt_fusion
  106.0 10.5 %all-to-all-done.2 = bf16[32,16,2,128]{3,2,1,0:T(2,128)(2,1)S(1)} async-done(((bf16[32,16,2,128]{3,2,1,0:T(2,128)(2,1)}), bf16[32,16,2,128]{3,2,1,0:T(2,128)(2,1)S(1)}, u32[]{:S(2)}, u32[]{:S(2)}) %all-to-all-start.2) | async-done | bytes 262176 | tf_op jit(solution)/shard_map/all_to_all | solution.py:253
  116.5 0.8 convolution_multiply_fusion
  117.3 1.2 %copy.43 = f32[128,2,512]{2,1,0:T(2,128)} copy(f32[128,2,512]{2,0,1:T(8,128)S(1)} %convolution_multiply_fusion) | data formatting | bytes 1048576 | tf_op jit(solution)/shard_map/mul | solution.py:265
  (29 shorter events, 0.2 us)
Async XLA Ops:
  6.5 33.5 %all-to-all-start = ((bf16[32,8,16,128]{3,2,1,0:T(8,128)(2,1)}), bf16[32,8,16,128]{3,2,1,0:T(8,128)(2,1)S(1)}, u32[]{:S(2)}, u32[]{:S(2)}) async-start(bf16[32,8,16,128]{3,2,1,0:T(8,128)(2,1)} %squeeze_reshape.6), calls=%async_computation | async-start | bytes 2097152 | tf_op jit(solution)/shard_map/all_to_all | solution.py:245
  19.0 1.3 %copy-start.5 = (s32[1024]{0:T(1024)S(1)}, s32[1024]{0:T(1024)}, u32[]{:S(2)}) copy-start(s32[1024]{0:T(1024)} %param.8) | copy-start | bytes 12292
  19.0 1.5 %copy-start.6 = (s32[1024]{0:T(1024)S(1)}, s32[1024]{0:T(1024)}, u32[]{:S(2)}) copy-start(s32[1024]{0:T(1024)} %param.9) | copy-start | bytes 12292
  28.1 15.7 %copy-start.4 = (f32[16,256]{1,0:T(8,128)S(1)}, f32[16,256]{1,0:T(8,128)}, u32[]{:S(2)}) copy-start(f32[16,256]{1,0:T(8,128)} %shard_map.74) | copy-start | bytes 49156
  40.0 4.3 %copy-start.1 = (bf16[32,8,16,128]{3,2,1,0:T(8,128)(2,1)}, bf16[32,8,16,128]{3,2,1,0:T(8,128)(2,1)S(1)}, u32[]{:S(2)}) copy-start(bf16[32,8,16,128]{3,2,1,0:T(8,128)(2,1)S(1)} %all-to-all-done) | copy-start | bytes 3145732
  40.0 29.9 %all-to-all-start.1 = ((bf16[32,8,16,128]{3,2,1,0:T(8,128)(2,1)}), bf16[32,8,16,128]{3,2,1,0:T(8,128)(2,1)S(1)}, u32[]{:S(2)}, u32[]{:S(2)}) async-start(bf16[32,8,16,128]{3,2,1,0:T(8,128)(2,1)} %squeeze_reshape.7), calls=%async_computation.1 | async-start | bytes 2097152 | tf_op jit(solution)/shard_map/all_to_all | solution.py:245
  69.9 1.0 copy-start.2
  70.8 24.4 %copy-start.3 = (f32[8,2,16,256]{3,2,1,0:T(8,128)S(1)}, f32[8,2,16,256]{3,2,1,0:T(8,128)}, u32[]{:S(2)}) copy-start(f32[8,2,16,256]{3,2,1,0:T(8,128)} %shard_map.73) | copy-start | bytes 786436
  95.2 3.7 %copy-start.7 = (f32[2]{0:T(128)S(1)}, f32[2]{0:T(128)}, u32[]{:S(2)}) copy-start(f32[2]{0:T(128)} %constant.44.clone) | copy-start | bytes 28
  98.0 18.5 %copy-start = (bf16[2,512,1024]{2,1,0:T(8,128)(2,1)S(1)}, bf16[2,512,1024]{2,1,0:T(8,128)(2,1)}, u32[]{:S(2)}) copy-start(bf16[2,512,1024]{2,1,0:T(8,128)(2,1)} %constant.52) | copy-start | bytes 6291460
  101.4 15.1 %all-to-all-start.2 = ((bf16[32,16,2,128]{3,2,1,0:T(2,128)(2,1)}), bf16[32,16,2,128]{3,2,1,0:T(2,128)(2,1)S(1)}, u32[]{:S(2)}, u32[]{:S(2)}) async-start(bf16[32,16,2,128]{3,2,1,0:T(2,128)(2,1)} %copy.40), calls=%async_computation.2 | async-start | bytes 524288 | tf_op jit(solution)/shard_map/all_to_all | solution.py:253
